TPU v7x, 128 devices: a whole 4x4x4 slice. The times are simulated.
128 devices in a mesh: section: 16 (over z_lo, x, core), ctx: 8 (over z_hi, y).
Axes of the slice: x: 4, y: 4, z: 4 (z_hi: 2, z_lo: 2; z = z_hi * 2 + z_lo), core: 2. Of those that a mesh axis runs over, the one named last changes fastest.
Arguments:
- sent_fwd: bfloat16 [16, 1024, 4096], P('section', 'ctx'), may hold values from -6 to 6
- sent_grad: bfloat16 [16, 1024, 4096], P('section', 'ctx'), may hold values from -6 to 6
- saved_bwd: bfloat16 [16, 1024, 4096], P('section', 'ctx'), may hold values from -6 to 6
- norm_gain: float32 [16, 4096], P('section'), may hold values from 0.5 to 1.5
- key_proj: bfloat16 [16, 4096, 512], P('section')
- value_proj: bfloat16 [16, 4096, 512], P('section'), may hold values from -0.09375 to 0.09375
- seg_fwd: int32 [1024], replicated, may hold values from 0 to 3, never falling along the last dimension, each value on 1 to 512 neighbouring positions
- seg_bwd: int32 [1024], replicated, may hold values from 0 to 3, never falling along the last dimension, each value on 1 to 512 neighbouring positions
Outputs:
- fwd_out: bfloat16 [16, 1024, 4096], P('section', 'ctx')
- grad_out: bfloat16 [16, 1024, 4096], P('section', 'ctx')
Inputs may be any that keep to these rules, and one draw needn't show every extreme that they name: `seg_fwd`: segment ids never fall along the sequence, each segment has 1 to 512 positions and one has exactly 512. `seg_bwd`: segment ids never fall along the sequence, each segment has 1 to 512 positions and one has exactly 512.
All inputs are finite; a program needn't handle non-finite values.
Results may differ from a plain program's by a relative error of at most 0.02.
The roundings to bfloat16 on the way count: a program that leaves them out, or rounds other values in their place, can miss the bound.
Values may be sent and summed in bfloat16 or wider, within the bound.
No kernel may reach another device: no remote copies, remote signals or barrier semaphores. Data moves between devices by JAX's collectives and lax.ppermute only.
A program may use at most 128 MiB of HBM per device.

v0:
```python
import functools

import jax
import jax.numpy as jnp
from jax import lax
from jax.sharding import PartitionSpec as P
from jax.experimental import pallas as pl

HD = 128


EPSILON = 1e-05
NEGATIVE = -1e30


def shifted(block, axis, distance):
    devices = range(lax.axis_size(axis))
    route = [((i - distance) % len(devices), i) for i in devices]
    return lax.ppermute(block, axis, route)


def gather_all(block, axis):
    count = lax.axis_size(axis)
    spread = jnp.broadcast_to(block[None], (count,) + block.shape)
    moved = lax.all_to_all(spread, axis, 0, 0)
    return moved.reshape((count * block.shape[0],) + block.shape[1:])


def reduce_all(terms, axis):
    count = lax.axis_size(axis)
    rows = terms.shape[0] // count
    moved = lax.all_to_all(terms.astype(jnp.bfloat16).reshape((count, rows) + terms.shape[1:]), axis, 0, 0)
    return jnp.sum(moved.astype(jnp.float32), axis=0)


def normalize(inputs, gain):
    wide = inputs.astype(jnp.float32)
    inverse = lax.rsqrt(jnp.mean(wide * wide, axis=-1, keepdims=True) + EPSILON)
    return (wide * inverse * gain, wide, inverse)


INTERPRET = False


def forward_kernel(mask_ref, query_ref, key_ref, value_ref, input_ref, out_ref, *, heads, scale):
    allowed = mask_ref[...] != 0
    keys = key_ref[...]
    values = value_ref[...]
    for head in range(heads):
        cols = slice(head * HD, (head + 1) * HD)
        scores = lax.dot_general(
            query_ref[:, cols], keys, (((1,), (1,)), ((), ())), preferred_element_type=jnp.float32
        ) * scale
        scores = jnp.where(allowed, scores, NEGATIVE)
        rowmax = jnp.max(scores, axis=1, keepdims=True)
        expo = jnp.where(allowed, jnp.exp(scores - rowmax), 0.0)
        total = jnp.sum(expo, axis=1, keepdims=True)
        product = jnp.dot(expo.astype(jnp.bfloat16), values, preferred_element_type=jnp.float32)
        out_ref[:, cols] = (input_ref[:, cols].astype(jnp.float32) + product / total).astype(out_ref.dtype)


def backward_kernel(mask_ref, query_ref, key_ref, value_ref, grad_ref, dquery_ref, dkey_ref, dvalue_ref, *, heads, scale):
    allowed = mask_ref[...] != 0
    keys = key_ref[...]
    values = value_ref[...]
    dkey_acc = jnp.zeros(dkey_ref.shape, jnp.float32)
    dvalue_acc = jnp.zeros(dvalue_ref.shape, jnp.float32)
    for head in range(heads):
        cols = slice(head * HD, (head + 1) * HD)
        query = query_ref[:, cols]
        grad = grad_ref[:, cols]
        scores = lax.dot_general(
            query, keys, (((1,), (1,)), ((), ())), preferred_element_type=jnp.float32
        ) * scale
        scores = jnp.where(allowed, scores, NEGATIVE)
        rowmax = jnp.max(scores, axis=1, keepdims=True)
        expo = jnp.where(allowed, jnp.exp(scores - rowmax), 0.0)
        total = jnp.sum(expo, axis=1, keepdims=True)
        probs = expo / total
        dprob = lax.dot_general(
            grad, values, (((1,), (1,)), ((), ())), preferred_element_type=jnp.float32
        )
        delta = jnp.sum(probs * dprob, axis=1, keepdims=True)
        dscore_b = (probs * (dprob - delta)).astype(jnp.bfloat16)
        probs_b = probs.astype(jnp.bfloat16)
        dquery_ref[:, cols] = jnp.dot(dscore_b, keys, preferred_element_type=jnp.float32) * scale
        dkey_acc = dkey_acc + lax.dot_general(
            dscore_b, query, (((0,), (0,)), ((), ())), preferred_element_type=jnp.float32
        )
        dvalue_acc = dvalue_acc + lax.dot_general(
            probs_b, grad, (((0,), (0,)), ((), ())), preferred_element_type=jnp.float32
        )
    dkey_ref[...] = dkey_acc * scale
    dvalue_ref[...] = dvalue_acc


def attention_forward(mask, query, keys, values, inputs, group_size):
    rows, width = query.shape
    seq_len, kv_width = keys.shape
    groups = kv_width // HD
    cols = group_size * HD
    kernel = functools.partial(forward_kernel, heads=group_size, scale=HD ** (-0.5))
    return pl.pallas_call(
        kernel,
        grid=(groups,),
        in_specs=[
            pl.BlockSpec((rows, seq_len), lambda g: (0, 0)),
            pl.BlockSpec((rows, cols), lambda g: (0, g)),
            pl.BlockSpec((seq_len, HD), lambda g: (0, g)),
            pl.BlockSpec((seq_len, HD), lambda g: (0, g)),
            pl.BlockSpec((rows, cols), lambda g: (0, g)),
        ],
        out_specs=pl.BlockSpec((rows, cols), lambda g: (0, g)),
        out_shape=jax.ShapeDtypeStruct((rows, width), jnp.bfloat16),
        interpret=INTERPRET,
    )(mask, query, keys, values, inputs)


def attention_backward(mask, query, keys, values, grad, group_size):
    rows, width = query.shape
    seq_len, kv_width = keys.shape
    groups = kv_width // HD
    cols = group_size * HD
    kernel = functools.partial(backward_kernel, heads=group_size, scale=HD ** (-0.5))
    return pl.pallas_call(
        kernel,
        grid=(groups,),
        in_specs=[
            pl.BlockSpec((rows, seq_len), lambda g: (0, 0)),
            pl.BlockSpec((rows, cols), lambda g: (0, g)),
            pl.BlockSpec((seq_len, HD), lambda g: (0, g)),
            pl.BlockSpec((seq_len, HD), lambda g: (0, g)),
            pl.BlockSpec((rows, cols), lambda g: (0, g)),
        ],
        out_specs=[
            pl.BlockSpec((rows, cols), lambda g: (0, g)),
            pl.BlockSpec((seq_len, HD), lambda g: (0, g)),
            pl.BlockSpec((seq_len, HD), lambda g: (0, g)),
        ],
        out_shape=[
            jax.ShapeDtypeStruct((rows, width), jnp.float32),
            jax.ShapeDtypeStruct((seq_len, kv_width), jnp.float32),
            jax.ShapeDtypeStruct((seq_len, kv_width), jnp.float32),
        ],
        interpret=INTERPRET,
    )(mask, query, keys, values, grad)


def body(sent_fwd, sent_grad, saved_bwd, norm_gain, key_proj, value_proj, seg_fwd, seg_bwd):
    tok_rows = sent_fwd.shape[1]
    width = sent_fwd.shape[2]
    kv_width = key_proj.shape[2]
    heads = width // HD
    kv_heads = kv_width // HD
    group_size = heads // kv_heads
    scale_factor = HD ** (-0.5)
    count = lax.axis_size("ctx")
    rank = lax.axis_index("ctx")
    offset = rank * tok_rows
    query_pos = offset + jnp.arange(tok_rows, dtype=jnp.int32)
    gain = norm_gain[0]
    key_weight = key_proj[0]
    value_weight = value_proj[0]
    arrived = shifted(sent_fwd, "section", 1)[0]
    upstream = shifted(sent_grad, "section", -1)[0]

    def layer_parts(inputs):
        normed, wide, inverse = normalize(inputs, gain)
        flat = normed.astype(jnp.bfloat16)
        keys = jnp.dot(flat, key_weight, preferred_element_type=jnp.float32).astype(jnp.bfloat16)
        values = jnp.dot(flat, value_weight, preferred_element_type=jnp.float32).astype(
            jnp.bfloat16
        )
        return (flat.reshape(tok_rows, heads, HD), keys, values, wide, inverse)

    def allowed_of(segment):
        seg_query = lax.dynamic_slice_in_dim(segment, offset, tok_rows)
        key_pos = jnp.arange(segment.shape[0], dtype=jnp.int32)
        return (key_pos[None, :] <= query_pos[:, None]) & (seg_query[:, None] == segment[None, :])

    bwd_query, bwd_keys, bwd_values, bwd_wide, bwd_inverse = layer_parts(saved_bwd[0])
    bwd_all = gather_all(jnp.concatenate([bwd_keys, bwd_values], axis=1), "ctx")
    fwd_query, fwd_keys, fwd_values, fwd_wide, fwd_inverse = layer_parts(arrived)
    fwd_all = gather_all(jnp.concatenate([fwd_keys, fwd_values], axis=1), "ctx")

    bwd_key_all = bwd_all[:, :kv_width]
    bwd_value_all = bwd_all[:, kv_width:]
    allowed = allowed_of(seg_bwd).astype(jnp.int32)
    dquery, dkey_terms, dvalue_terms = attention_backward(
        allowed, bwd_query.reshape(tok_rows, width), bwd_key_all, bwd_value_all, upstream, group_size
    )
    dkv_terms = jnp.concatenate([dkey_terms, dvalue_terms], axis=1)
    dkv_sum = reduce_all(dkv_terms, "ctx")
    dkv = dkv_sum.astype(jnp.bfloat16)
    dkeys = dkv[:, :kv_width]
    dvalues = dkv[:, kv_width:]

    key_piece = fwd_all[:, :kv_width]
    value_piece = fwd_all[:, kv_width:]
    allowed = allowed_of(seg_fwd).astype(jnp.int32)
    fwd_out = attention_forward(
        allowed, fwd_query.reshape(tok_rows, width), key_piece, value_piece, arrived, group_size
    )

    dnormed = dquery + jnp.dot(
        dkeys, jnp.transpose(key_weight), preferred_element_type=jnp.float32
    )
    dnormed = dnormed + jnp.dot(
        dvalues,
        jnp.transpose(value_weight),
        preferred_element_type=jnp.float32,
    )
    scaled = gain * dnormed
    grad_in = bwd_inverse * scaled - bwd_wide * bwd_inverse**3 * jnp.mean(
        bwd_wide * scaled, axis=-1, keepdims=True
    )
    grad_out = (upstream.astype(jnp.float32) + grad_in).astype(jnp.bfloat16)
    return (fwd_out[None], grad_out[None])


def solution(mesh):
    placed = (
        P("section", "ctx", None),
        P("section", "ctx", None),
        P("section", "ctx", None),
        P("section", None),
        P("section", None, None),
        P("section", None, None),
        P(),
        P(),
    )
    return jax.shard_map(
        body,
        mesh=mesh,
        in_specs=placed,
        out_specs=(P("section", "ctx", None), P("section", "ctx", None)),
        check_vma=False,
    )
```

profile of v0, /device:TPU:7, one launch (start us, length us, event | category | flops | bytes accessed | tf_op | source)
XLA Modules:
  0.0 170.8 jit_solution(7471023278709492385)
XLA Ops:
  0.6 2.2 %collective-permute-start = (bf16[1,128,4096]{2,1,0:T(8,128)(2,1)}, bf16[1,128,4096]{2,1,0:T(8,128)(2,1)S(1)}, u32[]{:S(2)}, u32[]{:S(2)}) collective-permute-start(bf16[1,128,4096]{2,1,0:T(8,128)(2,1)} %param.8), channel_id=1, source_target_pairs={{120,0},{0,8},{8,16},{16,24},{24,32},{32,40},{40,48},{48,56},{56,6... | collective-permute-start | bytes 3145736 | tf_op jit(solution)/shard_map/ppermute | solution.py:19
  2.8 1.5 fusion.19
  4.3 0.0 copy-start
  4.3 0.0 copy-start.2
  4.4 0.0 copy-start.9
  4.4 3.4 %fusion.38 = bf16[128,512]{1,0:T(8,128)(2,1)S(1)} fusion(bf16[1,4096,512]{2,1,0:T(8,128)(2,1)} %param.13, bf16[1,128,4096]{2,1,0:T(8,128)(2,1)} %param.10, f32[128]{0:T(128)S(1)} %get-tuple-element.16, f32[4096]{0:T(1024)} %bitcast.76), kind=kOutput, calls=%fused_computation.39 | convolution fusion | flops 539033600 | bytes 5390848 | tf_op jit(solution)/shard_map/dot_general | solution.py:171
  7.8 0.0 copy-done
  7.8 0.6 copy-done.2
  8.4 0.0 copy-done.9
  8.4 0.8 fusion.32
  9.3 1.6 broadcast_in_dim.10
  10.9 7.2 %all-to-all-start.1 = ((bf16[8,128,1024]{2,1,0:T(8,128)(2,1)}), bf16[8,128,1024]{2,1,0:T(8,128)(2,1)}, u32[]{:S(2)}, u32[]{:S(2)}) async-start(bf16[8,128,1024]{2,1,0:T(8,128)(2,1)} %broadcast_in_dim.10), calls=%async_computation.1 | async-start | bytes 4194304 | tf_op jit(solution)/shard_map/all_to_all | solution.py:25
  18.1 0.0 collective-permute-done
  18.1 0.0 copy-start.1
  18.1 0.3 fusion.16
  18.4 0.0 copy-start.3
  18.4 3.1 %fusion.35 = bf16[128,512]{1,0:T(8,128)(2,1)S(1)} fusion(bf16[1,4096,512]{2,1,0:T(8,128)(2,1)} %param.13, bf16[1,128,4096]{2,1,0:T(8,128)(2,1)S(1)} %collective-permute-done, f32[4096]{0:T(1024)S(1)} %bitcast.78, f32[128]{0:T(128)S(1)} %add_rsqrt_fusion.1), kind=kOutput, calls=%fused_computation.38 | convolution fusion | flops 539033600 | bytes 5390848 | tf_op jit(solution)/shard_map/dot_general | solution.py:171
  21.5 0.4 copy-done.3
  21.9 0.8 fusion.29
  22.8 23.8 %all-to-all-done.1 = bf16[8,128,1024]{2,1,0:T(8,128)(2,1)} async-done(((bf16[8,128,1024]{2,1,0:T(8,128)(2,1)}), bf16[8,128,1024]{2,1,0:T(8,128)(2,1)}, u32[]{:S(2)}, u32[]{:S(2)}) %all-to-all-start.1) | async-done | bytes 2097184 | tf_op jit(solution)/shard_map/all_to_all | solution.py:25
  46.5 1.6 broadcast_in_dim.8
  48.1 0.0 copy-start.10
  48.1 0.0 copy-start.11
  48.1 8.9 %all-to-all-start = ((bf16[8,128,1024]{2,1,0:T(8,128)(2,1)}), bf16[8,128,1024]{2,1,0:T(8,128)(2,1)}, u32[]{:S(2)}, u32[]{:S(2)}) async-start(bf16[8,128,1024]{2,1,0:T(8,128)(2,1)} %broadcast_in_dim.8), calls=%async_computation | async-start | bytes 4194304 | tf_op jit(solution)/shard_map/all_to_all | solution.py:25
  57.0 0.6 collective-permute-start.1
  57.5 0.0 copy-done.10
  57.5 0.1 dynamic_slice.7
  57.6 0.0 copy-done.11
  57.6 0.1 dynamic_slice.6
  57.7 1.2 fusion.47
  58.9 1.3 fusion.21.query_ref
  60.2 3.1 %fusion.54 = (bf16[1024,512]{1,0:T(8,128)(2,1)}, bf16[1024,512]{1,0:T(8,128)(2,1)}) fusion(bf16[1024,1024]{1,0:T(8,128)(2,1)} %bitcast.10), kind=kLoop, calls=%fused_computation.57 | loop fusion | bytes 4194304 | tf_op jit(solution)/shard_map/slice | solution.py:187
  63.3 25.5 %collective-permute-done.1 = bf16[1,128,4096]{2,1,0:T(8,128)(2,1)S(1)} collective-permute-done((bf16[1,128,4096]{2,1,0:T(8,128)(2,1)}, bf16[1,128,4096]{2,1,0:T(8,128)(2,1)S(1)}, u32[]{:S(2)}, u32[]{:S(2)}) %collective-permute-start.1) | collective-permute-done | bytes 1048608 | tf_op jit(solution)/shard_map/ppermute | solution.py:19
  88.8 0.0 copy-start.5
  88.8 1.0 copy-done.5
  89.8 27.1 %shard_map.96 = (f32[128,4096]{1,0:T(8,128)}, f32[1024,512]{1,0:T(8,128)}, f32[1024,512]{1,0:T(8,128)}) custom-call(s32[128,1024]{1,0:T(8,128)} %get-tuple-element.17.mask_ref, bf16[128,4096]{1,0:T(8,128)(2,1)} %fusion.21.query_ref, bf16[1024,512]{1,0:T(8,128)(2,1)} %get-tuple-element.11.key_ref, bf16[1024,512]{1,0:T(8,128)(2,1)} %get-tuple-element.10.value_ref, ...), custom_call_target="tpu_custom_call" | custom-call | tf_op jit(solution)/shard_map/pallas_call | solution.py:125
  116.9 0.0 copy-start.7
  116.9 1.9 %convert.11 = bf16[1024,512]{1,0:T(8,128)(2,1)S(1)} convert(f32[1024,512]{1,0:T(8,128)} %get-tuple-element.7) | non-fusion elementwise | flops 524288 | bytes 3145728 | tf_op jit(solution)/shard_map/convert.4
  118.8 0.3 copy-done.7
  119.1 0.1 convert.10
  119.3 1.6 pad_maximum_fusion
  120.9 0.0 all-to-all-done
  120.9 4.5 %all-to-all-start.2 = ((bf16[8,128,1024]{2,1,0:T(8,128)(2,1)}), bf16[8,128,1024]{2,1,0:T(8,128)(2,1)}, u32[]{:S(2)}, u32[]{:S(2)}) async-start(bf16[8,128,1024]{2,1,0:T(8,128)(2,1)} %pad_maximum_fusion), calls=%async_computation.2 | async-start | bytes 4194304 | tf_op jit(solution)/shard_map/all_to_all | solution.py:32
  125.4 3.1 %fusion.55 = (bf16[1024,512]{1,0:T(8,128)(2,1)}, bf16[1024,512]{1,0:T(8,128)(2,1)}) fusion(bf16[1024,1024]{1,0:T(8,128)(2,1)} %bitcast.5), kind=kLoop, calls=%fused_computation.58 | loop fusion | bytes 4194304 | tf_op jit(solution)/shard_map/slice | solution.py:199
  128.5 14.4 %all-to-all-done.2 = bf16[8,128,1024]{2,1,0:T(8,128)(2,1)} async-done(((bf16[8,128,1024]{2,1,0:T(8,128)(2,1)}), bf16[8,128,1024]{2,1,0:T(8,128)(2,1)}, u32[]{:S(2)}, u32[]{:S(2)}) %all-to-all-start.2) | async-done | bytes 2097184 | tf_op jit(solution)/shard_map/all_to_all | solution.py:32
  142.9 2.0 %reduce_sum.41 = bf16[128,1024]{1,0:T(8,128)(2,1)S(1)} reduce(bf16[8,128,1024]{2,1,0:T(8,128)(2,1)} %all-to-all-done.2, bf16[]{:T(256)} %constant.20.clone.1), dimensions={0}, to_apply=%region_2.0 | reduce | flops 917504 | bytes 2359298 | tf_op jit(solution)/shard_map/reduce_sum | solution.py:33
  144.9 0.0 copy-start.4
  144.9 3.8 %fusion = f32[128,4096]{1,0:T(8,128)S(1)} fusion(bf16[1,4096,512]{2,1,0:T(8,128)(2,1)} %param.13, bf16[128,1024]{1,0:T(8,128)(2,1)S(1)} %reduce_sum.41), kind=kOutput, calls=%fused_computation | convolution fusion | flops 536870912 | bytes 6422528 | tf_op jit(solution)/shard_map/dot_general | solution.py:208
  148.7 0.0 copy-done.4
  148.7 0.0 copy-start.8
  148.7 1.5 fusion.6
  150.2 0.0 copy-done.1
  150.2 0.1 copy-done.8
  150.3 2.2 %fusion.26 = (f32[128]{0:T(128)S(1)}, f32[128,4096]{1,0:T(8,128)}, bf16[128,4096]{1,0:T(8,128)(2,1)}) fusion(bf16[1,128,4096]{2,1,0:T(8,128)(2,1)S(1)} %copy-done, f32[128,4096]{1,0:T(8,128)S(1)} %fusion, f32[128,4096]{1,0:T(8,128)S(1)} %copy-done.8, f32[128,4096]{1,0:T(8,128)S(1)} %fusion.6, f32[4096]{0:T(1024)S(1)} %bitcast.81, ...), kind=kLoop, calls=%fused_computation.30 | loop fusion | flops 5242752 | bytes 11551744 | tf_op jit(solution)/shard_map/reduce_sum | solution.py:214
  152.5 0.0 copy-start.6
  152.5 15.0 %shard_map.95 = bf16[128,4096]{1,0:T(8,128)(2,1)} custom-call(s32[128,1024]{1,0:T(8,128)} %get-tuple-element.18.mask_ref, bf16[128,4096]{1,0:T(8,128)(2,1)} %get-tuple-element.14.query_ref, bf16[1024,512]{1,0:T(8,128)(2,1)} %get-tuple-element.13.key_ref, bf16[1024,512]{1,0:T(8,128)(2,1)} %get-tuple-element.12.value_ref, bf16[128,4096]{1,0:T(8,128)(2,1)} %bitcast.71), custom_call_target="tpu_custom_call" | custom-call | tf_op jit(solution)/shard_map/pallas_call | solution.py:103
  167.6 0.0 copy-done.6
  167.6 3.2 %fusion.43 = bf16[1,128,4096]{2,1,0:T(8,128)(2,1)} fusion(bf16[1,128,4096]{2,1,0:T(8,128)(2,1)S(1)} %copy-done, f32[128,4096]{1,0:T(8,128)} %get-tuple-element.9, f32[128]{0:T(128)S(1)} %broadcast_multiply_fusion, f32[128]{0:T(128)S(1)} %get-tuple-element.15, f32[128]{0:T(128)S(1)} %get-tuple-element.16, bf16[1,128,4096]{2,1,0:T(8,128)(2,1)S(1)} %copy-done.6), kind=kLoop, calls=%fused_computation.42 | loop fusion | flops 4194304 | bytes 5244416 | tf_op jit(solution)/shard_map/broadcast_in_dim | solution.py:218
  (6 shorter events, 0.1 us)
Async XLA Ops:
  0.6 17.5 %collective-permute-start = (bf16[1,128,4096]{2,1,0:T(8,128)(2,1)}, bf16[1,128,4096]{2,1,0:T(8,128)(2,1)S(1)}, u32[]{:S(2)}, u32[]{:S(2)}) collective-permute-start(bf16[1,128,4096]{2,1,0:T(8,128)(2,1)} %param.8), channel_id=1, source_target_pairs={{120,0},{0,8},{8,16},{16,24},{24,32},{32,40},{40,48},{48,56},{56,6... | collective-permute-start | bytes 3145736 | tf_op jit(solution)/shard_map/ppermute | solution.py:19
  4.3 3.5 %copy-start = (bf16[1,128,4096]{2,1,0:T(8,128)(2,1)S(1)}, bf16[1,128,4096]{2,1,0:T(8,128)(2,1)}, u32[]{:S(2)}) copy-start(bf16[1,128,4096]{2,1,0:T(8,128)(2,1)} %param.10) | copy-start | bytes 3145732
  4.3 4.1 %copy-start.2 = (bf16[1,4096,512]{2,1,0:T(8,128)(2,1)S(1)}, bf16[1,4096,512]{2,1,0:T(8,128)(2,1)}, u32[]{:S(2)}) copy-start(bf16[1,4096,512]{2,1,0:T(8,128)(2,1)} %param.12) | copy-start | bytes 12582916
  4.4 4.1 %copy-start.9 = (f32[1,4096]{1,0:T(1,128)S(1)}, f32[1,4096]{1,0:T(1,128)}, u32[]{:S(2)}) copy-start(f32[1,4096]{1,0:T(1,128)} %param.11) | copy-start | bytes 49156
  10.9 35.6 %all-to-all-start.1 = ((bf16[8,128,1024]{2,1,0:T(8,128)(2,1)}), bf16[8,128,1024]{2,1,0:T(8,128)(2,1)}, u32[]{:S(2)}, u32[]{:S(2)}) async-start(bf16[8,128,1024]{2,1,0:T(8,128)(2,1)} %broadcast_in_dim.10), calls=%async_computation.1 | async-start | bytes 4194304 | tf_op jit(solution)/shard_map/all_to_all | solution.py:25
  18.1 132.1 %copy-start.1 = (bf16[1,128,4096]{2,1,0:T(8,128)(2,1)}, bf16[1,128,4096]{2,1,0:T(8,128)(2,1)S(1)}, u32[]{:S(2)}) copy-start(bf16[1,128,4096]{2,1,0:T(8,128)(2,1)S(1)} %collective-permute-done) | copy-start | bytes 3145732
  18.4 3.5 %copy-start.3 = (bf16[1,4096,512]{2,1,0:T(8,128)(2,1)S(1)}, bf16[1,4096,512]{2,1,0:T(8,128)(2,1)}, u32[]{:S(2)}) copy-start(bf16[1,4096,512]{2,1,0:T(8,128)(2,1)} %param.12) | copy-start | bytes 12582916
  48.1 9.4 %copy-start.10 = (s32[1024]{0:T(1024)S(1)}, s32[1024]{0:T(1024)}, u32[]{:S(2)}) copy-start(s32[1024]{0:T(1024)} %param.15) | copy-start | bytes 12292
  48.1 9.5 %copy-start.11 = (s32[1024]{0:T(1024)S(1)}, s32[1024]{0:T(1024)}, u32[]{:S(2)}) copy-start(s32[1024]{0:T(1024)} %param.14) | copy-start | bytes 12292
  48.1 72.8 %all-to-all-start = ((bf16[8,128,1024]{2,1,0:T(8,128)(2,1)}), bf16[8,128,1024]{2,1,0:T(8,128)(2,1)}, u32[]{:S(2)}, u32[]{:S(2)}) async-start(bf16[8,128,1024]{2,1,0:T(8,128)(2,1)} %broadcast_in_dim.8), calls=%async_computation | async-start | bytes 4194304 | tf_op jit(solution)/shard_map/all_to_all | solution.py:25
  57.0 31.8 %collective-permute-start.1 = (bf16[1,128,4096]{2,1,0:T(8,128)(2,1)}, bf16[1,128,4096]{2,1,0:T(8,128)(2,1)S(1)}, u32[]{:S(2)}, u32[]{:S(2)}) collective-permute-start(bf16[1,128,4096]{2,1,0:T(8,128)(2,1)} %param.9), channel_id=1, source_target_pairs={{8,0},{16,8},{24,16},{32,24},{40,32},{48,40},{56,48},{64,56},{72,6... | collective-permute-start | bytes 3145736 | tf_op jit(solution)/shard_map/ppermute | solution.py:19
  88.8 1.0 copy-start.5
  116.9 2.2 %copy-start.7 = (f32[1024,512]{1,0:T(8,128)S(1)}, f32[1024,512]{1,0:T(8,128)}, u32[]{:S(2)}) copy-start(f32[1024,512]{1,0:T(8,128)} %get-tuple-element.6) | copy-start | bytes 6291460
  120.9 22.0 %all-to-all-start.2 = ((bf16[8,128,1024]{2,1,0:T(8,128)(2,1)}), bf16[8,128,1024]{2,1,0:T(8,128)(2,1)}, u32[]{:S(2)}, u32[]{:S(2)}) async-start(bf16[8,128,1024]{2,1,0:T(8,128)(2,1)} %pad_maximum_fusion), calls=%async_computation.2 | async-start | bytes 4194304 | tf_op jit(solution)/shard_map/all_to_all | solution.py:32
  144.9 3.8 %copy-start.4 = (bf16[1,4096,512]{2,1,0:T(8,128)(2,1)S(1)}, bf16[1,4096,512]{2,1,0:T(8,128)(2,1)}, u32[]{:S(2)}) copy-start(bf16[1,4096,512]{2,1,0:T(8,128)(2,1)} %param.12) | copy-start | bytes 12582916
  148.7 1.6 copy-start.8
  152.5 15.0 %copy-start.6 = (bf16[1,128,4096]{2,1,0:T(8,128)(2,1)S(1)}, bf16[1,128,4096]{2,1,0:T(8,128)(2,1)}, u32[]{:S(2)}) copy-start(bf16[1,128,4096]{2,1,0:T(8,128)(2,1)} %copy-done.5) | copy-start | bytes 3145732
where the time goes:
time: 171 us
  waiting for transfers between devices  63.7 us (37%)
  Pallas kernels  42.2 us (25%)
  starting transfers between devices  23.4 us (14%)
  other arithmetic  15.4 us (9%)
  matrix products  13.4 us (8%)
  local copies, waits for them, and re-layouts  12 us (7%)
    pallas_call x1, Pallas kernels, attention_backward(): pl.pallas_call(kernel, grid=(groups,), in_specs=[pl.BlockSpec((rows, seq_...  27.1 us
    ppermute x2, waiting for transfers between devices, shifted(): return lax.ppermute(block, axis, route)  25.5 us
    all_to_all x2, waiting for transfers between devices, gather_all(): moved = lax.all_to_all(spread, axis, 0, 0)  23.8 us
    all_to_all x2, starting transfers between devices, gather_all(): moved = lax.all_to_all(spread, axis, 0, 0)  16.1 us
    pallas_call x1, Pallas kernels, attention_forward(): pl.pallas_call(kernel, grid=(groups,), in_specs=[pl.BlockSpec((rows, seq_...  15 us
    all_to_all x1, waiting for transfers between devices, reduce_all(): lax.all_to_all(terms.astype(jnp.bfloat16).reshape((count, rows) + terms.s...  14.4 us
    dot_general x2, matrix products, layer_parts(): jnp.dot(flat, value_weight, preferred_element_type=jnp.float32)  6.52 us
    all_to_all x1, starting transfers between devices, reduce_all(): lax.all_to_all(terms.astype(jnp.bfloat16).reshape((count, rows) + terms.s...  4.54 us
  transfers between devices with their start and end apart: 5, of which 3 were waited for; matrix products, arithmetic and copies ran while one was open for 14% of the time, Pallas kernels for 16%

commit v1 on v0

--- a/solution.py
+++ b/solution.py
@@ -26,11 +26,18 @@
     return moved.reshape((count * block.shape[0],) + block.shape[1:])
 
 
-def reduce_all(terms, axis):
+def reduce_earlier(terms, axis):
     count = lax.axis_size(axis)
+    rank = lax.axis_index(axis)
     rows = terms.shape[0] // count
-    moved = lax.all_to_all(terms.astype(jnp.bfloat16).reshape((count, rows) + terms.shape[1:]), axis, 0, 0)
-    return jnp.sum(moved.astype(jnp.float32), axis=0)
+    narrow = terms.astype(jnp.bfloat16)
+    total = lax.dynamic_slice_in_dim(terms, rank * rows, rows)
+    for distance in range(1, count):
+        start = jnp.maximum(rank - distance, 0) * rows
+        piece = lax.dynamic_slice_in_dim(narrow, start, rows)
+        route = [(i + distance, i) for i in range(count - distance)]
+        total = total + lax.ppermute(piece, axis, route).astype(jnp.float32)
+    return total
 
 
 def normalize(inputs, gain):
@@ -190,7 +197,7 @@
         allowed, bwd_query.reshape(tok_rows, width), bwd_key_all, bwd_value_all, upstream, group_size
     )
     dkv_terms = jnp.concatenate([dkey_terms, dvalue_terms], axis=1)
-    dkv_sum = reduce_all(dkv_terms, "ctx")
+    dkv_sum = reduce_earlier(dkv_terms, "ctx")
     dkv = dkv_sum.astype(jnp.bfloat16)
     dkeys = dkv[:, :kv_width]
     dvalues = dkv[:, kv_width:]

time: 171 us -> 175 us (1.023)
  the two profiles are of different devices: /device:TPU:7 before, /device:TPU:6 now
where the time goes in v1:
time: 175 us
  waiting for transfers between devices  69.6 us (40%)
  Pallas kernels  42.1 us (24%)
  starting transfers between devices  25.3 us (14%)
  local copies, waits for them, and re-layouts  16.6 us (9%)
  matrix products  11.4 us (7%)
  other arithmetic  8.9 us (5%)
    all_to_all x2, waiting for transfers between devices, gather_all(): moved = lax.all_to_all(spread, axis, 0, 0)  51.5 us
    pallas_call x1, Pallas kernels, attention_backward(): pl.pallas_call(kernel, grid=(groups,), in_specs=[pl.BlockSpec((rows, seq_...  27.2 us
    ppermute x7, waiting for transfers between devices, reduce_earlier(): total = total + lax.ppermute(piece, axis, route).astype(jnp.float32)  18.1 us
    pallas_call x1, Pallas kernels, attention_forward(): pl.pallas_call(kernel, grid=(groups,), in_specs=[pl.BlockSpec((rows, seq_...  15 us
    all_to_all x2, starting transfers between devices, gather_all(): moved = lax.all_to_all(spread, axis, 0, 0)  14.5 us
    ppermute x7, starting transfers between devices, reduce_earlier(): total = total + lax.ppermute(piece, axis, route).astype(jnp.float32)  9.28 us
    unnamed x29, local copies, waits for them, and re-layouts  5.98 us
    dot_general x2, matrix products, layer_parts(): jnp.dot(flat, value_weight, preferred_element_type=jnp.float32)  4.18 us
  transfers between devices with their start and end apart: 11, of which 3 were waited for; matrix products, arithmetic and copies ran while one was open for 15% of the time, Pallas kernels for 0%

profile of v1, /device:TPU:6, one launch (start us, length us, event | category | flops | bytes accessed | tf_op | source)
XLA Modules:
  0.0 174.9 jit_solution(4864277404195470675)
XLA Ops:
  0.6 0.1 collective-permute-start
  0.7 1.5 fusion.19
  2.2 0.0 copy-start.5
  2.3 0.0 copy-start.11
  2.3 3.4 %fusion.38 = bf16[128,512]{1,0:T(8,128)(2,1)S(1)} fusion(bf16[1,4096,512]{2,1,0:T(8,128)(2,1)} %param.13, bf16[1,128,4096]{2,1,0:T(8,128)(2,1)} %param.10, f32[128]{0:T(128)S(1)} %get-tuple-element.22, f32[4096]{0:T(1024)} %bitcast.76), kind=kOutput, calls=%fused_computation.38 | convolution fusion | flops 539033600 | bytes 5390848 | tf_op jit(solution)/shard_map/dot_general | solution.py:178
  5.7 0.0 copy-done
  5.7 0.6 copy-done.5
  6.3 0.0 copy-done.11
  6.3 0.8 fusion.32
  7.2 1.6 broadcast_in_dim.10
  8.8 7.9 %all-to-all-start.1 = ((bf16[8,128,1024]{2,1,0:T(8,128)(2,1)}), bf16[8,128,1024]{2,1,0:T(8,128)(2,1)}, u32[]{:S(2)}, u32[]{:S(2)}) async-start(bf16[8,128,1024]{2,1,0:T(8,128)(2,1)} %broadcast_in_dim.10), calls=%async_computation.1 | async-start | bytes 4194304 | tf_op jit(solution)/shard_map/all_to_all | solution.py:25
  16.7 1.5 collective-permute-start.1
  18.1 0.0 copy-done.12
  18.1 0.1 dynamic_slice.31
  18.2 0.0 copy-done.13
  18.2 0.1 dynamic_slice.30
  18.3 1.2 fusion.47
  19.5 0.0 collective-permute-done
  19.5 0.3 fusion.16
  19.8 2.0 %fusion.21 = (bf16[128,4096]{1,0:T(8,128)(2,1)}, bf16[128,4096]{1,0:T(8,128)(2,1)}) fusion(bf16[1,128,4096]{2,1,0:T(8,128)(2,1)S(1)} %copy-done, f32[128]{0:T(128)S(1)} %get-tuple-element.22, f32[4096]{0:T(1024)S(1)} %bitcast.78, f32[128]{0:T(128)S(1)} %add_rsqrt_fusion.1, bf16[1,128,4096]{2,1,0:T(8,128)(2,1)S(1)} %collective-permute-done), kind=kLoop, calls=%fused_computation.25 | loop fusion | flops 4194304 | bytes 4211712 | tf_op jit(solution)/shard_map/convert_element_type | solution.py:176
  21.8 33.6 %all-to-all-done.1 = bf16[8,128,1024]{2,1,0:T(8,128)(2,1)} async-done(((bf16[8,128,1024]{2,1,0:T(8,128)(2,1)}), bf16[8,128,1024]{2,1,0:T(8,128)(2,1)}, u32[]{:S(2)}, u32[]{:S(2)}) %all-to-all-start.1) | async-done | bytes 2097184 | tf_op jit(solution)/shard_map/all_to_all | solution.py:25
  55.4 3.0 %fusion.58 = (bf16[1024,512]{1,0:T(8,128)(2,1)}, bf16[1024,512]{1,0:T(8,128)(2,1)}) fusion(bf16[1024,1024]{1,0:T(8,128)(2,1)} %bitcast.10), kind=kLoop, calls=%fused_computation.66 | loop fusion | bytes 4194304 | tf_op jit(solution)/shard_map/slice | solution.py:194
  58.3 0.0 collective-permute-done.1
  58.3 1.0 copy-done.7
  59.4 27.2 %shard_map.96 = (f32[128,4096]{1,0:T(8,128)}, f32[1024,512]{1,0:T(8,128)}, f32[1024,512]{1,0:T(8,128)}) custom-call(s32[128,1024]{1,0:T(8,128)} %get-tuple-element.23.mask_ref, bf16[128,4096]{1,0:T(8,128)(2,1)} %get-tuple-element.19.query_ref, bf16[1024,512]{1,0:T(8,128)(2,1)} %get-tuple-element.16.key_ref, bf16[1024,512]{1,0:T(8,128)(2,1)} %get-tuple-element.15.value_ref, ...), custom_call_target="tpu_custom_call" | custom-call | tf_op jit(solution)/shard_map/pallas_call | solution.py:132
  86.6 2.0 %constant_dynamic-update-slice_fusion.1 = f32[1024,1024]{1,0:T(8,128)S(1)} fusion(f32[1024,512]{1,0:T(8,128)} %get-tuple-element.6), kind=kLoop, calls=%fused_computation.53 | loop fusion | bytes 4194304
  88.6 0.2 copy-done.9
  88.8 0.2 constant_dynamic-update-slice_fusion
  89.0 0.0 copy-start.1
  89.0 0.0 copy-start.3
  89.0 0.3 convert_element_type.100
  89.4 1.8 %copy-done.1 = f32[1024,1024]{1,0:T(8,128)} copy-done((f32[1024,1024]{1,0:T(8,128)}, f32[1024,1024]{1,0:T(8,128)S(1)}, u32[]{:S(2)}) %copy-start.1) | copy-done | bytes 4194328
  91.1 1.0 constant_dynamic-slice_fusion.6
  92.1 1.3 collective-permute-start.8
  93.4 0.0 copy-start.6
  93.4 1.6 collective-permute-start.7
  95.0 0.0 copy-done.3
  95.0 0.8 fusion.35
  95.8 1.3 collective-permute-start.6
  97.1 1.3 collective-permute-start.5
  98.4 1.3 collective-permute-start.4
  99.7 18.1 %collective-permute-done.8 = bf16[128,1024]{1,0:T(8,128)(2,1)S(1)} collective-permute-done((bf16[128,1024]{1,0:T(8,128)(2,1)S(1)}, bf16[128,1024]{1,0:T(8,128)(2,1)S(1)}, u32[]{:S(2)}, u32[]{:S(2)}) %collective-permute-start.8) | collective-permute-done | bytes 262176 | tf_op jit(solution)/shard_map/ppermute | solution.py:39
  117.7 1.3 collective-permute-start.3
  119.0 0.0 collective-permute-done.7
  119.0 1.3 collective-permute-start.2
  120.3 0.0 copy-done.2
  120.4 0.8 fusion.29
  121.2 1.7 broadcast_in_dim.8
  122.9 6.6 %all-to-all-start = ((bf16[8,128,1024]{2,1,0:T(8,128)(2,1)}), bf16[8,128,1024]{2,1,0:T(8,128)(2,1)}, u32[]{:S(2)}, u32[]{:S(2)}) async-start(bf16[8,128,1024]{2,1,0:T(8,128)(2,1)} %broadcast_in_dim.8), calls=%async_computation | async-start | bytes 4194304 | tf_op jit(solution)/shard_map/all_to_all | solution.py:25
  129.5 0.0 collective-permute-done.6
  129.5 0.0 collective-permute-done.5
  129.5 0.0 collective-permute-done.4
  129.5 0.0 collective-permute-done.3
  129.5 0.0 collective-permute-done.2
  129.5 1.8 %add_convert_fusion = bf16[128,1024]{1,0:T(8,128)(2,1)S(1)} fusion(bf16[128,1024]{1,0:T(8,128)(2,1)S(1)} %collective-permute-done.8, bf16[128,1024]{1,0:T(8,128)(2,1)S(1)} %collective-permute-done.7, bf16[128,1024]{1,0:T(8,128)(2,1)} %collective-permute-done.6, bf16[128,1024]{1,0:T(8,128)(2,1)} %collective-permute-done.5, ...), kind=kLoop, calls=%fused_computation.42 | loop fusion | flops 1966080 | bytes 2621444 | tf_op jit(solution)/shard_map/convert_element_type | solution.py:201
  131.3 0.0 copy-start.4
  131.3 3.8 %fusion.6 = f32[128,4096]{1,0:T(8,128)S(1)} fusion(bf16[1,4096,512]{2,1,0:T(8,128)(2,1)} %param.12, bf16[128,1024]{1,0:T(8,128)(2,1)S(1)} %add_convert_fusion), kind=kOutput, calls=%fused_computation.6 | convolution fusion | flops 536870912 | bytes 6422528 | tf_op jit(solution)/shard_map/dot_general | solution.py:212
  135.2 0.3 copy-done.10
  135.4 1.7 fusion.26
  137.2 0.0 copy-done.8
  137.2 1.7 fusion.43
  138.9 18.0 %all-to-all-done = bf16[8,128,1024]{2,1,0:T(8,128)(2,1)} async-done(((bf16[8,128,1024]{2,1,0:T(8,128)(2,1)}), bf16[8,128,1024]{2,1,0:T(8,128)(2,1)}, u32[]{:S(2)}, u32[]{:S(2)}) %all-to-all-start) | async-done | bytes 2097184 | tf_op jit(solution)/shard_map/all_to_all | solution.py:25
  156.9 3.1 %fusion.59 = (bf16[1024,512]{1,0:T(8,128)(2,1)}, bf16[1024,512]{1,0:T(8,128)(2,1)}) fusion(bf16[1024,1024]{1,0:T(8,128)(2,1)} %bitcast.5), kind=kLoop, calls=%fused_computation.67 | loop fusion | bytes 4194304 | tf_op jit(solution)/shard_map/slice | solution.py:206
  160.0 15.0 %shard_map.95 = bf16[128,4096]{1,0:T(8,128)(2,1)} custom-call(s32[128,1024]{1,0:T(8,128)} %get-tuple-element.24.mask_ref, bf16[128,4096]{1,0:T(8,128)(2,1)} %get-tuple-element.20.query_ref, bf16[1024,512]{1,0:T(8,128)(2,1)} %get-tuple-element.18.key_ref, bf16[1024,512]{1,0:T(8,128)(2,1)} %get-tuple-element.17.value_ref, bf16[128,4096]{1,0:T(8,128)(2,1)} %bitcast.73), custom_call_target="tpu_custom_call" | custom-call | tf_op jit(solution)/shard_map/pallas_call | solution.py:110
  (16 shorter events, 0.1 us)
Async XLA Ops:
  0.6 18.9 %collective-permute-start = (bf16[1,128,4096]{2,1,0:T(8,128)(2,1)}, bf16[1,128,4096]{2,1,0:T(8,128)(2,1)S(1)}, u32[]{:S(2)}, u32[]{:S(2)}) collective-permute-start(bf16[1,128,4096]{2,1,0:T(8,128)(2,1)} %param.8), channel_id=1, source_target_pairs={{120,0},{0,8},{8,16},{16,24},{24,32},{32,40},{40,48},{48,56},{56,6... | collective-permute-start | bytes 3145736 | tf_op jit(solution)/shard_map/ppermute | solution.py:19
  2.2 3.5 %copy-start = (bf16[1,128,4096]{2,1,0:T(8,128)(2,1)S(1)}, bf16[1,128,4096]{2,1,0:T(8,128)(2,1)}, u32[]{:S(2)}) copy-start(bf16[1,128,4096]{2,1,0:T(8,128)(2,1)} %param.10) | copy-start | bytes 3145732
  2.2 4.1 %copy-start.5 = (bf16[1,4096,512]{2,1,0:T(8,128)(2,1)S(1)}, bf16[1,4096,512]{2,1,0:T(8,128)(2,1)}, u32[]{:S(2)}) copy-start(bf16[1,4096,512]{2,1,0:T(8,128)(2,1)} %param.12) | copy-start | bytes 12582916
  2.3 4.1 %copy-start.11 = (f32[1,4096]{1,0:T(1,128)S(1)}, f32[1,4096]{1,0:T(1,128)}, u32[]{:S(2)}) copy-start(f32[1,4096]{1,0:T(1,128)} %param.11) | copy-start | bytes 49156
  8.8 9.4 %copy-start.12 = (s32[1024]{0:T(1024)S(1)}, s32[1024]{0:T(1024)}, u32[]{:S(2)}) copy-start(s32[1024]{0:T(1024)} %param.15) | copy-start | bytes 12292
  8.8 9.4 %copy-start.13 = (s32[1024]{0:T(1024)S(1)}, s32[1024]{0:T(1024)}, u32[]{:S(2)}) copy-start(s32[1024]{0:T(1024)} %param.14) | copy-start | bytes 12292
  8.8 46.6 %all-to-all-start.1 = ((bf16[8,128,1024]{2,1,0:T(8,128)(2,1)}), bf16[8,128,1024]{2,1,0:T(8,128)(2,1)}, u32[]{:S(2)}, u32[]{:S(2)}) async-start(bf16[8,128,1024]{2,1,0:T(8,128)(2,1)} %broadcast_in_dim.10), calls=%async_computation.1 | async-start | bytes 4194304 | tf_op jit(solution)/shard_map/all_to_all | solution.py:25
  16.7 41.7 %collective-permute-start.1 = (bf16[1,128,4096]{2,1,0:T(8,128)(2,1)}, bf16[1,128,4096]{2,1,0:T(8,128)(2,1)S(1)}, u32[]{:S(2)}, u32[]{:S(2)}) collective-permute-start(bf16[1,128,4096]{2,1,0:T(8,128)(2,1)} %param.9), channel_id=1, source_target_pairs={{8,0},{16,8},{24,16},{32,24},{40,32},{48,40},{56,48},{64,56},{72,6... | collective-permute-start | bytes 3145736 | tf_op jit(solution)/shard_map/ppermute | solution.py:19
  19.5 100.9 %copy-start.2 = (bf16[1,128,4096]{2,1,0:T(8,128)(2,1)}, bf16[1,128,4096]{2,1,0:T(8,128)(2,1)S(1)}, u32[]{:S(2)}) copy-start(bf16[1,128,4096]{2,1,0:T(8,128)(2,1)S(1)} %collective-permute-done) | copy-start | bytes 3145732
  58.3 1.0 copy-start.7
  86.6 2.2 %copy-start.9 = (f32[1024,512]{1,0:T(8,128)S(1)}, f32[1024,512]{1,0:T(8,128)}, u32[]{:S(2)}) copy-start(f32[1024,512]{1,0:T(8,128)} %get-tuple-element.7) | copy-start | bytes 6291460
  89.0 2.1 %copy-start.1 = (f32[1024,1024]{1,0:T(8,128)}, f32[1024,1024]{1,0:T(8,128)S(1)}, u32[]{:S(2)}) copy-start(f32[1024,1024]{1,0:T(8,128)S(1)} %constant_dynamic-update-slice_fusion) | copy-start | bytes 12582916
  89.0 6.0 %copy-start.3 = (bf16[1,4096,512]{2,1,0:T(8,128)(2,1)S(1)}, bf16[1,4096,512]{2,1,0:T(8,128)(2,1)}, u32[]{:S(2)}) copy-start(bf16[1,4096,512]{2,1,0:T(8,128)(2,1)} %param.13) | copy-start | bytes 12582916
  92.1 25.6 %collective-permute-start.8 = (bf16[128,1024]{1,0:T(8,128)(2,1)S(1)}, bf16[128,1024]{1,0:T(8,128)(2,1)S(1)}, u32[]{:S(2)}, u32[]{:S(2)}) collective-permute-start(bf16[128,1024]{1,0:T(8,128)(2,1)S(1)} %get-tuple-element.9), channel_id=1, source_target_pairs={{7,0},{15,8},{23,16},{31,24},{39,32},{47,40},{55,48},{63,56},{71,6... | collective-permute-start | bytes 786440 | tf_op jit(solution)/shard_map/ppermute | solution.py:39
  93.4 26.9 %copy-start.6 = (bf16[1,4096,512]{2,1,0:T(8,128)(2,1)S(1)}, bf16[1,4096,512]{2,1,0:T(8,128)(2,1)}, u32[]{:S(2)}) copy-start(bf16[1,4096,512]{2,1,0:T(8,128)(2,1)} %param.12) | copy-start | bytes 12582916
  93.4 25.6 %collective-permute-start.7 = (bf16[128,1024]{1,0:T(8,128)(2,1)S(1)}, bf16[128,1024]{1,0:T(8,128)(2,1)S(1)}, u32[]{:S(2)}, u32[]{:S(2)}) collective-permute-start(bf16[128,1024]{1,0:T(8,128)(2,1)S(1)} %get-tuple-element.10), channel_id=1, source_target_pairs={{6,0},{7,1},{14,8},{15,9},{22,16},{23,17},{30,24},{31,25},{38,32},... | collective-permute-start | bytes 786440 | tf_op jit(solution)/shard_map/ppermute | solution.py:39
  95.8 33.7 %collective-permute-start.6 = (bf16[128,1024]{1,0:T(8,128)(2,1)}, bf16[128,1024]{1,0:T(8,128)(2,1)}, u32[]{:S(2)}, u32[]{:S(2)}) collective-permute-start(bf16[128,1024]{1,0:T(8,128)(2,1)} %get-tuple-element.11), channel_id=1, source_target_pairs={{5,0},{6,1},{7,2},{13,8},{14,9},{15,10},{21,16},{22,17},{23,18},{2... | collective-permute-start | bytes 786440 | tf_op jit(solution)/shard_map/ppermute | solution.py:39
  97.1 32.4 %collective-permute-start.5 = (bf16[128,1024]{1,0:T(8,128)(2,1)}, bf16[128,1024]{1,0:T(8,128)(2,1)}, u32[]{:S(2)}, u32[]{:S(2)}) collective-permute-start(bf16[128,1024]{1,0:T(8,128)(2,1)} %get-tuple-element.12), channel_id=1, source_target_pairs={{4,0},{5,1},{6,2},{7,3},{12,8},{13,9},{14,10},{15,11},{20,16},{21,... | collective-permute-start | bytes 786440 | tf_op jit(solution)/shard_map/ppermute | solution.py:39
  98.4 31.1 %collective-permute-start.4 = (bf16[128,1024]{1,0:T(8,128)(2,1)S(1)}, bf16[128,1024]{1,0:T(8,128)(2,1)}, u32[]{:S(2)}, u32[]{:S(2)}) collective-permute-start(bf16[128,1024]{1,0:T(8,128)(2,1)S(1)} %get-tuple-element.13), channel_id=1, source_target_pairs={{3,0},{4,1},{5,2},{6,3},{7,4},{11,8},{12,9},{13,10},{14,11},{15,12... | collective-permute-start | bytes 786440 | tf_op jit(solution)/shard_map/ppermute | solution.py:39
  117.7 11.8 %collective-permute-start.3 = (bf16[128,1024]{1,0:T(8,128)(2,1)S(1)}, bf16[128,1024]{1,0:T(8,128)(2,1)}, u32[]{:S(2)}, u32[]{:S(2)}) collective-permute-start(bf16[128,1024]{1,0:T(8,128)(2,1)S(1)} %get-tuple-element.14), channel_id=1, source_target_pairs={{2,0},{3,1},{4,2},{5,3},{6,4},{7,5},{10,8},{11,9},{12,10},{13,11},... | collective-permute-start | bytes 786440 | tf_op jit(solution)/shard_map/ppermute | solution.py:39
  119.0 10.5 %collective-permute-start.2 = (bf16[128,1024]{1,0:T(8,128)(2,1)S(1)}, bf16[128,1024]{1,0:T(8,128)(2,1)}, u32[]{:S(2)}, u32[]{:S(2)}) collective-permute-start(bf16[128,1024]{1,0:T(8,128)(2,1)S(1)} %get-tuple-element.8), channel_id=1, source_target_pairs={{1,0},{2,1},{3,2},{4,3},{5,4},{6,5},{7,6},{9,8},{10,9},{11,10},{12... | collective-permute-start | bytes 786440 | tf_op jit(solution)/shard_map/ppermute | solution.py:39
  122.9 34.0 %all-to-all-start = ((bf16[8,128,1024]{2,1,0:T(8,128)(2,1)}), bf16[8,128,1024]{2,1,0:T(8,128)(2,1)}, u32[]{:S(2)}, u32[]{:S(2)}) async-start(bf16[8,128,1024]{2,1,0:T(8,128)(2,1)} %broadcast_in_dim.8), calls=%async_computation | async-start | bytes 4194304 | tf_op jit(solution)/shard_map/all_to_all | solution.py:25
  131.3 3.8 %copy-start.4 = (bf16[1,4096,512]{2,1,0:T(8,128)(2,1)S(1)}, bf16[1,4096,512]{2,1,0:T(8,128)(2,1)}, u32[]{:S(2)}) copy-start(bf16[1,4096,512]{2,1,0:T(8,128)(2,1)} %param.13) | copy-start | bytes 12582916
  131.3 4.1 %copy-start.10 = (f32[128,4096]{1,0:T(8,128)S(1)}, f32[128,4096]{1,0:T(8,128)}, u32[]{:S(2)}) copy-start(f32[128,4096]{1,0:T(8,128)} %get-tuple-element.5) | copy-start | bytes 6291460
  135.4 1.8 %copy-start.8 = (bf16[1,128,4096]{2,1,0:T(8,128)(2,1)S(1)}, bf16[1,128,4096]{2,1,0:T(8,128)(2,1)}, u32[]{:S(2)}) copy-start(bf16[1,128,4096]{2,1,0:T(8,128)(2,1)} %copy-done.7) | copy-start | bytes 3145732

commit v2 on v0

--- a/solution.py
+++ b/solution.py
@@ -19,18 +19,26 @@
     return lax.ppermute(block, axis, route)
 
 
-def gather_all(block, axis):
-    count = lax.axis_size(axis)
-    spread = jnp.broadcast_to(block[None], (count,) + block.shape)
-    moved = lax.all_to_all(spread, axis, 0, 0)
-    return moved.reshape((count * block.shape[0],) + block.shape[1:])
-
-
-def reduce_all(terms, axis):
-    count = lax.axis_size(axis)
-    rows = terms.shape[0] // count
-    moved = lax.all_to_all(terms.astype(jnp.bfloat16).reshape((count, rows) + terms.shape[1:]), axis, 0, 0)
-    return jnp.sum(moved.astype(jnp.float32), axis=0)
+def gather_two_level(block):
+    zh = lax.axis_index("zh")
+    partner = lax.ppermute(block, "zh", [(0, 1), (1, 0)])
+    pair = jnp.where(zh == 0, jnp.stack([block, partner]), jnp.stack([partner, block]))
+    ring = lax.axis_size("y")
+    spread = jnp.broadcast_to(pair[None], (ring,) + pair.shape)
+    moved = lax.all_to_all(spread, "y", 0, 0)
+    return moved.reshape((-1,) + block.shape[1:])
+
+
+def reduce_two_level(terms, rows):
+    zh = lax.axis_index("zh")
+    ring = lax.axis_size("y")
+    narrow = terms.astype(jnp.bfloat16).reshape((ring, 2, rows) + terms.shape[1:])
+    moved = lax.all_to_all(narrow, "y", 0, 0)
+    partial = jnp.sum(moved.astype(jnp.float32), axis=0)
+    mine = jnp.where(zh == 0, partial[0], partial[1])
+    other = jnp.where(zh == 0, partial[1], partial[0])
+    got = lax.ppermute(other.astype(jnp.bfloat16), "zh", [(0, 1), (1, 0)])
+    return mine + got.astype(jnp.float32)
 
 
 def normalize(inputs, gain):
@@ -154,8 +162,8 @@
     kv_heads = kv_width // HD
     group_size = heads // kv_heads
     scale_factor = HD ** (-0.5)
-    count = lax.axis_size("ctx")
-    rank = lax.axis_index("ctx")
+    ring = lax.axis_size("y")
+    rank = lax.axis_index("zh") * ring + lax.axis_index("y")
     offset = rank * tok_rows
     query_pos = offset + jnp.arange(tok_rows, dtype=jnp.int32)
     gain = norm_gain[0]
@@ -173,15 +181,21 @@
         )
         return (flat.reshape(tok_rows, heads, HD), keys, values, wide, inverse)
 
+    key_pos = (
+        (jnp.arange(2, dtype=jnp.int32)[None, :, None] * ring + jnp.arange(ring, dtype=jnp.int32)[:, None, None])
+        * tok_rows
+        + jnp.arange(tok_rows, dtype=jnp.int32)[None, None, :]
+    ).reshape(-1)
+
     def allowed_of(segment):
         seg_query = lax.dynamic_slice_in_dim(segment, offset, tok_rows)
-        key_pos = jnp.arange(segment.shape[0], dtype=jnp.int32)
-        return (key_pos[None, :] <= query_pos[:, None]) & (seg_query[:, None] == segment[None, :])
+        seg_key = jnp.transpose(segment.reshape(2, ring, tok_rows), (1, 0, 2)).reshape(-1)
+        return (key_pos[None, :] <= query_pos[:, None]) & (seg_query[:, None] == seg_key[None, :])
 
     bwd_query, bwd_keys, bwd_values, bwd_wide, bwd_inverse = layer_parts(saved_bwd[0])
-    bwd_all = gather_all(jnp.concatenate([bwd_keys, bwd_values], axis=1), "ctx")
+    bwd_all = gather_two_level(jnp.concatenate([bwd_keys, bwd_values], axis=1))
     fwd_query, fwd_keys, fwd_values, fwd_wide, fwd_inverse = layer_parts(arrived)
-    fwd_all = gather_all(jnp.concatenate([fwd_keys, fwd_values], axis=1), "ctx")
+    fwd_all = gather_two_level(jnp.concatenate([fwd_keys, fwd_values], axis=1))
 
     bwd_key_all = bwd_all[:, :kv_width]
     bwd_value_all = bwd_all[:, kv_width:]
@@ -190,7 +204,7 @@
         allowed, bwd_query.reshape(tok_rows, width), bwd_key_all, bwd_value_all, upstream, group_size
     )
     dkv_terms = jnp.concatenate([dkey_terms, dvalue_terms], axis=1)
-    dkv_sum = reduce_all(dkv_terms, "ctx")
+    dkv_sum = reduce_two_level(dkv_terms, tok_rows)
     dkv = dkv_sum.astype(jnp.bfloat16)
     dkeys = dkv[:, :kv_width]
     dvalues = dkv[:, kv_width:]
@@ -219,10 +233,15 @@
 
 
 def solution(mesh):
+    sections, positions = mesh.devices.shape
+    split = jax.sharding.Mesh(
+        mesh.devices.reshape(sections, 2, positions // 2), ("section", "zh", "y")
+    )
+    rows = ("zh", "y")
     placed = (
-        P("section", "ctx", None),
-        P("section", "ctx", None),
-        P("section", "ctx", None),
+        P("section", rows, None),
+        P("section", rows, None),
+        P("section", rows, None),
         P("section", None),
         P("section", None, None),
         P("section", None, None),
@@ -231,8 +250,8 @@
     )
     return jax.shard_map(
         body,
-        mesh=mesh,
+        mesh=split,
         in_specs=placed,
-        out_specs=(P("section", "ctx", None), P("section", "ctx", None)),
+        out_specs=(P("section", rows, None), P("section", rows, None)),
         check_vma=False,
     )

time: 171 us -> 184 us (1.076)
  the two profiles are of different devices: /device:TPU:7 before, /device:TPU:6 now
where the time goes in v2:
time: 184 us; the launch traced here: 183 us
  waiting for transfers between devices  80.8 us (44%)
  Pallas kernels  42.1 us (23%)
  starting transfers between devices  19.3 us (10%)
  other arithmetic  14.8 us (8%)
  matrix products  13.7 us (7%)
  local copies, waits for them, and re-layouts  12 us (7%)
    all_to_all x2, waiting for transfers between devices, gather_two_level(): moved = lax.all_to_all(spread, 'y', 0, 0)  44.3 us
    pallas_call x1, Pallas kernels, attention_backward(): pl.pallas_call(kernel, grid=(groups,), in_specs=[pl.BlockSpec((rows, seq_...  27.2 us
    ppermute x2, waiting for transfers between devices, gather_two_level(): partner = lax.ppermute(block, 'zh', [(0, 1), (1, 0)])  23.8 us
    pallas_call x1, Pallas kernels, attention_forward(): pl.pallas_call(kernel, grid=(groups,), in_specs=[pl.BlockSpec((rows, seq_...  15 us
    all_to_all x1, waiting for transfers between devices, reduce_two_level(): moved = lax.all_to_all(narrow, 'y', 0, 0)  12.6 us
    all_to_all x2, starting transfers between devices, gather_two_level(): moved = lax.all_to_all(spread, 'y', 0, 0)  9.1 us
    dot_general x2, matrix products, layer_parts(): jnp.dot(flat, value_weight, preferred_element_type=jnp.float32)  6.52 us
    all_to_all x1, starting transfers between devices, reduce_two_level(): moved = lax.all_to_all(narrow, 'y', 0, 0)  4.45 us
  transfers between devices with their start and end apart: 8, of which 5 were waited for; matrix products, arithmetic and copies ran while one was open for 10% of the time, Pallas kernels for 8%

profile of v2, /device:TPU:6, one launch (start us, length us, event | category | flops | bytes accessed | tf_op | source)
XLA Modules:
  0.0 183.5 jit_solution(13594928996110328147)
XLA Ops:
  0.6 1.5 fusion.19
  2.2 0.0 copy-start
  2.2 0.0 copy-start.3
  2.2 0.0 copy-start.9
  2.2 3.4 %fusion.38 = bf16[128,512]{1,0:T(8,128)(2,1)S(1)} fusion(bf16[1,4096,512]{2,1,0:T(8,128)(2,1)} %param.13, bf16[1,128,4096]{2,1,0:T(8,128)(2,1)} %param.10, f32[128]{0:T(128)S(1)} %get-tuple-element.21, f32[4096]{0:T(1024)} %bitcast.102), kind=kOutput, calls=%fused_computation.40 | convolution fusion | flops 539033600 | bytes 5390848 | tf_op jit(solution)/shard_map/dot_general | solution.py:179
  5.6 0.0 copy-done
  5.6 0.6 copy-done.3
  6.3 0.0 copy-done.9
  6.3 0.8 fusion.32
  7.1 0.8 fusion.58
  7.8 3.9 %collective-permute-start.3 = (bf16[128,1024]{1,0:T(8,128)(2,1)}, bf16[128,1024]{1,0:T(8,128)(2,1)}, u32[]{:S(2)}, u32[]{:S(2)}) collective-permute-start(bf16[128,1024]{1,0:T(8,128)(2,1)} %get-tuple-element.13), channel_id=1, source_target_pairs={{0,4},{4,0},{1,5},{5,1},{2,6},{6,2},{3,7},{7,3},{8,12},{12,8},{9,1... | collective-permute-start | bytes 786440 | tf_op jit(solution)/shard_map/ppermute | solution.py:24
  11.7 0.0 collective-permute-start
  11.7 1.7 collective-permute-start.2
  13.5 0.0 copy-done.11
  13.5 0.1 dynamic_slice.6
  13.6 0.0 copy-done.10
  13.6 0.1 dynamic_slice.7
  13.7 0.1 iota_add_fusion
  13.7 15.8 %collective-permute-done.3 = bf16[128,1024]{1,0:T(8,128)(2,1)} collective-permute-done((bf16[128,1024]{1,0:T(8,128)(2,1)}, bf16[128,1024]{1,0:T(8,128)(2,1)}, u32[]{:S(2)}, u32[]{:S(2)}) %collective-permute-start.3) | collective-permute-done | bytes 262176 | tf_op jit(solution)/shard_map/ppermute | solution.py:24
  29.6 1.1 maximum_select_fusion.1
  30.7 1.6 broadcast_in_dim.10
  32.3 4.5 %all-to-all-start.1 = ((bf16[4,2,128,1024]{3,2,1,0:T(8,128)(2,1)}), bf16[4,2,128,1024]{3,2,1,0:T(8,128)(2,1)}, u32[]{:S(2)}, u32[]{:S(2)}) async-start(bf16[4,2,128,1024]{3,2,1,0:T(8,128)(2,1)} %broadcast_in_dim.10), calls=%async_computation.1 | async-start | bytes 4194304 | tf_op jit(solution)/shard_map/all_to_all | solution.py:28
  36.7 1.2 fusion.46
  37.9 0.0 collective-permute-done
  37.9 0.3 fusion.16
  38.2 2.1 %fusion.21 = (bf16[128,4096]{1,0:T(8,128)(2,1)}, bf16[128,4096]{1,0:T(8,128)(2,1)}) fusion(bf16[1,128,4096]{2,1,0:T(8,128)(2,1)S(1)} %copy-done, f32[128]{0:T(128)S(1)} %get-tuple-element.21, f32[4096]{0:T(1024)S(1)} %bitcast.104, f32[128]{0:T(128)S(1)} %add_rsqrt_fusion.1, bf16[1,128,4096]{2,1,0:T(8,128)(2,1)S(1)} %collective-permute-done), kind=kLoop, calls=%fused_computation.26 | loop fusion | flops 4194304 | bytes 4211712 | tf_op jit(solution)/shard_map/convert_element_type | solution.py:177
  40.4 22.4 %all-to-all-done.1 = bf16[4,2,128,1024]{3,2,1,0:T(8,128)(2,1)} async-done(((bf16[4,2,128,1024]{3,2,1,0:T(8,128)(2,1)}), bf16[4,2,128,1024]{3,2,1,0:T(8,128)(2,1)}, u32[]{:S(2)}, u32[]{:S(2)}) %all-to-all-start.1) | async-done | bytes 2097184 | tf_op jit(solution)/shard_map/all_to_all | solution.py:28
  62.8 3.0 %fusion.60 = (bf16[1024,512]{1,0:T(8,128)(2,1)}, bf16[1024,512]{1,0:T(8,128)(2,1)}) fusion(bf16[1024,1024]{1,0:T(8,128)(2,1)} %bitcast.21), kind=kLoop, calls=%fused_computation.68 | loop fusion | bytes 4194304 | tf_op jit(solution)/shard_map/slice | solution.py:201
  65.8 0.0 collective-permute-done.2
  65.8 1.0 copy-done.5
  66.8 27.2 %shard_map.96 = (f32[128,4096]{1,0:T(8,128)}, f32[1024,512]{1,0:T(8,128)}, f32[1024,512]{1,0:T(8,128)}) custom-call(s32[128,1024]{1,0:T(8,128)} %get-tuple-element.18.mask_ref, bf16[128,4096]{1,0:T(8,128)(2,1)} %get-tuple-element.16.query_ref, bf16[1024,512]{1,0:T(8,128)(2,1)} %get-tuple-element.9.key_ref, bf16[1024,512]{1,0:T(8,128)(2,1)} %get-tuple-element.8.value_ref, ...), custom_call_target="tpu_custom_call" | custom-call | tf_op jit(solution)/shard_map/pallas_call | solution.py:133
  93.9 1.9 %convert.9 = bf16[1024,512]{1,0:T(8,128)(2,1)S(1)} convert(f32[1024,512]{1,0:T(8,128)} %get-tuple-element.6) | non-fusion elementwise | flops 524288 | bytes 3145728 | tf_op jit(solution)/shard_map/convert.4
  95.8 0.3 copy-done.7
  96.2 0.1 convert.10
  96.3 1.6 pad_maximum_fusion
  97.9 4.5 %all-to-all-start.2 = ((bf16[4,2,128,1024]{3,2,1,0:T(8,128)(2,1)}), bf16[4,2,128,1024]{3,2,1,0:T(8,128)(2,1)}, u32[]{:S(2)}, u32[]{:S(2)}) async-start(bf16[4,2,128,1024]{3,2,1,0:T(8,128)(2,1)} %pad_maximum_fusion), calls=%async_computation.2 | async-start | bytes 4194304 | tf_op jit(solution)/shard_map/all_to_all | solution.py:36
  102.3 0.0 copy-start.4
  102.4 3.1 %fusion.35 = bf16[128,512]{1,0:T(8,128)(2,1)S(1)} fusion(bf16[1,4096,512]{2,1,0:T(8,128)(2,1)} %param.13, bf16[1,128,4096]{2,1,0:T(8,128)(2,1)S(1)} %collective-permute-done, f32[4096]{0:T(1024)S(1)} %bitcast.105, f32[128]{0:T(128)S(1)} %add_rsqrt_fusion.1), kind=kOutput, calls=%fused_computation.39 | convolution fusion | flops 539033600 | bytes 5390848 | tf_op jit(solution)/shard_map/dot_general | solution.py:179
  105.5 0.0 copy-done.1
  105.5 0.3 copy-done.4
  105.8 0.8 fusion.29
  106.6 0.1 fusion.59
  106.7 0.1 collective-permute-start.1
  106.8 8.0 %collective-permute-done.1 = bf16[128,1024]{1,0:T(8,128)(2,1)S(1)} collective-permute-done((bf16[128,1024]{1,0:T(8,128)(2,1)S(1)}, bf16[128,1024]{1,0:T(8,128)(2,1)S(1)}, u32[]{:S(2)}, u32[]{:S(2)}) %collective-permute-start.1) | collective-permute-done | bytes 262176 | tf_op jit(solution)/shard_map/ppermute | solution.py:24
  114.8 0.1 maximum_select_fusion
  114.8 12.6 %all-to-all-done.2 = bf16[4,2,128,1024]{3,2,1,0:T(8,128)(2,1)} async-done(((bf16[4,2,128,1024]{3,2,1,0:T(8,128)(2,1)}), bf16[4,2,128,1024]{3,2,1,0:T(8,128)(2,1)}, u32[]{:S(2)}, u32[]{:S(2)}) %all-to-all-start.2) | async-done | bytes 2097184 | tf_op jit(solution)/shard_map/all_to_all | solution.py:36
  127.5 1.6 broadcast_in_dim.8
  129.1 4.6 %all-to-all-start = ((bf16[4,2,128,1024]{3,2,1,0:T(8,128)(2,1)}), bf16[4,2,128,1024]{3,2,1,0:T(8,128)(2,1)}, u32[]{:S(2)}, u32[]{:S(2)}) async-start(bf16[4,2,128,1024]{3,2,1,0:T(8,128)(2,1)} %broadcast_in_dim.8), calls=%async_computation | async-start | bytes 4194304 | tf_op jit(solution)/shard_map/all_to_all | solution.py:28
  133.7 2.1 %convert_reduce_fusion = f32[2,128,1024]{2,1,0:T(8,128)S(1)} fusion(bf16[4,2,128,1024]{3,2,1,0:T(8,128)(2,1)} %all-to-all-done.2), kind=kLoop, calls=%fused_computation.12 | loop fusion | flops 1835008 | bytes 3145728 | tf_op jit(solution)/shard_map/reduce_sum | solution.py:37
  135.8 0.1 fusion.51
  135.9 0.1 collective-permute-start.4
  136.0 21.9 %all-to-all-done = bf16[4,2,128,1024]{3,2,1,0:T(8,128)(2,1)} async-done(((bf16[4,2,128,1024]{3,2,1,0:T(8,128)(2,1)}), bf16[4,2,128,1024]{3,2,1,0:T(8,128)(2,1)}, u32[]{:S(2)}, u32[]{:S(2)}) %all-to-all-start) | async-done | bytes 2097184 | tf_op jit(solution)/shard_map/all_to_all | solution.py:28
  157.8 3.0 %fusion.61 = (bf16[1024,512]{1,0:T(8,128)(2,1)}, bf16[1024,512]{1,0:T(8,128)(2,1)}) fusion(bf16[1024,1024]{1,0:T(8,128)(2,1)} %bitcast.11), kind=kLoop, calls=%fused_computation.69 | loop fusion | bytes 4194304 | tf_op jit(solution)/shard_map/slice | solution.py:213
  160.8 15.0 %shard_map.95 = bf16[128,4096]{1,0:T(8,128)(2,1)} custom-call(s32[128,1024]{1,0:T(8,128)} %get-tuple-element.19.mask_ref, bf16[128,4096]{1,0:T(8,128)(2,1)} %get-tuple-element.17.query_ref, bf16[1024,512]{1,0:T(8,128)(2,1)} %get-tuple-element.11.key_ref, bf16[1024,512]{1,0:T(8,128)(2,1)} %get-tuple-element.10.value_ref, bf16[128,4096]{1,0:T(8,128)(2,1)} %bitcast.96), custom_call_target="tpu_custom_call" | custom-call | tf_op jit(solution)/shard_map/pallas_call | solution.py:111
  175.8 0.0 collective-permute-done.4
  175.8 0.1 fusion.44
  175.9 0.0 copy-start.2
  175.9 0.0 copy-start.8
  175.9 3.8 %fusion.6 = f32[128,4096]{1,0:T(8,128)S(1)} fusion(bf16[1,4096,512]{2,1,0:T(8,128)(2,1)} %param.12, bf16[128,1024]{1,0:T(8,128)(2,1)S(1)} %fusion.44), kind=kOutput, calls=%fused_computation.6 | convolution fusion | flops 536870912 | bytes 6422528 | tf_op jit(solution)/shard_map/dot_general | solution.py:219
  179.7 0.0 copy-done.2
  179.7 0.3 copy-done.8
  180.0 1.7 fusion.26
  181.8 0.0 copy-done.6
  181.8 1.7 fusion.43
  (14 shorter events, 0.1 us)
Async XLA Ops:
  2.2 3.5 %copy-start = (bf16[1,128,4096]{2,1,0:T(8,128)(2,1)S(1)}, bf16[1,128,4096]{2,1,0:T(8,128)(2,1)}, u32[]{:S(2)}) copy-start(bf16[1,128,4096]{2,1,0:T(8,128)(2,1)} %param.10) | copy-start | bytes 3145732
  2.2 4.1 %copy-start.3 = (bf16[1,4096,512]{2,1,0:T(8,128)(2,1)S(1)}, bf16[1,4096,512]{2,1,0:T(8,128)(2,1)}, u32[]{:S(2)}) copy-start(bf16[1,4096,512]{2,1,0:T(8,128)(2,1)} %param.12) | copy-start | bytes 12582916
  2.2 4.1 %copy-start.9 = (f32[1,4096]{1,0:T(1,128)S(1)}, f32[1,4096]{1,0:T(1,128)}, u32[]{:S(2)}) copy-start(f32[1,4096]{1,0:T(1,128)} %param.11) | copy-start | bytes 49156
  6.3 7.2 %copy-start.11 = (s32[1024]{0:T(1024)S(1)}, s32[1024]{0:T(1024)}, u32[]{:S(2)}) copy-start(s32[1024]{0:T(1024)} %param.14) | copy-start | bytes 12292
  6.3 7.3 %copy-start.10 = (s32[1024]{0:T(1024)S(1)}, s32[1024]{0:T(1024)}, u32[]{:S(2)}) copy-start(s32[1024]{0:T(1024)} %param.15) | copy-start | bytes 12292
  7.8 21.7 %collective-permute-start.3 = (bf16[128,1024]{1,0:T(8,128)(2,1)}, bf16[128,1024]{1,0:T(8,128)(2,1)}, u32[]{:S(2)}, u32[]{:S(2)}) collective-permute-start(bf16[128,1024]{1,0:T(8,128)(2,1)} %get-tuple-element.13), channel_id=1, source_target_pairs={{0,4},{4,0},{1,5},{5,1},{2,6},{6,2},{3,7},{7,3},{8,12},{12,8},{9,1... | collective-permute-start | bytes 786440 | tf_op jit(solution)/shard_map/ppermute | solution.py:24
  11.7 26.2 %collective-permute-start = (bf16[1,128,4096]{2,1,0:T(8,128)(2,1)}, bf16[1,128,4096]{2,1,0:T(8,128)(2,1)S(1)}, u32[]{:S(2)}, u32[]{:S(2)}) collective-permute-start(bf16[1,128,4096]{2,1,0:T(8,128)(2,1)} %param.8), channel_id=1, source_target_pairs={{120,0},{0,8},{8,16},{16,24},{24,32},{32,40},{40,48},{48,56},{56,6... | collective-permute-start | bytes 3145736 | tf_op jit(solution)/shard_map/ppermute | solution.py:19
  11.7 54.1 %collective-permute-start.2 = (bf16[1,128,4096]{2,1,0:T(8,128)(2,1)}, bf16[1,128,4096]{2,1,0:T(8,128)(2,1)S(1)}, u32[]{:S(2)}, u32[]{:S(2)}) collective-permute-start(bf16[1,128,4096]{2,1,0:T(8,128)(2,1)} %param.9), channel_id=1, source_target_pairs={{8,0},{16,8},{24,16},{32,24},{40,32},{48,40},{56,48},{64,56},{72,6... | collective-permute-start | bytes 3145736 | tf_op jit(solution)/shard_map/ppermute | solution.py:19
  32.3 30.5 %all-to-all-start.1 = ((bf16[4,2,128,1024]{3,2,1,0:T(8,128)(2,1)}), bf16[4,2,128,1024]{3,2,1,0:T(8,128)(2,1)}, u32[]{:S(2)}, u32[]{:S(2)}) async-start(bf16[4,2,128,1024]{3,2,1,0:T(8,128)(2,1)} %broadcast_in_dim.10), calls=%async_computation.1 | async-start | bytes 4194304 | tf_op jit(solution)/shard_map/all_to_all | solution.py:28
  37.9 67.5 %copy-start.1 = (bf16[1,128,4096]{2,1,0:T(8,128)(2,1)}, bf16[1,128,4096]{2,1,0:T(8,128)(2,1)S(1)}, u32[]{:S(2)}) copy-start(bf16[1,128,4096]{2,1,0:T(8,128)(2,1)S(1)} %collective-permute-done) | copy-start | bytes 3145732
  65.8 1.0 copy-start.5
  93.9 2.2 %copy-start.7 = (f32[1024,512]{1,0:T(8,128)S(1)}, f32[1024,512]{1,0:T(8,128)}, u32[]{:S(2)}) copy-start(f32[1024,512]{1,0:T(8,128)} %get-tuple-element.7) | copy-start | bytes 6291460
  97.9 29.6 %all-to-all-start.2 = ((bf16[4,2,128,1024]{3,2,1,0:T(8,128)(2,1)}), bf16[4,2,128,1024]{3,2,1,0:T(8,128)(2,1)}, u32[]{:S(2)}, u32[]{:S(2)}) async-start(bf16[4,2,128,1024]{3,2,1,0:T(8,128)(2,1)} %pad_maximum_fusion), calls=%async_computation.2 | async-start | bytes 4194304 | tf_op jit(solution)/shard_map/all_to_all | solution.py:36
  102.3 3.5 %copy-start.4 = (bf16[1,4096,512]{2,1,0:T(8,128)(2,1)S(1)}, bf16[1,4096,512]{2,1,0:T(8,128)(2,1)}, u32[]{:S(2)}) copy-start(bf16[1,4096,512]{2,1,0:T(8,128)(2,1)} %param.12) | copy-start | bytes 12582916
  106.7 8.1 %collective-permute-start.1 = (bf16[128,1024]{1,0:T(8,128)(2,1)S(1)}, bf16[128,1024]{1,0:T(8,128)(2,1)S(1)}, u32[]{:S(2)}, u32[]{:S(2)}) collective-permute-start(bf16[128,1024]{1,0:T(8,128)(2,1)S(1)} %get-tuple-element.15), channel_id=1, source_target_pairs={{0,4},{4,0},{1,5},{5,1},{2,6},{6,2},{3,7},{7,3},{8,12},{12,8},{9,1... | collective-permute-start | bytes 786440 | tf_op jit(solution)/shard_map/ppermute | solution.py:24
  129.1 28.7 %all-to-all-start = ((bf16[4,2,128,1024]{3,2,1,0:T(8,128)(2,1)}), bf16[4,2,128,1024]{3,2,1,0:T(8,128)(2,1)}, u32[]{:S(2)}, u32[]{:S(2)}) async-start(bf16[4,2,128,1024]{3,2,1,0:T(8,128)(2,1)} %broadcast_in_dim.8), calls=%async_computation | async-start | bytes 4194304 | tf_op jit(solution)/shard_map/all_to_all | solution.py:28
  135.9 39.9 %collective-permute-start.4 = (bf16[128,1024]{1,0:T(8,128)(2,1)S(1)}, bf16[128,1024]{1,0:T(8,128)(2,1)S(1)}, u32[]{:S(2)}, u32[]{:S(2)}) collective-permute-start(bf16[128,1024]{1,0:T(8,128)(2,1)S(1)} %fusion.51), channel_id=1, source_target_pairs={{0,4},{4,0},{1,5},{5,1},{2,6},{6,2},{3,7},{7,3},{8,12},{12,8},{9,1... | collective-permute-start | bytes 786440 | tf_op jit(solution)/shard_map/ppermute | solution.py:40
  175.9 3.8 %copy-start.2 = (bf16[1,4096,512]{2,1,0:T(8,128)(2,1)S(1)}, bf16[1,4096,512]{2,1,0:T(8,128)(2,1)}, u32[]{:S(2)}) copy-start(bf16[1,4096,512]{2,1,0:T(8,128)(2,1)} %param.13) | copy-start | bytes 12582916
  175.9 4.1 %copy-start.8 = (f32[128,4096]{1,0:T(8,128)S(1)}, f32[128,4096]{1,0:T(8,128)}, u32[]{:S(2)}) copy-start(f32[128,4096]{1,0:T(8,128)} %get-tuple-element.5) | copy-start | bytes 6291460
  180.0 1.8 copy-start.6

commit v3 on v0

--- a/solution.py
+++ b/solution.py
@@ -186,21 +186,49 @@
     bwd_key_all = bwd_all[:, :kv_width]
     bwd_value_all = bwd_all[:, kv_width:]
     allowed = allowed_of(seg_bwd).astype(jnp.int32)
-    dquery, dkey_terms, dvalue_terms = attention_backward(
-        allowed, bwd_query.reshape(tok_rows, width), bwd_key_all, bwd_value_all, upstream, group_size
-    )
-    dkv_terms = jnp.concatenate([dkey_terms, dvalue_terms], axis=1)
-    dkv_sum = reduce_all(dkv_terms, "ctx")
-    dkv = dkv_sum.astype(jnp.bfloat16)
-    dkeys = dkv[:, :kv_width]
-    dvalues = dkv[:, kv_width:]
+    halves = 2
+    half_kv = kv_width // halves
+    half_q = width // halves
+    dquery_parts, dkey_parts, dvalue_parts = ([], [], [])
+    for half in range(halves):
+        kv_cols = slice(half * half_kv, (half + 1) * half_kv)
+        q_cols = slice(half * half_q, (half + 1) * half_q)
+        dquery_half, dkey_half, dvalue_half = attention_backward(
+            allowed,
+            bwd_query.reshape(tok_rows, width)[:, q_cols],
+            bwd_key_all[:, kv_cols],
+            bwd_value_all[:, kv_cols],
+            upstream[:, q_cols],
+            group_size,
+        )
+        if half == 0:
+            fwd_all, dkey_half, dvalue_half = lax.optimization_barrier((fwd_all, dkey_half, dvalue_half))
+        dkv_half = reduce_all(jnp.concatenate([dkey_half, dvalue_half], axis=1), "ctx").astype(jnp.bfloat16)
+        dquery_parts.append(dquery_half)
+        dkey_parts.append(dkv_half[:, :half_kv])
+        dvalue_parts.append(dkv_half[:, half_kv:])
+    dquery = jnp.concatenate(dquery_parts, axis=1)
+    dkeys = jnp.concatenate(dkey_parts, axis=1)
+    dvalues = jnp.concatenate(dvalue_parts, axis=1)
 
     key_piece = fwd_all[:, :kv_width]
     value_piece = fwd_all[:, kv_width:]
     allowed = allowed_of(seg_fwd).astype(jnp.int32)
-    fwd_out = attention_forward(
-        allowed, fwd_query.reshape(tok_rows, width), key_piece, value_piece, arrived, group_size
-    )
+    fwd_parts = []
+    for half in range(halves):
+        kv_cols = slice(half * half_kv, (half + 1) * half_kv)
+        q_cols = slice(half * half_q, (half + 1) * half_q)
+        fwd_parts.append(
+            attention_forward(
+                allowed,
+                fwd_query.reshape(tok_rows, width)[:, q_cols],
+                key_piece[:, kv_cols],
+                value_piece[:, kv_cols],
+                arrived[:, q_cols],
+                group_size,
+            )
+        )
+    fwd_out = jnp.concatenate(fwd_parts, axis=1)
 
     dnormed = dquery + jnp.dot(
         dkeys, jnp.transpose(key_weight), preferred_element_type=jnp.float32

time: 171 us -> 166 us (0.971)
  the two profiles are of different devices: /device:TPU:7 before, /device:TPU:6 now
where the time goes in v3:
time: 166 us; the launch traced here: 165 us
  Pallas kernels  46.7 us (28%)
  waiting for transfers between devices  46.1 us (28%)
  starting transfers between devices  27.4 us (17%)
  local copies, waits for them, and re-layouts  15.6 us (9%)
  other arithmetic  14 us (8%)
  matrix products  13.9 us (8%)
    all_to_all x2, waiting for transfers between devices, gather_all(): moved = lax.all_to_all(spread, axis, 0, 0)  34.2 us
    pallas_call x2, Pallas kernels, attention_backward(): pl.pallas_call(kernel, grid=(groups,), in_specs=[pl.BlockSpec((rows, seq_...  29.5 us
    pallas_call x2, Pallas kernels, attention_forward(): pl.pallas_call(kernel, grid=(groups,), in_specs=[pl.BlockSpec((rows, seq_...  17.2 us
    all_to_all x2, starting transfers between devices, reduce_all(): lax.all_to_all(terms.astype(jnp.bfloat16).reshape((count, rows) + terms.s...  13.1 us
    all_to_all x2, starting transfers between devices, gather_all(): moved = lax.all_to_all(spread, axis, 0, 0)  12.4 us
    all_to_all x2, waiting for transfers between devices, reduce_all(): lax.all_to_all(terms.astype(jnp.bfloat16).reshape((count, rows) + terms.s...  11.9 us
    dot_general x2, matrix products, layer_parts(): jnp.dot(flat, value_weight, preferred_element_type=jnp.float32)  6.53 us
    dot_general x1, matrix products, body(): jnp.dot(dkeys, jnp.transpose(key_weight), preferred_element_type=jnp.floa...  4.12 us
  transfers between devices with their start and end apart: 6, of which 3 were waited for; matrix products, arithmetic and copies ran while one was open for 15% of the time, Pallas kernels for 19%

profile of v3, /device:TPU:6, one launch (start us, length us, event | category | flops | bytes accessed | tf_op | source)
XLA Modules:
  0.0 164.5 jit_solution(5393655562495783378)
XLA Ops:
  0.6 0.1 collective-permute-start
  0.7 1.7 %collective-permute-start.1 = (bf16[1,128,4096]{2,1,0:T(8,128)(2,1)}, bf16[1,128,4096]{2,1,0:T(8,128)(2,1)S(1)}, u32[]{:S(2)}, u32[]{:S(2)}) collective-permute-start(bf16[1,128,4096]{2,1,0:T(8,128)(2,1)} %param.9), channel_id=1, source_target_pairs={{8,0},{16,8},{24,16},{32,24},{40,32},{48,40},{56,48},{64,56},{72,6... | collective-permute-start | bytes 3145736 | tf_op jit(solution)/shard_map/ppermute | solution.py:19
  2.4 1.5 fusion.18
  4.0 0.0 copy-start
  4.0 0.0 copy-start.2
  4.0 0.0 copy-start.10
  4.0 3.4 %fusion.37 = bf16[128,512]{1,0:T(8,128)(2,1)S(1)} fusion(bf16[1,4096,512]{2,1,0:T(8,128)(2,1)} %param.13, bf16[1,128,4096]{2,1,0:T(8,128)(2,1)} %param.10, f32[128]{0:T(128)S(1)} %get-tuple-element.43, f32[4096]{0:T(1024)} %bitcast.82), kind=kOutput, calls=%fused_computation.38 | convolution fusion | flops 539033600 | bytes 5390848 | tf_op jit(solution)/shard_map/dot_general | solution.py:171
  7.4 0.0 copy-done
  7.5 0.6 copy-done.2
  8.1 0.0 copy-done.10
  8.1 0.8 fusion.31
  8.9 1.6 broadcast_in_dim.9
  10.5 0.0 copy-start.12
  10.5 7.9 %all-to-all-start.1 = ((bf16[8,128,1024]{2,1,0:T(8,128)(2,1)}), bf16[8,128,1024]{2,1,0:T(8,128)(2,1)}, u32[]{:S(2)}, u32[]{:S(2)}) async-start(bf16[8,128,1024]{2,1,0:T(8,128)(2,1)} %broadcast_in_dim.9), calls=%async_computation.1 | async-start | bytes 4194304 | tf_op jit(solution)/shard_map/all_to_all | solution.py:25
  18.4 0.0 copy-done.12
  18.4 0.1 dynamic_slice.6
  18.5 0.0 copy-done.11
  18.5 0.1 dynamic_slice.7
  18.6 1.3 fusion.46
  19.8 0.0 collective-permute-done.1
  19.8 1.1 fusion.61
  21.0 0.0 collective-permute-done
  21.0 0.3 fusion.15
  21.2 0.0 copy-done.4
  21.3 0.6 fusion.20
  21.9 1.1 fusion.62
  22.9 24.1 %all-to-all-done.1 = bf16[8,128,1024]{2,1,0:T(8,128)(2,1)} async-done(((bf16[8,128,1024]{2,1,0:T(8,128)(2,1)}), bf16[8,128,1024]{2,1,0:T(8,128)(2,1)}, u32[]{:S(2)}, u32[]{:S(2)}) %all-to-all-start.1) | async-done | bytes 2097184 | tf_op jit(solution)/shard_map/all_to_all | solution.py:25
  47.0 2.9 %fusion.59 = (bf16[1024,256]{1,0:T(8,128)(2,1)}, bf16[1024,256]{1,0:T(8,128)(2,1)}, bf16[1024,256]{1,0:T(8,128)(2,1)}, bf16[1024,256]{1,0:T(8,128)(2,1)}) fusion(bf16[1024,1024]{1,0:T(8,128)(2,1)} %bitcast.8), kind=kLoop, calls=%fused_computation.65 | loop fusion | bytes 4194304 | tf_op jit(solution)/shard_map/slice | solution.py:200
  50.0 14.8 %shard_map.98 = (f32[128,2048]{1,0:T(8,128)}, f32[1024,256]{1,0:T(8,128)}, f32[1024,256]{1,0:T(8,128)}) custom-call(s32[128,1024]{1,0:T(8,128)} %get-tuple-element.44.mask_ref, bf16[128,2048]{1,0:T(8,128)(2,1)} %get-tuple-element.30.query_ref, bf16[1024,256]{1,0:T(8,128)(2,1)} %get-tuple-element.21.key_ref, bf16[1024,256]{1,0:T(8,128)(2,1)} %get-tuple-element.20.value_ref, ...), custom_call_target="tpu_custom_call" | custom-call | tf_op jit(solution)/shard_map/pallas_call | solution.py:125
  64.7 1.4 convert.21
  66.1 0.2 copy-done.8
  66.3 0.1 convert.22
  66.3 1.1 pad_maximum_fusion.1
  67.4 6.4 %all-to-all-start.3 = ((bf16[8,128,512]{2,1,0:T(8,128)(2,1)}), bf16[8,128,512]{2,1,0:T(8,128)(2,1)}, u32[]{:S(2)}, u32[]{:S(2)}) async-start(bf16[8,128,512]{2,1,0:T(8,128)(2,1)} %pad_maximum_fusion.1), calls=%async_computation.3 | async-start | bytes 2097152 | tf_op jit(solution)/shard_map/all_to_all | solution.py:32
  73.8 3.1 %fusion.34 = bf16[128,512]{1,0:T(8,128)(2,1)S(1)} fusion(bf16[1,4096,512]{2,1,0:T(8,128)(2,1)} %param.13, bf16[1,128,4096]{2,1,0:T(8,128)(2,1)S(1)} %collective-permute-done, f32[4096]{0:T(1024)S(1)} %bitcast.85, f32[128]{0:T(128)S(1)} %add_rsqrt_fusion.1), kind=kOutput, calls=%fused_computation.37 | convolution fusion | flops 539033600 | bytes 5390848 | tf_op jit(solution)/shard_map/dot_general | solution.py:171
  76.9 0.3 copy-done.3
  77.2 0.8 fusion.28
  78.1 11.9 %all-to-all-done.3 = bf16[8,128,512]{2,1,0:T(8,128)(2,1)} async-done(((bf16[8,128,512]{2,1,0:T(8,128)(2,1)}), bf16[8,128,512]{2,1,0:T(8,128)(2,1)}, u32[]{:S(2)}, u32[]{:S(2)}) %all-to-all-start.3) | async-done | bytes 1048608 | tf_op jit(solution)/shard_map/all_to_all | solution.py:32
  90.0 1.6 broadcast_in_dim.8
  91.6 4.5 %all-to-all-start = ((bf16[8,128,1024]{2,1,0:T(8,128)(2,1)}), bf16[8,128,1024]{2,1,0:T(8,128)(2,1)}, u32[]{:S(2)}, u32[]{:S(2)}) async-start(bf16[8,128,1024]{2,1,0:T(8,128)(2,1)} %broadcast_in_dim.8), calls=%async_computation | async-start | bytes 4194304 | tf_op jit(solution)/shard_map/all_to_all | solution.py:25
  96.1 1.1 fusion.63
  97.2 1.0 fusion.64
  98.2 14.7 %shard_map.95 = (f32[128,2048]{1,0:T(8,128)}, f32[1024,256]{1,0:T(8,128)}, f32[1024,256]{1,0:T(8,128)}) custom-call(s32[128,1024]{1,0:T(8,128)} %get-tuple-element.44.mask_ref, bf16[128,2048]{1,0:T(8,128)(2,1)} %get-tuple-element.31.query_ref, bf16[1024,256]{1,0:T(8,128)(2,1)} %get-tuple-element.23.key_ref, bf16[1024,256]{1,0:T(8,128)(2,1)} %get-tuple-element.22.value_ref, ...), custom_call_target="tpu_custom_call" | custom-call | tf_op jit(solution)/shard_map/pallas_call | solution.py:125
  113.0 1.5 reduce_sum.54
  114.4 10.1 %all-to-all-done = bf16[8,128,1024]{2,1,0:T(8,128)(2,1)} async-done(((bf16[8,128,1024]{2,1,0:T(8,128)(2,1)}), bf16[8,128,1024]{2,1,0:T(8,128)(2,1)}, u32[]{:S(2)}, u32[]{:S(2)}) %all-to-all-start) | async-done | bytes 2097184 | tf_op jit(solution)/shard_map/all_to_all | solution.py:25
  124.5 1.3 convert.19
  125.8 0.0 copy-done.7
  125.8 0.1 convert.20
  125.9 1.1 pad_maximum_fusion
  126.9 6.7 %all-to-all-start.2 = ((bf16[8,128,512]{2,1,0:T(8,128)(2,1)}), bf16[8,128,512]{2,1,0:T(8,128)(2,1)S(1)}, u32[]{:S(2)}, u32[]{:S(2)}) async-start(bf16[8,128,512]{2,1,0:T(8,128)(2,1)} %pad_maximum_fusion), calls=%async_computation.2 | async-start | bytes 2097152 | tf_op jit(solution)/shard_map/all_to_all | solution.py:32
  133.7 2.9 %fusion.60 = (bf16[1024,256]{1,0:T(8,128)(2,1)}, bf16[1024,256]{1,0:T(8,128)(2,1)}, bf16[1024,256]{1,0:T(8,128)(2,1)}, bf16[1024,256]{1,0:T(8,128)(2,1)}) fusion(bf16[1024,1024]{1,0:T(8,128)(2,1)} %bitcast.5), kind=kLoop, calls=%fused_computation.66 | loop fusion | bytes 4194304 | tf_op jit(solution)/shard_map/slice | solution.py:226
  136.6 8.6 %shard_map.97 = bf16[128,2048]{1,0:T(8,128)(2,1)} custom-call(s32[128,1024]{1,0:T(8,128)} %get-tuple-element.45.mask_ref, bf16[128,2048]{1,0:T(8,128)(2,1)} %get-tuple-element.35.query_ref, bf16[1024,256]{1,0:T(8,128)(2,1)} %get-tuple-element.26.key_ref, bf16[1024,256]{1,0:T(8,128)(2,1)} %get-tuple-element.25.value_ref, ...), custom_call_target="tpu_custom_call" | custom-call | tf_op jit(solution)/shard_map/pallas_call | solution.py:103
  145.2 8.6 %shard_map.96 = bf16[128,2048]{1,0:T(8,128)(2,1)} custom-call(s32[128,1024]{1,0:T(8,128)} %get-tuple-element.45.mask_ref, bf16[128,2048]{1,0:T(8,128)(2,1)} %get-tuple-element.34.query_ref, bf16[1024,256]{1,0:T(8,128)(2,1)} %get-tuple-element.27.key_ref, bf16[1024,256]{1,0:T(8,128)(2,1)} %get-tuple-element.24.value_ref, ...), custom_call_target="tpu_custom_call" | custom-call | tf_op jit(solution)/shard_map/pallas_call | solution.py:103
  153.8 0.0 copy-done.6
  153.8 2.1 %maximum_bitcast_fusion = bf16[1,128,4096]{2,1,0:T(8,128)(2,1)} fusion(bf16[128,2048]{1,0:T(8,128)(2,1)S(1)} %copy-done.6, bf16[128,2048]{1,0:T(8,128)(2,1)} %shard_map.96), kind=kLoop, calls=%fused_computation.42 | loop fusion | flops 2097152 | bytes 2097152 | tf_op jit(solution)/shard_map/broadcast_in_dim | solution.py:246
  155.9 0.0 all-to-all-done.2
  155.9 0.1 reduce_sum.53
  156.0 1.0 copy-done.9
  157.1 4.1 %convolution_add_fusion.1 = f32[128,4096]{1,0:T(8,128)S(1)} fusion(bf16[1,4096,512]{2,1,0:T(8,128)(2,1)} %param.12, f32[128,2048]{1,0:T(8,128)S(1)} %copy-done.9, f32[128,2048]{1,0:T(8,128)} %get-tuple-element.14, bf16[128,256]{1,0:T(8,128)(2,1)S(1)} %get-tuple-element.39, bf16[128,256]{1,0:T(8,128)(2,1)S(1)} %get-tuple-element.37), kind=kOutput, calls=%fused_computation.2 | convolution fusion | flops 538181632 | bytes 8519680 | tf_op jit(solution)/shard_map/dot_general | solution.py:233
  161.2 0.0 copy-done.1
  161.2 0.0 copy-start.5
  161.2 1.6 fusion.25
  162.8 0.0 copy-done.5
  162.9 1.7 %fusion.42 = bf16[1,128,4096]{2,1,0:T(8,128)(2,1)} fusion(bf16[1,128,4096]{2,1,0:T(8,128)(2,1)S(1)} %copy-done, f32[128,4096]{1,0:T(8,128)S(1)} %get-tuple-element.47, f32[128]{0:T(128)S(1)} %broadcast_multiply_fusion, f32[128]{0:T(128)S(1)} %get-tuple-element.42, f32[128]{0:T(128)S(1)} %get-tuple-element.43, bf16[1,128,4096]{2,1,0:T(8,128)(2,1)S(1)} %copy-done.5), kind=kLoop, calls=%fused_computation.41 | loop fusion | flops 4194304 | bytes 5244416 | tf_op jit(solution)/shard_map/broadcast_in_dim | solution.py:246
  (16 shorter events, 0.1 us)
Async XLA Ops:
  0.6 20.3 %collective-permute-start = (bf16[1,128,4096]{2,1,0:T(8,128)(2,1)}, bf16[1,128,4096]{2,1,0:T(8,128)(2,1)S(1)}, u32[]{:S(2)}, u32[]{:S(2)}) collective-permute-start(bf16[1,128,4096]{2,1,0:T(8,128)(2,1)} %param.8), channel_id=1, source_target_pairs={{120,0},{0,8},{8,16},{16,24},{24,32},{32,40},{40,48},{48,56},{56,6... | collective-permute-start | bytes 3145736 | tf_op jit(solution)/shard_map/ppermute | solution.py:19
  0.7 19.1 %collective-permute-start.1 = (bf16[1,128,4096]{2,1,0:T(8,128)(2,1)}, bf16[1,128,4096]{2,1,0:T(8,128)(2,1)S(1)}, u32[]{:S(2)}, u32[]{:S(2)}) collective-permute-start(bf16[1,128,4096]{2,1,0:T(8,128)(2,1)} %param.9), channel_id=1, source_target_pairs={{8,0},{16,8},{24,16},{32,24},{40,32},{48,40},{56,48},{64,56},{72,6... | collective-permute-start | bytes 3145736 | tf_op jit(solution)/shard_map/ppermute | solution.py:19
  4.0 3.5 %copy-start = (bf16[1,128,4096]{2,1,0:T(8,128)(2,1)S(1)}, bf16[1,128,4096]{2,1,0:T(8,128)(2,1)}, u32[]{:S(2)}) copy-start(bf16[1,128,4096]{2,1,0:T(8,128)(2,1)} %param.10) | copy-start | bytes 3145732
  4.0 4.1 %copy-start.2 = (bf16[1,4096,512]{2,1,0:T(8,128)(2,1)S(1)}, bf16[1,4096,512]{2,1,0:T(8,128)(2,1)}, u32[]{:S(2)}) copy-start(bf16[1,4096,512]{2,1,0:T(8,128)(2,1)} %param.12) | copy-start | bytes 12582916
  4.0 4.1 %copy-start.10 = (f32[1,4096]{1,0:T(1,128)S(1)}, f32[1,4096]{1,0:T(1,128)}, u32[]{:S(2)}) copy-start(f32[1,4096]{1,0:T(1,128)} %param.11) | copy-start | bytes 49156
  10.5 7.9 %copy-start.12 = (s32[1024]{0:T(1024)S(1)}, s32[1024]{0:T(1024)}, u32[]{:S(2)}) copy-start(s32[1024]{0:T(1024)} %param.14) | copy-start | bytes 12292
  10.5 8.0 %copy-start.11 = (s32[1024]{0:T(1024)S(1)}, s32[1024]{0:T(1024)}, u32[]{:S(2)}) copy-start(s32[1024]{0:T(1024)} %param.15) | copy-start | bytes 12292
  10.5 36.5 %all-to-all-start.1 = ((bf16[8,128,1024]{2,1,0:T(8,128)(2,1)}), bf16[8,128,1024]{2,1,0:T(8,128)(2,1)}, u32[]{:S(2)}, u32[]{:S(2)}) async-start(bf16[8,128,1024]{2,1,0:T(8,128)(2,1)} %broadcast_in_dim.9), calls=%async_computation.1 | async-start | bytes 4194304 | tf_op jit(solution)/shard_map/all_to_all | solution.py:25
  19.8 1.4 copy-start.4
  64.7 1.5 copy-start.8
  67.4 22.6 %all-to-all-start.3 = ((bf16[8,128,512]{2,1,0:T(8,128)(2,1)}), bf16[8,128,512]{2,1,0:T(8,128)(2,1)}, u32[]{:S(2)}, u32[]{:S(2)}) async-start(bf16[8,128,512]{2,1,0:T(8,128)(2,1)} %pad_maximum_fusion.1), calls=%async_computation.3 | async-start | bytes 2097152 | tf_op jit(solution)/shard_map/all_to_all | solution.py:32
  73.8 3.4 %copy-start.3 = (bf16[1,4096,512]{2,1,0:T(8,128)(2,1)S(1)}, bf16[1,4096,512]{2,1,0:T(8,128)(2,1)}, u32[]{:S(2)}) copy-start(bf16[1,4096,512]{2,1,0:T(8,128)(2,1)} %param.12) | copy-start | bytes 12582916
  91.6 33.0 %all-to-all-start = ((bf16[8,128,1024]{2,1,0:T(8,128)(2,1)}), bf16[8,128,1024]{2,1,0:T(8,128)(2,1)}, u32[]{:S(2)}, u32[]{:S(2)}) async-start(bf16[8,128,1024]{2,1,0:T(8,128)(2,1)} %broadcast_in_dim.8), calls=%async_computation | async-start | bytes 4194304 | tf_op jit(solution)/shard_map/all_to_all | solution.py:25
  113.0 12.9 %copy-start.7 = (f32[1024,256]{1,0:T(8,128)S(1)}, f32[1024,256]{1,0:T(8,128)}, u32[]{:S(2)}) copy-start(f32[1024,256]{1,0:T(8,128)} %get-tuple-element.17) | copy-start | bytes 3145732
  126.9 28.9 %all-to-all-start.2 = ((bf16[8,128,512]{2,1,0:T(8,128)(2,1)}), bf16[8,128,512]{2,1,0:T(8,128)(2,1)S(1)}, u32[]{:S(2)}, u32[]{:S(2)}) async-start(bf16[8,128,512]{2,1,0:T(8,128)(2,1)} %pad_maximum_fusion), calls=%async_computation.2 | async-start | bytes 2097152 | tf_op jit(solution)/shard_map/all_to_all | solution.py:32
  145.2 8.6 %copy-start.6 = (bf16[128,2048]{1,0:T(8,128)(2,1)S(1)}, bf16[128,2048]{1,0:T(8,128)(2,1)}, u32[]{:S(2)}) copy-start(bf16[128,2048]{1,0:T(8,128)(2,1)} %shard_map.97) | copy-start | bytes 1572868
  155.9 1.2 copy-start.9
  157.1 4.1 %copy-start.1 = (bf16[1,4096,512]{2,1,0:T(8,128)(2,1)S(1)}, bf16[1,4096,512]{2,1,0:T(8,128)(2,1)}, u32[]{:S(2)}) copy-start(bf16[1,4096,512]{2,1,0:T(8,128)(2,1)} %param.13) | copy-start | bytes 12582916
  161.2 1.6 copy-start.5

commit v4 on v3

--- a/solution.py
+++ b/solution.py
@@ -179,12 +179,23 @@
         return (key_pos[None, :] <= query_pos[:, None]) & (seg_query[:, None] == segment[None, :])
 
     bwd_query, bwd_keys, bwd_values, bwd_wide, bwd_inverse = layer_parts(saved_bwd[0])
-    bwd_all = gather_all(jnp.concatenate([bwd_keys, bwd_values], axis=1), "ctx")
+    bwd_half_kv = bwd_keys.shape[1] // 2
+    bwd_halves = [
+        gather_all(
+            jnp.concatenate(
+                [
+                    bwd_keys[:, half * bwd_half_kv:(half + 1) * bwd_half_kv],
+                    bwd_values[:, half * bwd_half_kv:(half + 1) * bwd_half_kv],
+                ],
+                axis=1,
+            ),
+            "ctx",
+        )
+        for half in range(2)
+    ]
     fwd_query, fwd_keys, fwd_values, fwd_wide, fwd_inverse = layer_parts(arrived)
     fwd_all = gather_all(jnp.concatenate([fwd_keys, fwd_values], axis=1), "ctx")
 
-    bwd_key_all = bwd_all[:, :kv_width]
-    bwd_value_all = bwd_all[:, kv_width:]
     allowed = allowed_of(seg_bwd).astype(jnp.int32)
     halves = 2
     half_kv = kv_width // halves
@@ -196,8 +207,8 @@
         dquery_half, dkey_half, dvalue_half = attention_backward(
             allowed,
             bwd_query.reshape(tok_rows, width)[:, q_cols],
-            bwd_key_all[:, kv_cols],
-            bwd_value_all[:, kv_cols],
+            bwd_halves[half][:, :half_kv],
+            bwd_halves[half][:, half_kv:],
             upstream[:, q_cols],
             group_size,
         )

time: 166 us -> 172 us (1.036)
  starting transfers between devices: 27.4 us -> 37 us
  waiting for transfers between devices: 46.1 us -> 39 us
  local copies, waits for them, and re-layouts: 15.6 us -> 17.8 us
    all_to_all x2 -> x3, starting transfers between devices: 12.4 us -> 21.2 us  [gather_all(): moved = lax.all_to_all(spread, axis, 0, 0)]
    all_to_all x2 -> x3, waiting for transfers between devices: 34.2 us -> 26.4 us  [gather_all(): moved = lax.all_to_all(spread, axis, 0, 0)]
    dot_general x2, matrix products: 6.53 us -> 3.9 us  [layer_parts(): jnp.dot(flat, value_weight, preferred_element_type=jnp.float32)]
    dot_general x2, matrix products: 1.61 us -> 4.24 us  [layer_parts(): jnp.dot(flat, key_weight, preferred_element_type=jnp.float32)]
    broadcast_in_dim x2 -> x3, local copies, waits for them, and re-layouts: 3.13 us -> 3.71 us  [gather_all(): spread = jnp.broadcast_to(block[None], (count,) + block.shape)]
  transfers between devices with their start and end apart: 6 -> 7, of which waited for: 3 -> 3; matrix products, arithmetic and copies ran while one was open for 15% -> 15% of each run, Pallas kernels for 19% -> 27%
where the time goes in v4:
time: 172 us; the launch traced here: 170 us
  Pallas kernels  46.7 us (27%)
  waiting for transfers between devices  39 us (23%)
  starting transfers between devices  37 us (22%)
  local copies, waits for them, and re-layouts  17.8 us (10%)
  other arithmetic  15.1 us (9%)
  matrix products  13.9 us (8%)
    pallas_call x2, Pallas kernels, attention_backward(): pl.pallas_call(kernel, grid=(groups,), in_specs=[pl.BlockSpec((rows, seq_...  29.5 us
    all_to_all x3, waiting for transfers between devices, gather_all(): moved = lax.all_to_all(spread, axis, 0, 0)  26.4 us
    all_to_all x3, starting transfers between devices, gather_all(): moved = lax.all_to_all(spread, axis, 0, 0)  21.2 us
    pallas_call x2, Pallas kernels, attention_forward(): pl.pallas_call(kernel, grid=(groups,), in_specs=[pl.BlockSpec((rows, seq_...  17.2 us
    all_to_all x2, starting transfers between devices, reduce_all(): lax.all_to_all(terms.astype(jnp.bfloat16).reshape((count, rows) + terms.s...  14 us
    all_to_all x2, waiting for transfers between devices, reduce_all(): lax.all_to_all(terms.astype(jnp.bfloat16).reshape((count, rows) + terms.s...  12.6 us
    broadcast_in_dim x2, other arithmetic, body(): return (fwd_out[None], grad_out[None])  4.98 us
    dot_general x2, matrix products, layer_parts(): jnp.dot(flat, key_weight, preferred_element_type=jnp.float32)  4.24 us
  transfers between devices with their start and end apart: 7, of which 3 were waited for; matrix products, arithmetic and copies ran while one was open for 15% of the time, Pallas kernels for 27%

profile of v4, /device:TPU:6, one launch (start us, length us, event | category | flops | bytes accessed | tf_op | source)
XLA Modules:
  0.0 170.3 jit_solution(11146322043168664246)
XLA Ops:
  0.6 1.5 fusion.18
  2.2 0.0 copy-start.1
  2.2 0.0 copy-start.8
  2.2 3.4 %fusion.31 = bf16[128,512]{1,0:T(8,128)(2,1)S(1)} fusion(bf16[1,4096,512]{2,1,0:T(8,128)(2,1)} %param.12, bf16[1,128,4096]{2,1,0:T(8,128)(2,1)} %param.10, f32[128]{0:T(128)S(1)} %get-tuple-element.47, f32[4096]{0:T(1024)} %bitcast.83), kind=kOutput, calls=%fused_computation.36 | convolution fusion | flops 539033600 | bytes 5390848 | tf_op jit(solution)/shard_map/dot_general | solution.py:170
  5.6 0.0 copy-done
  5.6 0.6 copy-done.1
  6.3 0.0 copy-done.8
  6.3 0.8 fusion.37
  7.1 0.0 copy-start.9
  7.1 0.0 copy-start.10
  7.1 1.1 broadcast_in_dim.13
  8.2 7.8 %all-to-all-start.2 = ((bf16[8,128,512]{2,1,0:T(8,128)(2,1)}), bf16[8,128,512]{2,1,0:T(8,128)(2,1)S(1)}, u32[]{:S(2)}, u32[]{:S(2)}) async-start(bf16[8,128,512]{2,1,0:T(8,128)(2,1)} %broadcast_in_dim.13), calls=%async_computation.2 | async-start | bytes 2097152 | tf_op jit(solution)/shard_map/all_to_all | solution.py:25
  16.0 0.0 collective-permute-start
  16.0 1.7 %collective-permute-start.1 = (bf16[1,128,4096]{2,1,0:T(8,128)(2,1)}, bf16[1,128,4096]{2,1,0:T(8,128)(2,1)}, u32[]{:S(2)}, u32[]{:S(2)}) collective-permute-start(bf16[1,128,4096]{2,1,0:T(8,128)(2,1)} %param.9), channel_id=1, source_target_pairs={{8,0},{16,8},{24,16},{32,24},{40,32},{48,40},{56,48},{64,56},{72,6... | collective-permute-start | bytes 3145736 | tf_op jit(solution)/shard_map/ppermute | solution.py:19
  17.7 0.0 copy-done.9
  17.7 0.1 dynamic_slice.7
  17.8 0.0 copy-done.10
  17.8 0.1 dynamic_slice.6
  17.9 1.3 fusion.46
  19.2 18.5 %all-to-all-done.2 = bf16[8,128,512]{2,1,0:T(8,128)(2,1)S(1)} async-done(((bf16[8,128,512]{2,1,0:T(8,128)(2,1)}), bf16[8,128,512]{2,1,0:T(8,128)(2,1)S(1)}, u32[]{:S(2)}, u32[]{:S(2)}) %all-to-all-start.2) | async-done | bytes 1048608 | tf_op jit(solution)/shard_map/all_to_all | solution.py:25
  37.6 1.1 broadcast_in_dim.11
  38.7 8.9 %all-to-all-start.1 = ((bf16[8,128,512]{2,1,0:T(8,128)(2,1)}), bf16[8,128,512]{2,1,0:T(8,128)(2,1)}, u32[]{:S(2)}, u32[]{:S(2)}) async-start(bf16[8,128,512]{2,1,0:T(8,128)(2,1)} %broadcast_in_dim.11), calls=%async_computation.1 | async-start | bytes 2097152 | tf_op jit(solution)/shard_map/all_to_all | solution.py:25
  47.6 1.1 fusion.61
  48.7 0.0 collective-permute-done
  48.7 0.3 fusion.15
  49.0 0.6 fusion.20
  49.6 1.1 fusion.62
  50.7 0.0 collective-permute-done.1
  50.7 2.3 %fusion.60 = (bf16[128,2048]{1,0:T(8,128)(2,1)}, bf16[128,2048]{1,0:T(8,128)(2,1)}) fusion(bf16[128,4096]{1,0:T(8,128)(2,1)} %bitcast.9), kind=kLoop, calls=%fused_computation.67 | loop fusion | bytes 2097152 | tf_op jit(solution)/shard_map/slice | solution.py:212
  53.0 14.7 %shard_map.98 = (f32[128,2048]{1,0:T(8,128)}, f32[1024,256]{1,0:T(8,128)}, f32[1024,256]{1,0:T(8,128)}) custom-call(s32[128,1024]{1,0:T(8,128)} %get-tuple-element.48.mask_ref, bf16[128,2048]{1,0:T(8,128)(2,1)} %get-tuple-element.28.query_ref, bf16[1024,256]{1,0:T(8,128)(2,1)} %get-tuple-element.27.key_ref, bf16[1024,256]{1,0:T(8,128)(2,1)} %get-tuple-element.26.value_ref, ...), custom_call_target="tpu_custom_call" | custom-call | tf_op jit(solution)/shard_map/pallas_call | solution.py:125
  67.7 1.4 convert.22
  69.1 0.2 copy-done.6
  69.3 0.1 convert.21
  69.3 1.1 pad_maximum_fusion.1
  70.4 0.0 all-to-all-done.1
  70.4 7.2 %all-to-all-start.4 = ((bf16[8,128,512]{2,1,0:T(8,128)(2,1)}), bf16[8,128,512]{2,1,0:T(8,128)(2,1)}, u32[]{:S(2)}, u32[]{:S(2)}) async-start(bf16[8,128,512]{2,1,0:T(8,128)(2,1)} %pad_maximum_fusion.1), calls=%async_computation.4 | async-start | bytes 2097152 | tf_op jit(solution)/shard_map/all_to_all | solution.py:32
  77.6 3.1 %fusion.34 = bf16[128,512]{1,0:T(8,128)(2,1)S(1)} fusion(bf16[1,4096,512]{2,1,0:T(8,128)(2,1)} %param.13, bf16[1,128,4096]{2,1,0:T(8,128)(2,1)S(1)} %collective-permute-done, f32[4096]{0:T(1024)S(1)} %bitcast.86, f32[128]{0:T(128)S(1)} %add_rsqrt_fusion.1), kind=kOutput, calls=%fused_computation.37 | convolution fusion | flops 539033600 | bytes 5390848 | tf_op jit(solution)/shard_map/dot_general | solution.py:171
  80.7 0.3 copy-done.3
  81.1 0.8 fusion.28
  81.9 12.6 %all-to-all-done.4 = bf16[8,128,512]{2,1,0:T(8,128)(2,1)} async-done(((bf16[8,128,512]{2,1,0:T(8,128)(2,1)}), bf16[8,128,512]{2,1,0:T(8,128)(2,1)}, u32[]{:S(2)}, u32[]{:S(2)}) %all-to-all-start.4) | async-done | bytes 1048608 | tf_op jit(solution)/shard_map/all_to_all | solution.py:32
  94.5 1.6 broadcast_in_dim.10
  96.1 4.5 %all-to-all-start = ((bf16[8,128,1024]{2,1,0:T(8,128)(2,1)}), bf16[8,128,1024]{2,1,0:T(8,128)(2,1)}, u32[]{:S(2)}, u32[]{:S(2)}) async-start(bf16[8,128,1024]{2,1,0:T(8,128)(2,1)} %broadcast_in_dim.10), calls=%async_computation | async-start | bytes 4194304 | tf_op jit(solution)/shard_map/all_to_all | solution.py:25
  100.6 2.3 %fusion.65 = (bf16[1024,256]{1,0:T(8,128)(2,1)}, bf16[1024,256]{1,0:T(8,128)(2,1)}) fusion(bf16[1024,512]{1,0:T(8,128)(2,1)} %bitcast.8), kind=kLoop, calls=%fused_computation.72 | loop fusion | bytes 2097152 | tf_op jit(solution)/shard_map/slice | solution.py:211
  102.9 14.8 %shard_map.95 = (f32[128,2048]{1,0:T(8,128)}, f32[1024,256]{1,0:T(8,128)}, f32[1024,256]{1,0:T(8,128)}) custom-call(s32[128,1024]{1,0:T(8,128)} %get-tuple-element.48.mask_ref, bf16[128,2048]{1,0:T(8,128)(2,1)} %get-tuple-element.29.query_ref, bf16[1024,256]{1,0:T(8,128)(2,1)} %get-tuple-element.35.key_ref, bf16[1024,256]{1,0:T(8,128)(2,1)} %get-tuple-element.34.value_ref, ...), custom_call_target="tpu_custom_call" | custom-call | tf_op jit(solution)/shard_map/pallas_call | solution.py:125
  117.7 1.1 fusion.64
  118.7 1.1 fusion.63
  119.8 1.4 reduce_sum.54
  121.2 7.9 %all-to-all-done = bf16[8,128,1024]{2,1,0:T(8,128)(2,1)} async-done(((bf16[8,128,1024]{2,1,0:T(8,128)(2,1)}), bf16[8,128,1024]{2,1,0:T(8,128)(2,1)}, u32[]{:S(2)}, u32[]{:S(2)}) %all-to-all-start) | async-done | bytes 2097184 | tf_op jit(solution)/shard_map/all_to_all | solution.py:25
  129.1 1.3 convert.20
  130.4 0.0 copy-done.5
  130.4 0.1 convert.19
  130.4 1.1 pad_maximum_fusion
  131.5 6.7 %all-to-all-start.3 = ((bf16[8,128,512]{2,1,0:T(8,128)(2,1)}), bf16[8,128,512]{2,1,0:T(8,128)(2,1)S(1)}, u32[]{:S(2)}, u32[]{:S(2)}) async-start(bf16[8,128,512]{2,1,0:T(8,128)(2,1)} %pad_maximum_fusion), calls=%async_computation.3 | async-start | bytes 2097152 | tf_op jit(solution)/shard_map/all_to_all | solution.py:32
  138.2 2.9 %fusion.59 = (bf16[1024,256]{1,0:T(8,128)(2,1)}, bf16[1024,256]{1,0:T(8,128)(2,1)}, bf16[1024,256]{1,0:T(8,128)(2,1)}, bf16[1024,256]{1,0:T(8,128)(2,1)}) fusion(bf16[1024,1024]{1,0:T(8,128)(2,1)} %bitcast.5), kind=kLoop, calls=%fused_computation.66 | loop fusion | bytes 4194304 | tf_op jit(solution)/shard_map/slice | solution.py:237
  141.1 8.6 %shard_map.97 = bf16[128,2048]{1,0:T(8,128)(2,1)} custom-call(s32[128,1024]{1,0:T(8,128)} %get-tuple-element.49.mask_ref, bf16[128,2048]{1,0:T(8,128)(2,1)} %get-tuple-element.33.query_ref, bf16[1024,256]{1,0:T(8,128)(2,1)} %get-tuple-element.22.key_ref, bf16[1024,256]{1,0:T(8,128)(2,1)} %get-tuple-element.21.value_ref, ...), custom_call_target="tpu_custom_call" | custom-call | tf_op jit(solution)/shard_map/pallas_call | solution.py:103
  149.7 8.6 %shard_map.96 = bf16[128,2048]{1,0:T(8,128)(2,1)} custom-call(s32[128,1024]{1,0:T(8,128)} %get-tuple-element.49.mask_ref, bf16[128,2048]{1,0:T(8,128)(2,1)} %get-tuple-element.32.query_ref, bf16[1024,256]{1,0:T(8,128)(2,1)} %get-tuple-element.23.key_ref, bf16[1024,256]{1,0:T(8,128)(2,1)} %get-tuple-element.20.value_ref, ...), custom_call_target="tpu_custom_call" | custom-call | tf_op jit(solution)/shard_map/pallas_call | solution.py:103
  158.3 0.0 copy-done.4
  158.3 2.1 %maximum_bitcast_fusion = bf16[1,128,4096]{2,1,0:T(8,128)(2,1)} fusion(bf16[128,2048]{1,0:T(8,128)(2,1)S(1)} %copy-done.4, bf16[128,2048]{1,0:T(8,128)(2,1)} %shard_map.96), kind=kLoop, calls=%fused_computation.42 | loop fusion | flops 2097152 | bytes 2097152 | tf_op jit(solution)/shard_map/broadcast_in_dim | solution.py:257
  160.4 0.0 all-to-all-done.3
  160.4 0.1 reduce_sum.53
  160.6 1.0 copy-done.7
  161.6 4.1 %convolution_add_fusion.1 = f32[128,4096]{1,0:T(8,128)S(1)} fusion(bf16[1,4096,512]{2,1,0:T(8,128)(2,1)} %param.12, f32[128,2048]{1,0:T(8,128)S(1)} %copy-done.7, f32[128,2048]{1,0:T(8,128)} %get-tuple-element.14, bf16[128,256]{1,0:T(8,128)(2,1)S(1)} %get-tuple-element.39, bf16[128,256]{1,0:T(8,128)(2,1)S(1)} %get-tuple-element.37), kind=kOutput, calls=%fused_computation.2 | convolution fusion | flops 538181632 | bytes 8519680 | tf_op jit(solution)/shard_map/dot_general | solution.py:244
  165.8 1.6 fusion.25
  167.4 2.9 %fusion.42 = bf16[1,128,4096]{2,1,0:T(8,128)(2,1)} fusion(bf16[1,128,4096]{2,1,0:T(8,128)(2,1)S(1)} %copy-done, f32[128,4096]{1,0:T(8,128)S(1)} %get-tuple-element.51, f32[128]{0:T(128)S(1)} %broadcast_multiply_fusion, f32[128]{0:T(128)S(1)} %get-tuple-element.46, f32[128]{0:T(128)S(1)} %get-tuple-element.47, bf16[1,128,4096]{2,1,0:T(8,128)(2,1)} %collective-permute-done.1), kind=kLoop, calls=%fused_computation.41 | loop fusion | flops 4194304 | bytes 5244416 | tf_op jit(solution)/shard_map/broadcast_in_dim | solution.py:257
  (18 shorter events, 0.1 us)
Async XLA Ops:
  2.2 3.5 %copy-start = (bf16[1,128,4096]{2,1,0:T(8,128)(2,1)S(1)}, bf16[1,128,4096]{2,1,0:T(8,128)(2,1)}, u32[]{:S(2)}) copy-start(bf16[1,128,4096]{2,1,0:T(8,128)(2,1)} %param.10) | copy-start | bytes 3145732
  2.2 4.1 %copy-start.1 = (bf16[1,4096,512]{2,1,0:T(8,128)(2,1)S(1)}, bf16[1,4096,512]{2,1,0:T(8,128)(2,1)}, u32[]{:S(2)}) copy-start(bf16[1,4096,512]{2,1,0:T(8,128)(2,1)} %param.13) | copy-start | bytes 12582916
  2.2 4.1 %copy-start.8 = (f32[1,4096]{1,0:T(1,128)S(1)}, f32[1,4096]{1,0:T(1,128)}, u32[]{:S(2)}) copy-start(f32[1,4096]{1,0:T(1,128)} %param.11) | copy-start | bytes 49156
  7.1 10.7 %copy-start.9 = (s32[1024]{0:T(1024)S(1)}, s32[1024]{0:T(1024)}, u32[]{:S(2)}) copy-start(s32[1024]{0:T(1024)} %param.15) | copy-start | bytes 12292
  7.1 10.7 %copy-start.10 = (s32[1024]{0:T(1024)S(1)}, s32[1024]{0:T(1024)}, u32[]{:S(2)}) copy-start(s32[1024]{0:T(1024)} %param.14) | copy-start | bytes 12292
  8.2 29.4 %all-to-all-start.2 = ((bf16[8,128,512]{2,1,0:T(8,128)(2,1)}), bf16[8,128,512]{2,1,0:T(8,128)(2,1)S(1)}, u32[]{:S(2)}, u32[]{:S(2)}) async-start(bf16[8,128,512]{2,1,0:T(8,128)(2,1)} %broadcast_in_dim.13), calls=%async_computation.2 | async-start | bytes 2097152 | tf_op jit(solution)/shard_map/all_to_all | solution.py:25
  16.0 32.7 %collective-permute-start = (bf16[1,128,4096]{2,1,0:T(8,128)(2,1)}, bf16[1,128,4096]{2,1,0:T(8,128)(2,1)S(1)}, u32[]{:S(2)}, u32[]{:S(2)}) collective-permute-start(bf16[1,128,4096]{2,1,0:T(8,128)(2,1)} %param.8), channel_id=1, source_target_pairs={{120,0},{0,8},{8,16},{16,24},{24,32},{32,40},{40,48},{48,56},{56,6... | collective-permute-start | bytes 3145736 | tf_op jit(solution)/shard_map/ppermute | solution.py:19
  16.0 34.7 %collective-permute-start.1 = (bf16[1,128,4096]{2,1,0:T(8,128)(2,1)}, bf16[1,128,4096]{2,1,0:T(8,128)(2,1)}, u32[]{:S(2)}, u32[]{:S(2)}) collective-permute-start(bf16[1,128,4096]{2,1,0:T(8,128)(2,1)} %param.9), channel_id=1, source_target_pairs={{8,0},{16,8},{24,16},{32,24},{40,32},{48,40},{56,48},{64,56},{72,6... | collective-permute-start | bytes 3145736 | tf_op jit(solution)/shard_map/ppermute | solution.py:19
  38.7 31.6 %all-to-all-start.1 = ((bf16[8,128,512]{2,1,0:T(8,128)(2,1)}), bf16[8,128,512]{2,1,0:T(8,128)(2,1)}, u32[]{:S(2)}, u32[]{:S(2)}) async-start(bf16[8,128,512]{2,1,0:T(8,128)(2,1)} %broadcast_in_dim.11), calls=%async_computation.1 | async-start | bytes 2097152 | tf_op jit(solution)/shard_map/all_to_all | solution.py:25
  67.7 1.5 copy-start.6
  70.4 24.1 %all-to-all-start.4 = ((bf16[8,128,512]{2,1,0:T(8,128)(2,1)}), bf16[8,128,512]{2,1,0:T(8,128)(2,1)}, u32[]{:S(2)}, u32[]{:S(2)}) async-start(bf16[8,128,512]{2,1,0:T(8,128)(2,1)} %pad_maximum_fusion.1), calls=%async_computation.4 | async-start | bytes 2097152 | tf_op jit(solution)/shard_map/all_to_all | solution.py:32
  77.6 3.4 %copy-start.3 = (bf16[1,4096,512]{2,1,0:T(8,128)(2,1)S(1)}, bf16[1,4096,512]{2,1,0:T(8,128)(2,1)}, u32[]{:S(2)}) copy-start(bf16[1,4096,512]{2,1,0:T(8,128)(2,1)} %param.12) | copy-start | bytes 12582916
  96.1 33.0 %all-to-all-start = ((bf16[8,128,1024]{2,1,0:T(8,128)(2,1)}), bf16[8,128,1024]{2,1,0:T(8,128)(2,1)}, u32[]{:S(2)}, u32[]{:S(2)}) async-start(bf16[8,128,1024]{2,1,0:T(8,128)(2,1)} %broadcast_in_dim.10), calls=%async_computation | async-start | bytes 4194304 | tf_op jit(solution)/shard_map/all_to_all | solution.py:25
  118.7 11.6 %copy-start.5 = (f32[1024,256]{1,0:T(8,128)S(1)}, f32[1024,256]{1,0:T(8,128)}, u32[]{:S(2)}) copy-start(f32[1024,256]{1,0:T(8,128)} %get-tuple-element.16) | copy-start | bytes 3145732
  131.5 28.9 %all-to-all-start.3 = ((bf16[8,128,512]{2,1,0:T(8,128)(2,1)}), bf16[8,128,512]{2,1,0:T(8,128)(2,1)S(1)}, u32[]{:S(2)}, u32[]{:S(2)}) async-start(bf16[8,128,512]{2,1,0:T(8,128)(2,1)} %pad_maximum_fusion), calls=%async_computation.3 | async-start | bytes 2097152 | tf_op jit(solution)/shard_map/all_to_all | solution.py:32
  149.7 8.6 %copy-start.4 = (bf16[128,2048]{1,0:T(8,128)(2,1)S(1)}, bf16[128,2048]{1,0:T(8,128)(2,1)}, u32[]{:S(2)}) copy-start(bf16[128,2048]{1,0:T(8,128)(2,1)} %shard_map.97) | copy-start | bytes 1572868
  160.4 1.2 copy-start.7
  161.6 4.1 %copy-start.2 = (bf16[1,4096,512]{2,1,0:T(8,128)(2,1)S(1)}, bf16[1,4096,512]{2,1,0:T(8,128)(2,1)}, u32[]{:S(2)}) copy-start(bf16[1,4096,512]{2,1,0:T(8,128)(2,1)} %param.13) | copy-start | bytes 12582916

commit v5 on v3

--- a/solution.py
+++ b/solution.py
@@ -179,9 +179,10 @@
         return (key_pos[None, :] <= query_pos[:, None]) & (seg_query[:, None] == segment[None, :])
 
     bwd_query, bwd_keys, bwd_values, bwd_wide, bwd_inverse = layer_parts(saved_bwd[0])
-    bwd_all = gather_all(jnp.concatenate([bwd_keys, bwd_values], axis=1), "ctx")
     fwd_query, fwd_keys, fwd_values, fwd_wide, fwd_inverse = layer_parts(arrived)
-    fwd_all = gather_all(jnp.concatenate([fwd_keys, fwd_values], axis=1), "ctx")
+    both_all = gather_all(jnp.concatenate([bwd_keys, bwd_values, fwd_keys, fwd_values], axis=1), "ctx")
+    bwd_all = both_all[:, :2 * kv_width]
+    fwd_all = both_all[:, 2 * kv_width:]
 
     bwd_key_all = bwd_all[:, :kv_width]
     bwd_value_all = bwd_all[:, kv_width:]
@@ -201,8 +202,6 @@
             upstream[:, q_cols],
             group_size,
         )
-        if half == 0:
-            fwd_all, dkey_half, dvalue_half = lax.optimization_barrier((fwd_all, dkey_half, dvalue_half))
         dkv_half = reduce_all(jnp.concatenate([dkey_half, dvalue_half], axis=1), "ctx").astype(jnp.bfloat16)
         dquery_parts.append(dquery_half)
         dkey_parts.append(dkv_half[:, :half_kv])

time: 166 us -> 177 us (1.066)
  waiting for transfers between devices: 46.1 us -> 62.3 us
  local copies, waits for them, and re-layouts: 15.6 us -> 12.7 us
  other arithmetic: 14 us -> 16.6 us
  matrix products: 13.9 us -> 11.3 us
  starting transfers between devices: 27.4 us -> 25.6 us
    ppermute x2, waiting for transfers between devices: 0.01 us -> 17.6 us  [shifted(): return lax.ppermute(block, axis, route)]
    all_to_all x2, waiting for transfers between devices: 11.9 us -> 0.01 us  [reduce_all(): lax.all_to_all(terms.astype(jnp.bfloat16).reshape((count, rows) + terms.s...]
    all_to_all x2 -> x1, waiting for transfers between devices: 34.2 us -> 44.7 us  [gather_all(): moved = lax.all_to_all(spread, axis, 0, 0)]
    all_to_all x2, starting transfers between devices: 13.1 us -> 17.6 us  [reduce_all(): lax.all_to_all(terms.astype(jnp.bfloat16).reshape((count, rows) + terms.s...]
    all_to_all x2 -> x1, starting transfers between devices: 12.4 us -> 7.92 us  [gather_all(): moved = lax.all_to_all(spread, axis, 0, 0)]
    slice x2 -> x0, local copies, waits for them, and re-layouts: 3.93 us -> none  [the longest x1 2.9 us: body(): value_piece[:, kv_cols]]
    dot_general x2, matrix products: 6.53 us -> 4.24 us  [layer_parts(): jnp.dot(flat, value_weight, preferred_element_type=jnp.float32)]
  transfers between devices with their start and end apart: 6 -> 5, of which waited for: 3 -> 3; matrix products, arithmetic and copies ran while one was open for 15% -> 11% of each run, Pallas kernels for 19% -> 18%
where the time goes in v5:
time: 177 us; the launch traced here: 176 us
  waiting for transfers between devices  62.3 us (35%)
  Pallas kernels  46.7 us (26%)
  starting transfers between devices  25.6 us (14%)
  other arithmetic  16.6 us (9%)
  local copies, waits for them, and re-layouts  12.7 us (7%)
  matrix products  11.3 us (6%)
    all_to_all x1, waiting for transfers between devices, gather_all(): moved = lax.all_to_all(spread, axis, 0, 0)  44.7 us
    pallas_call x2, Pallas kernels, attention_backward(): pl.pallas_call(kernel, grid=(groups,), in_specs=[pl.BlockSpec((rows, seq_...  29.6 us
    all_to_all x2, starting transfers between devices, reduce_all(): lax.all_to_all(terms.astype(jnp.bfloat16).reshape((count, rows) + terms.s...  17.6 us
    ppermute x2, waiting for transfers between devices, shifted(): return lax.ppermute(block, axis, route)  17.6 us
    pallas_call x2, Pallas kernels, attention_forward(): pl.pallas_call(kernel, grid=(groups,), in_specs=[pl.BlockSpec((rows, seq_...  17.1 us
    all_to_all x1, starting transfers between devices, gather_all(): moved = lax.all_to_all(spread, axis, 0, 0)  7.92 us
    broadcast_in_dim x2, other arithmetic, body(): return (fwd_out[None], grad_out[None])  5.08 us
    slice x1, local copies, waits for them, and re-layouts, body(): bwd_value_all[:, kv_cols]  4.3 us
  transfers between devices with their start and end apart: 5, of which 3 were waited for; matrix products, arithmetic and copies ran while one was open for 11% of the time, Pallas kernels for 18%

profile of v5, /device:TPU:6, one launch (start us, length us, event | category | flops | bytes accessed | tf_op | source)
XLA Modules:
  0.0 176.0 jit_solution(11747091593418761163)
XLA Ops:
  0.6 0.1 collective-permute-start
  0.7 1.5 fusion.18
  2.2 0.0 copy-start
  2.2 0.0 copy-start.3
  2.3 0.0 copy-start.9
  2.3 3.4 %fusion.34 = bf16[128,512]{1,0:T(8,128)(2,1)S(1)} fusion(bf16[1,4096,512]{2,1,0:T(8,128)(2,1)} %param.13, bf16[1,128,4096]{2,1,0:T(8,128)(2,1)} %param.10, f32[4096]{0:T(1024)} %bitcast.80, f32[128]{0:T(128)S(1)} %get-tuple-element.37), kind=kOutput, calls=%fused_computation.37 | convolution fusion | flops 539033600 | bytes 5390848 | tf_op jit(solution)/shard_map/dot_general | solution.py:171
  5.7 0.0 copy-done
  5.7 0.6 copy-done.3
  6.3 0.0 copy-done.9
  6.3 0.0 copy-start.1
  6.3 0.8 fusion.28
  7.1 8.0 %collective-permute-done = bf16[1,128,4096]{2,1,0:T(8,128)(2,1)S(1)} collective-permute-done((bf16[1,128,4096]{2,1,0:T(8,128)(2,1)}, bf16[1,128,4096]{2,1,0:T(8,128)(2,1)S(1)}, u32[]{:S(2)}, u32[]{:S(2)}) %collective-permute-start) | collective-permute-done | bytes 1048608 | tf_op jit(solution)/shard_map/ppermute | solution.py:19
  15.1 0.3 fusion.15
  15.4 0.0 copy-done.1
  15.4 0.8 fusion.37
  16.3 0.8 fusion.31
  17.1 2.5 %broadcast_in_dim.6 = bf16[8,128,2048]{2,1,0:T(8,128)(2,1)} broadcast(bf16[128,2048]{1,0:T(8,128)(2,1)S(1)} %pad_maximum_fusion.2), dimensions={1,2} | broadcast | bytes 4718592 | tf_op jit(solution)/shard_map/broadcast_in_dim | solution.py:24
  19.6 0.0 copy-start.10
  19.6 0.0 copy-start.11
  19.6 7.9 %all-to-all-start = ((bf16[8,128,2048]{2,1,0:T(8,128)(2,1)}), bf16[8,128,2048]{2,1,0:T(8,128)(2,1)}, u32[]{:S(2)}, u32[]{:S(2)}) async-start(bf16[8,128,2048]{2,1,0:T(8,128)(2,1)} %broadcast_in_dim.6), calls=%async_computation | async-start | bytes 8388608 | tf_op jit(solution)/shard_map/all_to_all | solution.py:25
  27.6 0.0 collective-permute-start.1
  27.6 0.0 copy-done.10
  27.6 0.1 dynamic_slice.7
  27.7 0.0 copy-done.11
  27.7 0.1 dynamic_slice.6
  27.7 1.2 fusion.46
  28.9 0.6 fusion.20
  29.5 1.0 fusion.61
  30.6 9.6 %collective-permute-done.1 = bf16[1,128,4096]{2,1,0:T(8,128)(2,1)} collective-permute-done((bf16[1,128,4096]{2,1,0:T(8,128)(2,1)}, bf16[1,128,4096]{2,1,0:T(8,128)(2,1)}, u32[]{:S(2)}, u32[]{:S(2)}) %collective-permute-start.1) | collective-permute-done | bytes 1048608 | tf_op jit(solution)/shard_map/ppermute | solution.py:19
  40.2 2.3 %fusion.60 = (bf16[128,2048]{1,0:T(8,128)(2,1)}, bf16[128,2048]{1,0:T(8,128)(2,1)}) fusion(bf16[128,4096]{1,0:T(8,128)(2,1)} %bitcast.9), kind=kLoop, calls=%fused_computation.65 | loop fusion | bytes 2097152 | tf_op jit(solution)/shard_map/slice | solution.py:202
  42.5 44.7 %all-to-all-done = bf16[8,128,2048]{2,1,0:T(8,128)(2,1)} async-done(((bf16[8,128,2048]{2,1,0:T(8,128)(2,1)}), bf16[8,128,2048]{2,1,0:T(8,128)(2,1)}, u32[]{:S(2)}, u32[]{:S(2)}) %all-to-all-start) | async-done | bytes 4194336 | tf_op jit(solution)/shard_map/all_to_all | solution.py:25
  87.1 4.3 %fusion.59 = (bf16[1024,256]{1,0:T(8,128)(2,1)}, bf16[1024,256]{1,0:T(8,128)(2,1)}, bf16[1024,256]{1,0:T(8,128)(2,1)}, bf16[1024,256]{1,0:T(8,128)(2,1)}, bf16[1...) fusion(bf16[1024,2048]{1,0:T(8,128)(2,1)} %bitcast.7), kind=kLoop, calls=%fused_computation.64 | loop fusion | bytes 8388608 | tf_op jit(solution)/shard_map/slice | solution.py:201
  91.4 14.8 %shard_map.98 = (f32[128,2048]{1,0:T(8,128)}, f32[1024,256]{1,0:T(8,128)}, f32[1024,256]{1,0:T(8,128)}) custom-call(s32[128,1024]{1,0:T(8,128)} %get-tuple-element.38.mask_ref, bf16[128,2048]{1,0:T(8,128)(2,1)} %get-tuple-element.25.query_ref, bf16[1024,256]{1,0:T(8,128)(2,1)} %get-tuple-element.16.key_ref, bf16[1024,256]{1,0:T(8,128)(2,1)} %get-tuple-element.15.value_ref, ...), custom_call_target="tpu_custom_call" | custom-call | tf_op jit(solution)/shard_map/pallas_call | solution.py:125
  106.2 0.0 copy-start.6
  106.2 1.4 convert.22
  107.6 0.2 copy-done.6
  107.8 0.1 convert.21
  107.8 1.1 pad_maximum_fusion.1
  108.9 10.4 %all-to-all-start.2 = ((bf16[8,128,512]{2,1,0:T(8,128)(2,1)}), bf16[8,128,512]{2,1,0:T(8,128)(2,1)}, u32[]{:S(2)}, u32[]{:S(2)}) async-start(bf16[8,128,512]{2,1,0:T(8,128)(2,1)} %pad_maximum_fusion.1), calls=%async_computation.2 | async-start | bytes 2097152 | tf_op jit(solution)/shard_map/all_to_all | solution.py:32
  119.3 14.8 %shard_map.97 = (f32[128,2048]{1,0:T(8,128)}, f32[1024,256]{1,0:T(8,128)}, f32[1024,256]{1,0:T(8,128)}) custom-call(s32[128,1024]{1,0:T(8,128)} %get-tuple-element.38.mask_ref, bf16[128,2048]{1,0:T(8,128)(2,1)} %get-tuple-element.24.query_ref, bf16[1024,256]{1,0:T(8,128)(2,1)} %get-tuple-element.17.key_ref, bf16[1024,256]{1,0:T(8,128)(2,1)} %get-tuple-element.14.value_ref, ...), custom_call_target="tpu_custom_call" | custom-call | tf_op jit(solution)/shard_map/pallas_call | solution.py:125
  134.1 0.0 copy-start.5
  134.1 1.4 convert.20
  135.5 0.2 copy-done.5
  135.6 0.1 convert.19
  135.7 1.1 pad_maximum_fusion
  136.7 0.0 all-to-all-done.2
  136.7 7.2 %all-to-all-start.1 = ((bf16[8,128,512]{2,1,0:T(8,128)(2,1)}), bf16[8,128,512]{2,1,0:T(8,128)(2,1)}, u32[]{:S(2)}, u32[]{:S(2)}) async-start(bf16[8,128,512]{2,1,0:T(8,128)(2,1)} %pad_maximum_fusion), calls=%async_computation.1 | async-start | bytes 2097152 | tf_op jit(solution)/shard_map/all_to_all | solution.py:32
  144.0 1.4 fusion.62
  145.3 8.5 %shard_map.96 = bf16[128,2048]{1,0:T(8,128)(2,1)} custom-call(s32[128,1024]{1,0:T(8,128)} %get-tuple-element.39.mask_ref, bf16[128,2048]{1,0:T(8,128)(2,1)} %get-tuple-element.42.query_ref, bf16[1024,256]{1,0:T(8,128)(2,1)} %get-tuple-element.19.key_ref, bf16[1024,256]{1,0:T(8,128)(2,1)} %get-tuple-element.18.value_ref, ...), custom_call_target="tpu_custom_call" | custom-call | tf_op jit(solution)/shard_map/pallas_call | solution.py:103
  153.9 0.0 copy-start.4
  153.9 8.6 %shard_map.95 = bf16[128,2048]{1,0:T(8,128)(2,1)} custom-call(s32[128,1024]{1,0:T(8,128)} %get-tuple-element.39.mask_ref, bf16[128,2048]{1,0:T(8,128)(2,1)} %get-tuple-element.43.query_ref, bf16[1024,256]{1,0:T(8,128)(2,1)} %get-tuple-element.21.key_ref, bf16[1024,256]{1,0:T(8,128)(2,1)} %get-tuple-element.20.value_ref, ...), custom_call_target="tpu_custom_call" | custom-call | tf_op jit(solution)/shard_map/pallas_call | solution.py:103
  162.5 0.0 copy-done.4
  162.5 2.2 %maximum_bitcast_fusion = bf16[1,128,4096]{2,1,0:T(8,128)(2,1)} fusion(bf16[128,2048]{1,0:T(8,128)(2,1)S(1)} %copy-done.4, bf16[128,2048]{1,0:T(8,128)(2,1)} %shard_map.95), kind=kLoop, calls=%fused_computation.42 | loop fusion | flops 2097152 | bytes 2097152 | tf_op jit(solution)/shard_map/broadcast_in_dim | solution.py:245
  164.7 0.0 copy-start.8
  164.7 1.5 reduce_sum.54
  166.2 0.0 all-to-all-done.1
  166.2 1.4 reduce_sum.53
  167.6 0.0 copy-done.7
  167.6 0.0 copy-done.8
  167.6 0.0 copy-start.2
  167.6 3.8 %convolution_add_fusion.1 = f32[128,4096]{1,0:T(8,128)S(1)} fusion(bf16[1,4096,512]{2,1,0:T(8,128)(2,1)} %param.12, f32[128,2048]{1,0:T(8,128)S(1)} %copy-done.7, f32[128,2048]{1,0:T(8,128)S(1)} %copy-done.8, bf16[128,256]{1,0:T(8,128)(2,1)S(1)} %get-tuple-element.33, bf16[128,256]{1,0:T(8,128)(2,1)S(1)} %get-tuple-element.31), kind=kOutput, calls=%fused_computation.2 | convolution fusion | flops 538181632 | bytes 8519680 | tf_op jit(solution)/shard_map/dot_general | solution.py:232
  171.5 0.0 copy-done.2
  171.5 1.6 fusion.25
  173.1 2.9 %fusion.42 = bf16[1,128,4096]{2,1,0:T(8,128)(2,1)} fusion(bf16[1,128,4096]{2,1,0:T(8,128)(2,1)S(1)} %copy-done, f32[128,4096]{1,0:T(8,128)S(1)} %get-tuple-element.41, f32[128]{0:T(128)S(1)} %broadcast_multiply_fusion, f32[128]{0:T(128)S(1)} %get-tuple-element.36, f32[128]{0:T(128)S(1)} %get-tuple-element.37, bf16[1,128,4096]{2,1,0:T(8,128)(2,1)} %collective-permute-done.1), kind=kLoop, calls=%fused_computation.41 | loop fusion | flops 4194304 | bytes 5244416 | tf_op jit(solution)/shard_map/broadcast_in_dim | solution.py:245
  (8 shorter events, 0.1 us)
Async XLA Ops:
  0.6 14.5 %collective-permute-start = (bf16[1,128,4096]{2,1,0:T(8,128)(2,1)}, bf16[1,128,4096]{2,1,0:T(8,128)(2,1)S(1)}, u32[]{:S(2)}, u32[]{:S(2)}) collective-permute-start(bf16[1,128,4096]{2,1,0:T(8,128)(2,1)} %param.8), channel_id=1, source_target_pairs={{120,0},{0,8},{8,16},{16,24},{24,32},{32,40},{40,48},{48,56},{56,6... | collective-permute-start | bytes 3145736 | tf_op jit(solution)/shard_map/ppermute | solution.py:19
  2.2 3.5 %copy-start = (bf16[1,128,4096]{2,1,0:T(8,128)(2,1)S(1)}, bf16[1,128,4096]{2,1,0:T(8,128)(2,1)}, u32[]{:S(2)}) copy-start(bf16[1,128,4096]{2,1,0:T(8,128)(2,1)} %param.10) | copy-start | bytes 3145732
  2.2 4.1 %copy-start.3 = (bf16[1,4096,512]{2,1,0:T(8,128)(2,1)S(1)}, bf16[1,4096,512]{2,1,0:T(8,128)(2,1)}, u32[]{:S(2)}) copy-start(bf16[1,4096,512]{2,1,0:T(8,128)(2,1)} %param.12) | copy-start | bytes 12582916
  2.3 4.1 %copy-start.9 = (f32[1,4096]{1,0:T(1,128)S(1)}, f32[1,4096]{1,0:T(1,128)}, u32[]{:S(2)}) copy-start(f32[1,4096]{1,0:T(1,128)} %param.11) | copy-start | bytes 49156
  6.3 9.1 %copy-start.1 = (bf16[1,4096,512]{2,1,0:T(8,128)(2,1)S(1)}, bf16[1,4096,512]{2,1,0:T(8,128)(2,1)}, u32[]{:S(2)}) copy-start(bf16[1,4096,512]{2,1,0:T(8,128)(2,1)} %param.13) | copy-start | bytes 12582916
  19.6 7.9 %copy-start.10 = (s32[1024]{0:T(1024)S(1)}, s32[1024]{0:T(1024)}, u32[]{:S(2)}) copy-start(s32[1024]{0:T(1024)} %param.15) | copy-start | bytes 12292
  19.6 8.0 %copy-start.11 = (s32[1024]{0:T(1024)S(1)}, s32[1024]{0:T(1024)}, u32[]{:S(2)}) copy-start(s32[1024]{0:T(1024)} %param.14) | copy-start | bytes 12292
  19.6 67.5 %all-to-all-start = ((bf16[8,128,2048]{2,1,0:T(8,128)(2,1)}), bf16[8,128,2048]{2,1,0:T(8,128)(2,1)}, u32[]{:S(2)}, u32[]{:S(2)}) async-start(bf16[8,128,2048]{2,1,0:T(8,128)(2,1)} %broadcast_in_dim.6), calls=%async_computation | async-start | bytes 8388608 | tf_op jit(solution)/shard_map/all_to_all | solution.py:25
  27.6 12.6 %collective-permute-start.1 = (bf16[1,128,4096]{2,1,0:T(8,128)(2,1)}, bf16[1,128,4096]{2,1,0:T(8,128)(2,1)}, u32[]{:S(2)}, u32[]{:S(2)}) collective-permute-start(bf16[1,128,4096]{2,1,0:T(8,128)(2,1)} %param.9), channel_id=1, source_target_pairs={{8,0},{16,8},{24,16},{32,24},{40,32},{48,40},{56,48},{64,56},{72,6... | collective-permute-start | bytes 3145736 | tf_op jit(solution)/shard_map/ppermute | solution.py:19
  106.2 1.5 copy-start.6
  108.9 27.8 %all-to-all-start.2 = ((bf16[8,128,512]{2,1,0:T(8,128)(2,1)}), bf16[8,128,512]{2,1,0:T(8,128)(2,1)}, u32[]{:S(2)}, u32[]{:S(2)}) async-start(bf16[8,128,512]{2,1,0:T(8,128)(2,1)} %pad_maximum_fusion.1), calls=%async_computation.2 | async-start | bytes 2097152 | tf_op jit(solution)/shard_map/all_to_all | solution.py:32
  134.1 1.5 copy-start.5
  136.7 29.5 %all-to-all-start.1 = ((bf16[8,128,512]{2,1,0:T(8,128)(2,1)}), bf16[8,128,512]{2,1,0:T(8,128)(2,1)}, u32[]{:S(2)}, u32[]{:S(2)}) async-start(bf16[8,128,512]{2,1,0:T(8,128)(2,1)} %pad_maximum_fusion), calls=%async_computation.1 | async-start | bytes 2097152 | tf_op jit(solution)/shard_map/all_to_all | solution.py:32
  153.9 8.6 %copy-start.4 = (bf16[128,2048]{1,0:T(8,128)(2,1)S(1)}, bf16[128,2048]{1,0:T(8,128)(2,1)}, u32[]{:S(2)}) copy-start(bf16[128,2048]{1,0:T(8,128)(2,1)} %shard_map.96) | copy-start | bytes 1572868
  162.5 5.1 %copy-start.7 = (f32[128,2048]{1,0:T(8,128)S(1)}, f32[128,2048]{1,0:T(8,128)}, u32[]{:S(2)}) copy-start(f32[128,2048]{1,0:T(8,128)} %get-tuple-element.9) | copy-start | bytes 3145732
  164.7 2.9 %copy-start.8 = (f32[128,2048]{1,0:T(8,128)S(1)}, f32[128,2048]{1,0:T(8,128)}, u32[]{:S(2)}) copy-start(f32[128,2048]{1,0:T(8,128)} %get-tuple-element.8) | copy-start | bytes 3145732
  167.6 3.8 %copy-start.2 = (bf16[1,4096,512]{2,1,0:T(8,128)(2,1)S(1)}, bf16[1,4096,512]{2,1,0:T(8,128)(2,1)}, u32[]{:S(2)}) copy-start(bf16[1,4096,512]{2,1,0:T(8,128)(2,1)} %param.13) | copy-start | bytes 12582916

commit v6 on v3

--- a/solution.py
+++ b/solution.py
@@ -190,6 +190,7 @@
     half_kv = kv_width // halves
     half_q = width // halves
     dquery_parts, dkey_parts, dvalue_parts = ([], [], [])
+    half_terms = []
     for half in range(halves):
         kv_cols = slice(half * half_kv, (half + 1) * half_kv)
         q_cols = slice(half * half_q, (half + 1) * half_q)
@@ -201,10 +202,11 @@
             upstream[:, q_cols],
             group_size,
         )
-        if half == 0:
-            fwd_all, dkey_half, dvalue_half = lax.optimization_barrier((fwd_all, dkey_half, dvalue_half))
-        dkv_half = reduce_all(jnp.concatenate([dkey_half, dvalue_half], axis=1), "ctx").astype(jnp.bfloat16)
         dquery_parts.append(dquery_half)
+        half_terms.append(jnp.concatenate([dkey_half, dvalue_half], axis=1))
+    fwd_all, half_terms = lax.optimization_barrier((fwd_all, half_terms))
+    for terms in half_terms:
+        dkv_half = reduce_all(terms, "ctx").astype(jnp.bfloat16)
         dkey_parts.append(dkv_half[:, :half_kv])
         dvalue_parts.append(dkv_half[:, half_kv:])
     dquery = jnp.concatenate(dquery_parts, axis=1)

time: 166 us -> 166 us (level)
    dot_general x2, matrix products: 1.61 us -> 6.52 us  [layer_parts(): jnp.dot(flat, key_weight, preferred_element_type=jnp.float32)]
    dot_general x2, matrix products: 6.53 us -> 1.63 us  [layer_parts(): jnp.dot(flat, value_weight, preferred_element_type=jnp.float32)]
    all_to_all x2, starting transfers between devices: 12.4 us -> 15.5 us  [gather_all(): moved = lax.all_to_all(spread, axis, 0, 0)]
    all_to_all x2, waiting for transfers between devices: 11.9 us -> 15 us  [reduce_all(): lax.all_to_all(terms.astype(jnp.bfloat16).reshape((count, rows) + terms.s...]
    all_to_all x2, waiting for transfers between devices: 34.2 us -> 31.3 us  [gather_all(): moved = lax.all_to_all(spread, axis, 0, 0)]
    another operation x4 -> x0, other arithmetic: 2.75 us -> none
    all_to_all x2, starting transfers between devices: 13.1 us -> 11 us  [reduce_all(): lax.all_to_all(terms.astype(jnp.bfloat16).reshape((count, rows) + terms.s...]
    concatenate x2 -> x1, other arithmetic: 2.13 us -> 3.74 us  [body(): half_terms.append(jnp.concatenate([dkey_half, dvalue_half], axis=1))]
  transfers between devices with their start and end apart: 6 -> 6, of which waited for: 3 -> 2; matrix products, arithmetic and copies ran while one was open for 15% -> 20% of each run, Pallas kernels for 19% -> 28%
where the time goes in v6:
time: 166 us; the launch traced here: 165 us
  Pallas kernels  46.7 us (28%)
  waiting for transfers between devices  46.3 us (28%)
  starting transfers between devices  28 us (17%)
  local copies, waits for them, and re-layouts  15.7 us (9%)
  other arithmetic  14 us (8%)
  matrix products  13.9 us (8%)
    all_to_all x2, waiting for transfers between devices, gather_all(): moved = lax.all_to_all(spread, axis, 0, 0)  31.3 us
    pallas_call x2, Pallas kernels, attention_backward(): pl.pallas_call(kernel, grid=(groups,), in_specs=[pl.BlockSpec((rows, seq_...  29.6 us
    pallas_call x2, Pallas kernels, attention_forward(): pl.pallas_call(kernel, grid=(groups,), in_specs=[pl.BlockSpec((rows, seq_...  17.1 us
    all_to_all x2, starting transfers between devices, gather_all(): moved = lax.all_to_all(spread, axis, 0, 0)  15.5 us
    all_to_all x2, waiting for transfers between devices, reduce_all(): lax.all_to_all(terms.astype(jnp.bfloat16).reshape((count, rows) + terms.s...  15 us
    all_to_all x2, starting transfers between devices, reduce_all(): lax.all_to_all(terms.astype(jnp.bfloat16).reshape((count, rows) + terms.s...  11 us
    dot_general x2, matrix products, layer_parts(): jnp.dot(flat, key_weight, preferred_element_type=jnp.float32)  6.52 us
    broadcast_in_dim x2, other arithmetic, body(): return (fwd_out[None], grad_out[None])  4.98 us
  transfers between devices with their start and end apart: 6, of which 2 were waited for; matrix products, arithmetic and copies ran while one was open for 20% of the time, Pallas kernels for 28%

profile of v6, /device:TPU:6, one launch (start us, length us, event | category | flops | bytes accessed | tf_op | source)
XLA Modules:
  0.0 165.4 jit_solution(6265830209393795494)
XLA Ops:
  0.6 0.1 collective-permute-start
  0.7 1.5 fusion.18
  2.2 0.0 copy-start
  2.2 0.0 copy-start.1
  2.3 0.0 copy-start.6
  2.3 3.4 %fusion.31 = bf16[128,512]{1,0:T(8,128)(2,1)S(1)} fusion(bf16[1,4096,512]{2,1,0:T(8,128)(2,1)} %param.12, bf16[1,128,4096]{2,1,0:T(8,128)(2,1)} %param.10, f32[128]{0:T(128)S(1)} %get-tuple-element.43, f32[4096]{0:T(1024)} %bitcast.76), kind=kOutput, calls=%fused_computation.38 | convolution fusion | flops 539033600 | bytes 5390848 | tf_op jit(solution)/shard_map/dot_general | solution.py:170
  5.7 0.0 copy-done
  5.7 0.6 copy-done.1
  6.3 0.0 copy-done.6
  6.3 0.8 fusion.37
  7.2 1.6 broadcast_in_dim.9
  8.8 0.0 copy-start.8
  8.8 0.0 copy-start.7
  8.8 7.9 %all-to-all-start.1 = ((bf16[8,128,1024]{2,1,0:T(8,128)(2,1)}), bf16[8,128,1024]{2,1,0:T(8,128)(2,1)}, u32[]{:S(2)}, u32[]{:S(2)}) async-start(bf16[8,128,1024]{2,1,0:T(8,128)(2,1)} %broadcast_in_dim.9), calls=%async_computation.1 | async-start | bytes 4194304 | tf_op jit(solution)/shard_map/all_to_all | solution.py:25
  16.7 1.5 collective-permute-start.1
  18.1 0.0 copy-done.8
  18.1 0.1 dynamic_slice.6
  18.2 0.0 copy-done.7
  18.2 0.1 dynamic_slice.7
  18.3 1.2 fusion.46
  19.5 0.0 collective-permute-done
  19.5 0.3 fusion.15
  19.8 0.0 copy-start.2
  19.8 3.1 %fusion.28 = bf16[128,512]{1,0:T(8,128)(2,1)S(1)} fusion(bf16[1,4096,512]{2,1,0:T(8,128)(2,1)} %param.12, bf16[1,128,4096]{2,1,0:T(8,128)(2,1)S(1)} %collective-permute-done, f32[4096]{0:T(1024)S(1)} %bitcast.78, f32[128]{0:T(128)S(1)} %add_rsqrt_fusion.1), kind=kOutput, calls=%fused_computation.37 | convolution fusion | flops 539033600 | bytes 5390848 | tf_op jit(solution)/shard_map/dot_general | solution.py:170
  22.9 0.3 copy-done.2
  23.2 0.8 fusion.34
  24.1 31.3 %all-to-all-done.1 = bf16[8,128,1024]{2,1,0:T(8,128)(2,1)} async-done(((bf16[8,128,1024]{2,1,0:T(8,128)(2,1)}), bf16[8,128,1024]{2,1,0:T(8,128)(2,1)}, u32[]{:S(2)}, u32[]{:S(2)}) %all-to-all-start.1) | async-done | bytes 2097184 | tf_op jit(solution)/shard_map/all_to_all | solution.py:25
  55.4 1.6 broadcast_in_dim.8
  57.0 7.6 %all-to-all-start = ((bf16[8,128,1024]{2,1,0:T(8,128)(2,1)}), bf16[8,128,1024]{2,1,0:T(8,128)(2,1)}, u32[]{:S(2)}, u32[]{:S(2)}) async-start(bf16[8,128,1024]{2,1,0:T(8,128)(2,1)} %broadcast_in_dim.8), calls=%async_computation | async-start | bytes 4194304 | tf_op jit(solution)/shard_map/all_to_all | solution.py:25
  64.6 0.6 fusion.20
  65.2 1.1 fusion.64
  66.3 0.0 collective-permute-done.1
  66.3 2.3 %fusion.63 = (bf16[128,2048]{1,0:T(8,128)(2,1)}, bf16[128,2048]{1,0:T(8,128)(2,1)}) fusion(bf16[128,4096]{1,0:T(8,128)(2,1)} %bitcast.9), kind=kLoop, calls=%fused_computation.69 | loop fusion | bytes 2097152 | tf_op jit(solution)/shard_map/slice | solution.py:202
  68.6 2.9 %fusion.60 = (bf16[1024,256]{1,0:T(8,128)(2,1)}, bf16[1024,256]{1,0:T(8,128)(2,1)}, bf16[1024,256]{1,0:T(8,128)(2,1)}, bf16[1024,256]{1,0:T(8,128)(2,1)}) fusion(bf16[1024,1024]{1,0:T(8,128)(2,1)} %bitcast.8), kind=kLoop, calls=%fused_computation.66 | loop fusion | bytes 4194304 | tf_op jit(solution)/shard_map/slice | solution.py:201
  71.5 14.8 %shard_map.96 = (f32[128,2048]{1,0:T(8,128)}, f32[1024,256]{1,0:T(8,128)}, f32[1024,256]{1,0:T(8,128)}) custom-call(s32[128,1024]{1,0:T(8,128)} %get-tuple-element.44.mask_ref, bf16[128,2048]{1,0:T(8,128)(2,1)} %get-tuple-element.34.query_ref, bf16[1024,256]{1,0:T(8,128)(2,1)} %get-tuple-element.25.key_ref, bf16[1024,256]{1,0:T(8,128)(2,1)} %get-tuple-element.24.value_ref, ...), custom_call_target="tpu_custom_call" | custom-call | tf_op jit(solution)/shard_map/pallas_call | solution.py:125
  86.3 14.8 %shard_map.95 = (f32[128,2048]{1,0:T(8,128)}, f32[1024,256]{1,0:T(8,128)}, f32[1024,256]{1,0:T(8,128)}) custom-call(s32[128,1024]{1,0:T(8,128)} %get-tuple-element.44.mask_ref, bf16[128,2048]{1,0:T(8,128)(2,1)} %get-tuple-element.35.query_ref, bf16[1024,256]{1,0:T(8,128)(2,1)} %get-tuple-element.27.key_ref, bf16[1024,256]{1,0:T(8,128)(2,1)} %get-tuple-element.26.value_ref, ...), custom_call_target="tpu_custom_call" | custom-call | tf_op jit(solution)/shard_map/pallas_call | solution.py:125
  101.1 3.7 %pad_maximum_fusion = (bf16[1024,512]{1,0:T(8,128)(2,1)}, bf16[1024,512]{1,0:T(8,128)(2,1)}) fusion(f32[1024,256]{1,0:T(8,128)} %get-tuple-element.12, f32[1024,256]{1,0:T(8,128)} %get-tuple-element.11, f32[1024,256]{1,0:T(8,128)} %get-tuple-element.14, f32[1024,256]{1,0:T(8,128)} %get-tuple-element.13), kind=kLoop, calls=%fused_computation.34 | loop fusion | flops 4194304 | bytes 6291456 | tf_op jit(solution)/shard_map/concatenate | solution.py:206
  104.8 0.0 all-to-all-done
  104.8 7.2 %all-to-all-start.2 = ((bf16[8,128,512]{2,1,0:T(8,128)(2,1)}), bf16[8,128,512]{2,1,0:T(8,128)(2,1)}, u32[]{:S(2)}, u32[]{:S(2)}) async-start(bf16[8,128,512]{2,1,0:T(8,128)(2,1)} %bitcast.75), calls=%async_computation.2 | async-start | bytes 2097152 | tf_op jit(solution)/shard_map/all_to_all | solution.py:32
  112.0 1.0 fusion.62
  113.1 1.1 fusion.61
  114.1 15.0 %all-to-all-done.2 = bf16[8,128,512]{2,1,0:T(8,128)(2,1)} async-done(((bf16[8,128,512]{2,1,0:T(8,128)(2,1)}), bf16[8,128,512]{2,1,0:T(8,128)(2,1)}, u32[]{:S(2)}, u32[]{:S(2)}) %all-to-all-start.2) | async-done | bytes 1048608 | tf_op jit(solution)/shard_map/all_to_all | solution.py:32
  129.1 3.8 %all-to-all-start.3 = ((bf16[8,128,512]{2,1,0:T(8,128)(2,1)}), bf16[8,128,512]{2,1,0:T(8,128)(2,1)S(1)}, u32[]{:S(2)}, u32[]{:S(2)}) async-start(bf16[8,128,512]{2,1,0:T(8,128)(2,1)} %bitcast.12), calls=%async_computation.3 | async-start | bytes 2097152 | tf_op jit(solution)/shard_map/all_to_all | solution.py:32
  132.9 3.0 %fusion.59 = (bf16[1024,256]{1,0:T(8,128)(2,1)}, bf16[1024,256]{1,0:T(8,128)(2,1)}, bf16[1024,256]{1,0:T(8,128)(2,1)}, bf16[1024,256]{1,0:T(8,128)(2,1)}) fusion(bf16[1024,1024]{1,0:T(8,128)(2,1)} %bitcast.5), kind=kLoop, calls=%fused_computation.65 | loop fusion | bytes 4194304 | tf_op jit(solution)/shard_map/slice | solution.py:228
  135.9 8.5 %shard_map.97 = bf16[128,2048]{1,0:T(8,128)(2,1)} custom-call(s32[128,1024]{1,0:T(8,128)} %get-tuple-element.45.mask_ref, bf16[128,2048]{1,0:T(8,128)(2,1)} %get-tuple-element.30.query_ref, bf16[1024,256]{1,0:T(8,128)(2,1)} %get-tuple-element.23.key_ref, bf16[1024,256]{1,0:T(8,128)(2,1)} %get-tuple-element.20.value_ref, ...), custom_call_target="tpu_custom_call" | custom-call | tf_op jit(solution)/shard_map/pallas_call | solution.py:103
  144.4 0.0 copy-start.4
  144.4 8.6 %shard_map.98 = bf16[128,2048]{1,0:T(8,128)(2,1)} custom-call(s32[128,1024]{1,0:T(8,128)} %get-tuple-element.45.mask_ref, bf16[128,2048]{1,0:T(8,128)(2,1)} %get-tuple-element.31.query_ref, bf16[1024,256]{1,0:T(8,128)(2,1)} %get-tuple-element.22.key_ref, bf16[1024,256]{1,0:T(8,128)(2,1)} %get-tuple-element.21.value_ref, ...), custom_call_target="tpu_custom_call" | custom-call | tf_op jit(solution)/shard_map/pallas_call | solution.py:103
  153.0 0.0 copy-done.4
  153.0 2.1 %maximum_bitcast_fusion = bf16[1,128,4096]{2,1,0:T(8,128)(2,1)} fusion(bf16[128,2048]{1,0:T(8,128)(2,1)} %shard_map.98, bf16[128,2048]{1,0:T(8,128)(2,1)S(1)} %copy-done.4), kind=kLoop, calls=%fused_computation.44 | loop fusion | flops 2097152 | bytes 2097152 | tf_op jit(solution)/shard_map/broadcast_in_dim | solution.py:248
  155.1 0.0 copy-start.5
  155.1 1.5 reduce_sum.53
  156.6 0.0 all-to-all-done.3
  156.6 0.1 reduce_sum.54
  156.8 0.0 copy-done.5
  156.8 0.0 copy-start.3
  156.8 4.1 %convolution_add_fusion.1 = f32[128,4096]{1,0:T(8,128)S(1)} fusion(bf16[1,4096,512]{2,1,0:T(8,128)(2,1)} %param.12, f32[128,2048]{1,0:T(8,128)S(1)} %copy-done.5, f32[128,2048]{1,0:T(8,128)} %get-tuple-element.16, bf16[128,256]{1,0:T(8,128)(2,1)S(1)} %get-tuple-element.39, bf16[128,256]{1,0:T(8,128)(2,1)S(1)} %get-tuple-element.37), kind=kOutput, calls=%fused_computation.2 | convolution fusion | flops 538181632 | bytes 8519680 | tf_op jit(solution)/shard_map/dot_general | solution.py:235
  160.9 0.0 copy-done.3
  160.9 1.6 fusion.25
  162.6 2.9 %fusion.42 = bf16[1,128,4096]{2,1,0:T(8,128)(2,1)} fusion(bf16[1,128,4096]{2,1,0:T(8,128)(2,1)S(1)} %copy-done, f32[128,4096]{1,0:T(8,128)S(1)} %get-tuple-element.47, f32[128]{0:T(128)S(1)} %broadcast_multiply_fusion, f32[128]{0:T(128)S(1)} %get-tuple-element.42, f32[128]{0:T(128)S(1)} %get-tuple-element.43, bf16[1,128,4096]{2,1,0:T(8,128)(2,1)} %collective-permute-done.1), kind=kLoop, calls=%fused_computation.43 | loop fusion | flops 4194304 | bytes 5244416 | tf_op jit(solution)/shard_map/broadcast_in_dim | solution.py:248
  (8 shorter events, 0.1 us)
Async XLA Ops:
  0.6 18.9 %collective-permute-start = (bf16[1,128,4096]{2,1,0:T(8,128)(2,1)}, bf16[1,128,4096]{2,1,0:T(8,128)(2,1)S(1)}, u32[]{:S(2)}, u32[]{:S(2)}) collective-permute-start(bf16[1,128,4096]{2,1,0:T(8,128)(2,1)} %param.8), channel_id=1, source_target_pairs={{120,0},{0,8},{8,16},{16,24},{24,32},{32,40},{40,48},{48,56},{56,6... | collective-permute-start | bytes 3145736 | tf_op jit(solution)/shard_map/ppermute | solution.py:19
  2.2 3.5 %copy-start = (bf16[1,128,4096]{2,1,0:T(8,128)(2,1)S(1)}, bf16[1,128,4096]{2,1,0:T(8,128)(2,1)}, u32[]{:S(2)}) copy-start(bf16[1,128,4096]{2,1,0:T(8,128)(2,1)} %param.10) | copy-start | bytes 3145732
  2.2 4.1 %copy-start.1 = (bf16[1,4096,512]{2,1,0:T(8,128)(2,1)S(1)}, bf16[1,4096,512]{2,1,0:T(8,128)(2,1)}, u32[]{:S(2)}) copy-start(bf16[1,4096,512]{2,1,0:T(8,128)(2,1)} %param.13) | copy-start | bytes 12582916
  2.3 4.1 %copy-start.6 = (f32[1,4096]{1,0:T(1,128)S(1)}, f32[1,4096]{1,0:T(1,128)}, u32[]{:S(2)}) copy-start(f32[1,4096]{1,0:T(1,128)} %param.11) | copy-start | bytes 49156
  8.8 9.4 %copy-start.8 = (s32[1024]{0:T(1024)S(1)}, s32[1024]{0:T(1024)}, u32[]{:S(2)}) copy-start(s32[1024]{0:T(1024)} %param.14) | copy-start | bytes 12292
  8.8 9.4 %copy-start.7 = (s32[1024]{0:T(1024)S(1)}, s32[1024]{0:T(1024)}, u32[]{:S(2)}) copy-start(s32[1024]{0:T(1024)} %param.15) | copy-start | bytes 12292
  8.8 46.6 %all-to-all-start.1 = ((bf16[8,128,1024]{2,1,0:T(8,128)(2,1)}), bf16[8,128,1024]{2,1,0:T(8,128)(2,1)}, u32[]{:S(2)}, u32[]{:S(2)}) async-start(bf16[8,128,1024]{2,1,0:T(8,128)(2,1)} %broadcast_in_dim.9), calls=%async_computation.1 | async-start | bytes 4194304 | tf_op jit(solution)/shard_map/all_to_all | solution.py:25
  16.7 49.6 %collective-permute-start.1 = (bf16[1,128,4096]{2,1,0:T(8,128)(2,1)}, bf16[1,128,4096]{2,1,0:T(8,128)(2,1)}, u32[]{:S(2)}, u32[]{:S(2)}) collective-permute-start(bf16[1,128,4096]{2,1,0:T(8,128)(2,1)} %param.9), channel_id=1, source_target_pairs={{8,0},{16,8},{24,16},{32,24},{40,32},{48,40},{56,48},{64,56},{72,6... | collective-permute-start | bytes 3145736 | tf_op jit(solution)/shard_map/ppermute | solution.py:19
  19.8 3.5 %copy-start.2 = (bf16[1,4096,512]{2,1,0:T(8,128)(2,1)S(1)}, bf16[1,4096,512]{2,1,0:T(8,128)(2,1)}, u32[]{:S(2)}) copy-start(bf16[1,4096,512]{2,1,0:T(8,128)(2,1)} %param.13) | copy-start | bytes 12582916
  57.0 47.8 %all-to-all-start = ((bf16[8,128,1024]{2,1,0:T(8,128)(2,1)}), bf16[8,128,1024]{2,1,0:T(8,128)(2,1)}, u32[]{:S(2)}, u32[]{:S(2)}) async-start(bf16[8,128,1024]{2,1,0:T(8,128)(2,1)} %broadcast_in_dim.8), calls=%async_computation | async-start | bytes 4194304 | tf_op jit(solution)/shard_map/all_to_all | solution.py:25
  104.8 24.3 %all-to-all-start.2 = ((bf16[8,128,512]{2,1,0:T(8,128)(2,1)}), bf16[8,128,512]{2,1,0:T(8,128)(2,1)}, u32[]{:S(2)}, u32[]{:S(2)}) async-start(bf16[8,128,512]{2,1,0:T(8,128)(2,1)} %bitcast.75), calls=%async_computation.2 | async-start | bytes 2097152 | tf_op jit(solution)/shard_map/all_to_all | solution.py:32
  129.1 27.5 %all-to-all-start.3 = ((bf16[8,128,512]{2,1,0:T(8,128)(2,1)}), bf16[8,128,512]{2,1,0:T(8,128)(2,1)S(1)}, u32[]{:S(2)}, u32[]{:S(2)}) async-start(bf16[8,128,512]{2,1,0:T(8,128)(2,1)} %bitcast.12), calls=%async_computation.3 | async-start | bytes 2097152 | tf_op jit(solution)/shard_map/all_to_all | solution.py:32
  144.4 8.6 %copy-start.4 = (bf16[128,2048]{1,0:T(8,128)(2,1)S(1)}, bf16[128,2048]{1,0:T(8,128)(2,1)}, u32[]{:S(2)}) copy-start(bf16[128,2048]{1,0:T(8,128)(2,1)} %shard_map.97) | copy-start | bytes 1572868
  155.1 1.7 %copy-start.5 = (f32[128,2048]{1,0:T(8,128)S(1)}, f32[128,2048]{1,0:T(8,128)}, u32[]{:S(2)}) copy-start(f32[128,2048]{1,0:T(8,128)} %get-tuple-element.17) | copy-start | bytes 3145732
  156.8 4.1 %copy-start.3 = (bf16[1,4096,512]{2,1,0:T(8,128)(2,1)S(1)}, bf16[1,4096,512]{2,1,0:T(8,128)(2,1)}, u32[]{:S(2)}) copy-start(bf16[1,4096,512]{2,1,0:T(8,128)(2,1)} %param.13) | copy-start | bytes 12582916

commit v7 on v6

--- a/solution.py
+++ b/solution.py
@@ -11,6 +11,7 @@
 
 EPSILON = 1e-05
 NEGATIVE = -1e30
+SEGMENT_MAX = 512
 
 
 def shifted(block, axis, distance):
@@ -178,6 +179,13 @@
         key_pos = jnp.arange(segment.shape[0], dtype=jnp.int32)
         return (key_pos[None, :] <= query_pos[:, None]) & (seg_query[:, None] == segment[None, :])
 
+    back_blocks = -(-(SEGMENT_MAX - 1) // tok_rows)
+    window = min(back_blocks + 1, count) * tok_rows
+    window_start = jnp.minimum(jnp.maximum(rank - back_blocks, 0) * tok_rows, count * tok_rows - window)
+
+    def windowed(array):
+        return lax.dynamic_slice_in_dim(array, window_start, window, axis=0)
+
     bwd_query, bwd_keys, bwd_values, bwd_wide, bwd_inverse = layer_parts(saved_bwd[0])
     bwd_all = gather_all(jnp.concatenate([bwd_keys, bwd_values], axis=1), "ctx")
     fwd_query, fwd_keys, fwd_values, fwd_wide, fwd_inverse = layer_parts(arrived)
@@ -185,7 +193,9 @@
 
     bwd_key_all = bwd_all[:, :kv_width]
     bwd_value_all = bwd_all[:, kv_width:]
-    allowed = allowed_of(seg_bwd).astype(jnp.int32)
+    allowed = lax.dynamic_slice_in_dim(allowed_of(seg_bwd).astype(jnp.int32), window_start, window, axis=1)
+    bwd_key_all = windowed(bwd_key_all)
+    bwd_value_all = windowed(bwd_value_all)
     halves = 2
     half_kv = kv_width // halves
     half_q = width // halves
@@ -203,7 +213,12 @@
             group_size,
         )
         dquery_parts.append(dquery_half)
-        half_terms.append(jnp.concatenate([dkey_half, dvalue_half], axis=1))
+        terms = jnp.concatenate([dkey_half, dvalue_half], axis=1)
+        half_terms.append(
+            lax.dynamic_update_slice_in_dim(
+                jnp.zeros((count * tok_rows, terms.shape[1]), terms.dtype), terms, window_start, axis=0
+            )
+        )
     fwd_all, half_terms = lax.optimization_barrier((fwd_all, half_terms))
     for terms in half_terms:
         dkv_half = reduce_all(terms, "ctx").astype(jnp.bfloat16)
@@ -213,9 +228,9 @@
     dkeys = jnp.concatenate(dkey_parts, axis=1)
     dvalues = jnp.concatenate(dvalue_parts, axis=1)
 
-    key_piece = fwd_all[:, :kv_width]
-    value_piece = fwd_all[:, kv_width:]
-    allowed = allowed_of(seg_fwd).astype(jnp.int32)
+    key_piece = windowed(fwd_all[:, :kv_width])
+    value_piece = windowed(fwd_all[:, kv_width:])
+    allowed = lax.dynamic_slice_in_dim(allowed_of(seg_fwd).astype(jnp.int32), window_start, window, axis=1)
     fwd_parts = []
     for half in range(halves):
         kv_cols = slice(half * half_kv, (half + 1) * half_kv)

time: 166 us -> 174 us (1.048)
  local copies, waits for them, and re-layouts: 15.7 us -> 28.5 us
  Pallas kernels: 46.7 us -> 40.6 us
    dynamic_update_slice x0 -> x2, local copies, waits for them, and re-layouts: none -> 9.38 us  [body(): lax.dynamic_update_slice_in_dim(jnp.zeros((count * tok_rows, terms.shape[...]
    pallas_call x2, Pallas kernels: 29.6 us -> 25.5 us  [attention_backward(): pl.pallas_call(kernel, grid=(groups,), in_specs=[pl.BlockSpec((rows, seq_...]
    slice x1 -> x4, local copies, waits for them, and re-layouts: 2.96 us -> 5.97 us  [the longest x1 1.68 us: body(): value_piece = windowed(fwd_all[:, kv_width:])]
    another operation x0 -> x2, local copies, waits for them, and re-layouts: none -> 2.16 us
    pallas_call x2, Pallas kernels: 17.1 us -> 15.1 us  [attention_forward(): pl.pallas_call(kernel, grid=(groups,), in_specs=[pl.BlockSpec((rows, seq_...]
    slice x1, local copies, waits for them, and re-layouts: 2.89 us -> 1.06 us  [body(): bwd_value_all[:, kv_cols]]
    concatenate x1 -> x2, other arithmetic: 3.74 us -> 4.49 us  [body(): terms = jnp.concatenate([dkey_half, dvalue_half], axis=1)]
  transfers between devices with their start and end apart: 6 -> 6, of which waited for: 2 -> 2; matrix products, arithmetic and copies ran while one was open for 20% -> 27% of each run, Pallas kernels for 28% -> 23%
where the time goes in v7:
time: 174 us; the launch traced here: 173 us
  waiting for transfers between devices  46.2 us (27%)
  Pallas kernels  40.6 us (23%)
  local copies, waits for them, and re-layouts  28.5 us (16%)
  starting transfers between devices  28 us (16%)
  other arithmetic  14.7 us (8%)
  matrix products  13.9 us (8%)
    all_to_all x2, waiting for transfers between devices, gather_all(): moved = lax.all_to_all(spread, axis, 0, 0)  31.1 us
    pallas_call x2, Pallas kernels, attention_backward(): pl.pallas_call(kernel, grid=(groups,), in_specs=[pl.BlockSpec((rows, seq_...  25.5 us
    all_to_all x2, starting transfers between devices, gather_all(): moved = lax.all_to_all(spread, axis, 0, 0)  15.5 us
    pallas_call x2, Pallas kernels, attention_forward(): pl.pallas_call(kernel, grid=(groups,), in_specs=[pl.BlockSpec((rows, seq_...  15.1 us
    all_to_all x2, waiting for transfers between devices, reduce_all(): lax.all_to_all(terms.astype(jnp.bfloat16).reshape((count, rows) + terms.s...  15 us
    all_to_all x2, starting transfers between devices, reduce_all(): lax.all_to_all(terms.astype(jnp.bfloat16).reshape((count, rows) + terms.s...  11 us
    dynamic_update_slice x2, local copies, waits for them, and re-layouts, body(): lax.dynamic_update_slice_in_dim(jnp.zeros((count * tok_rows, terms.shape[...  9.38 us
    dot_general x2, matrix products, layer_parts(): jnp.dot(flat, key_weight, preferred_element_type=jnp.float32)  6.52 us
  transfers between devices with their start and end apart: 6, of which 2 were waited for; matrix products, arithmetic and copies ran while one was open for 27% of the time, Pallas kernels for 23%

profile of v7, /device:TPU:6, one launch (start us, length us, event | category | flops | bytes accessed | tf_op | source)
XLA Modules:
  0.0 172.8 jit_solution(16185075679671274109)
XLA Ops:
  0.6 0.1 collective-permute-start
  0.7 1.5 fusion.18
  2.2 0.0 copy-start.1
  2.3 0.0 copy-start.6
  2.3 3.4 %fusion.31 = bf16[128,512]{1,0:T(8,128)(2,1)S(1)} fusion(bf16[1,4096,512]{2,1,0:T(8,128)(2,1)} %param.12, bf16[1,128,4096]{2,1,0:T(8,128)(2,1)} %param.10, f32[128]{0:T(128)S(1)} %get-tuple-element.49, f32[4096]{0:T(1024)} %bitcast.76), kind=kOutput, calls=%fused_computation.38 | convolution fusion | flops 539033600 | bytes 5390848 | tf_op jit(solution)/shard_map/dot_general | solution.py:171
  5.7 0.0 copy-done
  5.7 0.6 copy-done.1
  6.3 0.0 copy-done.6
  6.3 0.8 fusion.37
  7.2 1.6 broadcast_in_dim.9
  8.8 7.9 %all-to-all-start.1 = ((bf16[8,128,1024]{2,1,0:T(8,128)(2,1)}), bf16[8,128,1024]{2,1,0:T(8,128)(2,1)}, u32[]{:S(2)}, u32[]{:S(2)}) async-start(bf16[8,128,1024]{2,1,0:T(8,128)(2,1)} %broadcast_in_dim.9), calls=%async_computation.1 | async-start | bytes 4194304 | tf_op jit(solution)/shard_map/all_to_all | solution.py:26
  16.7 1.5 collective-permute-start.1
  18.2 0.0 copy-done.7
  18.2 0.1 dynamic-slice
  18.2 0.0 copy-done.8
  18.2 0.1 dynamic-slice.1
  18.3 0.1 dynamic_slice.24
  18.4 0.1 dynamic_slice.26
  18.5 0.1 iota_compare_fusion
  18.6 1.0 and_convert_fusion
  19.7 0.0 collective-permute-done
  19.7 0.3 fusion.15
  20.0 0.0 copy-start.2
  20.0 3.1 %fusion.28 = bf16[128,512]{1,0:T(8,128)(2,1)S(1)} fusion(bf16[1,4096,512]{2,1,0:T(8,128)(2,1)} %param.12, bf16[1,128,4096]{2,1,0:T(8,128)(2,1)S(1)} %collective-permute-done, f32[4096]{0:T(1024)S(1)} %bitcast.78, f32[128]{0:T(128)S(1)} %add_rsqrt_fusion.1), kind=kOutput, calls=%fused_computation.37 | convolution fusion | flops 539033600 | bytes 5390848 | tf_op jit(solution)/shard_map/dot_general | solution.py:171
  23.1 0.3 copy-done.2
  23.4 0.8 fusion.34
  24.3 31.1 %all-to-all-done.1 = bf16[8,128,1024]{2,1,0:T(8,128)(2,1)} async-done(((bf16[8,128,1024]{2,1,0:T(8,128)(2,1)}), bf16[8,128,1024]{2,1,0:T(8,128)(2,1)}, u32[]{:S(2)}, u32[]{:S(2)}) %all-to-all-start.1) | async-done | bytes 2097184 | tf_op jit(solution)/shard_map/all_to_all | solution.py:26
  55.4 1.6 broadcast_in_dim.8
  57.0 7.6 %all-to-all-start = ((bf16[8,128,1024]{2,1,0:T(8,128)(2,1)}), bf16[8,128,1024]{2,1,0:T(8,128)(2,1)}, u32[]{:S(2)}, u32[]{:S(2)}) async-start(bf16[8,128,1024]{2,1,0:T(8,128)(2,1)} %broadcast_in_dim.8), calls=%async_computation | async-start | bytes 4194304 | tf_op jit(solution)/shard_map/all_to_all | solution.py:26
  64.6 0.6 fusion.20
  65.2 1.1 fusion.62
  66.3 0.0 collective-permute-done.1
  66.3 2.3 %fusion.59 = (bf16[128,2048]{1,0:T(8,128)(2,1)}, bf16[128,2048]{1,0:T(8,128)(2,1)}) fusion(bf16[128,4096]{1,0:T(8,128)(2,1)} %bitcast.9), kind=kLoop, calls=%fused_computation.71 | loop fusion | bytes 2097152 | tf_op jit(solution)/shard_map/slice | solution.py:212
  68.6 1.7 fusion.56
  70.3 1.1 fusion.60
  71.3 1.1 fusion.61
  72.4 12.7 %shard_map.96 = (f32[128,2048]{1,0:T(8,128)}, f32[640,256]{1,0:T(8,128)}, f32[640,256]{1,0:T(8,128)}) custom-call(s32[128,640]{1,0:T(8,128)} %get-tuple-element.44.mask_ref, bf16[128,2048]{1,0:T(8,128)(2,1)} %get-tuple-element.38.query_ref, bf16[640,256]{1,0:T(8,128)(2,1)} %get-tuple-element.36.key_ref, bf16[640,256]{1,0:T(8,128)(2,1)} %get-tuple-element.34.value_ref, ...), custom_call_target="tpu_custom_call" | custom-call | tf_op jit(solution)/shard_map/pallas_call | solution.py:126
  85.2 2.2 %pad_maximum_fusion.1 = bf16[640,512]{1,0:T(8,128)(2,1)} fusion(f32[640,256]{1,0:T(8,128)} %get-tuple-element.14, f32[640,256]{1,0:T(8,128)} %get-tuple-element.13), kind=kLoop, calls=%fused_computation.36 | loop fusion | flops 1310720 | bytes 1966080 | tf_op jit(solution)/shard_map/concatenate | solution.py:216
  87.4 1.1 broadcast.83.clone.1
  88.5 4.7 %dynamic_update_slice.7 = bf16[1024,512]{1,0:T(8,128)(2,1)} dynamic-update-slice(bf16[1024,512]{1,0:T(8,128)(2,1)} %broadcast.83.clone.1, bf16[640,512]{1,0:T(8,128)(2,1)} %pad_maximum_fusion.1, s32[]{:T(128)S(6)} %select_n.5, s32[]{:T(128)} %constant.8.clone.1) | dynamic-update-slice | bytes 1310724 | tf_op jit(solution)/shard_map/dynamic_update_slice | solution.py:218
  93.2 12.8 %shard_map.95 = (f32[128,2048]{1,0:T(8,128)}, f32[640,256]{1,0:T(8,128)}, f32[640,256]{1,0:T(8,128)}) custom-call(s32[128,640]{1,0:T(8,128)} %get-tuple-element.44.mask_ref, bf16[128,2048]{1,0:T(8,128)(2,1)} %get-tuple-element.39.query_ref, bf16[640,256]{1,0:T(8,128)(2,1)} %get-tuple-element.37.key_ref, bf16[640,256]{1,0:T(8,128)(2,1)} %get-tuple-element.35.value_ref, ...), custom_call_target="tpu_custom_call" | custom-call | tf_op jit(solution)/shard_map/pallas_call | solution.py:126
  106.0 2.3 %pad_maximum_fusion = bf16[640,512]{1,0:T(8,128)(2,1)} fusion(f32[640,256]{1,0:T(8,128)} %get-tuple-element.12, f32[640,256]{1,0:T(8,128)} %get-tuple-element.11), kind=kLoop, calls=%fused_computation.35 | loop fusion | flops 1310720 | bytes 1966080 | tf_op jit(solution)/shard_map/concatenate | solution.py:216
  108.3 1.0 broadcast.83.clone
  109.3 4.7 %dynamic_update_slice.6 = bf16[1024,512]{1,0:T(8,128)(2,1)} dynamic-update-slice(bf16[1024,512]{1,0:T(8,128)(2,1)} %broadcast.83.clone, bf16[640,512]{1,0:T(8,128)(2,1)} %pad_maximum_fusion, s32[]{:T(128)S(6)} %select_n.5, s32[]{:T(128)} %constant.8.clone.1) | dynamic-update-slice | bytes 1310724 | tf_op jit(solution)/shard_map/dynamic_update_slice | solution.py:218
  114.0 0.0 all-to-all-done
  114.0 7.2 %all-to-all-start.2 = ((bf16[8,128,512]{2,1,0:T(8,128)(2,1)}), bf16[8,128,512]{2,1,0:T(8,128)(2,1)}, u32[]{:S(2)}, u32[]{:S(2)}) async-start(bf16[8,128,512]{2,1,0:T(8,128)(2,1)} %bitcast.75), calls=%async_computation.2 | async-start | bytes 2097152 | tf_op jit(solution)/shard_map/all_to_all | solution.py:33
  121.2 1.0 fusion.58
  122.2 1.1 fusion.57
  123.2 15.0 %all-to-all-done.2 = bf16[8,128,512]{2,1,0:T(8,128)(2,1)} async-done(((bf16[8,128,512]{2,1,0:T(8,128)(2,1)}), bf16[8,128,512]{2,1,0:T(8,128)(2,1)}, u32[]{:S(2)}, u32[]{:S(2)}) %all-to-all-start.2) | async-done | bytes 1048608 | tf_op jit(solution)/shard_map/all_to_all | solution.py:33
  138.3 3.8 %all-to-all-start.3 = ((bf16[8,128,512]{2,1,0:T(8,128)(2,1)}), bf16[8,128,512]{2,1,0:T(8,128)(2,1)S(1)}, u32[]{:S(2)}, u32[]{:S(2)}) async-start(bf16[8,128,512]{2,1,0:T(8,128)(2,1)} %bitcast.12), calls=%async_computation.3 | async-start | bytes 2097152 | tf_op jit(solution)/shard_map/all_to_all | solution.py:33
  142.1 1.7 fusion.55
  143.8 1.5 constant_dynamic-slice_fusion.2
  145.3 7.5 %shard_map.97 = bf16[128,2048]{1,0:T(8,128)(2,1)} custom-call(s32[128,640]{1,0:T(8,128)} %get-tuple-element.45.mask_ref, bf16[128,2048]{1,0:T(8,128)(2,1)} %get-tuple-element.30.query_ref, bf16[640,256]{1,0:T(8,128)(2,1)} %get-tuple-element.28.key_ref, bf16[640,256]{1,0:T(8,128)(2,1)} %get-tuple-element.53.value_ref, ...), custom_call_target="tpu_custom_call" | custom-call | tf_op jit(solution)/shard_map/pallas_call | solution.py:104
  152.8 7.6 %shard_map.98 = bf16[128,2048]{1,0:T(8,128)(2,1)} custom-call(s32[128,640]{1,0:T(8,128)} %get-tuple-element.45.mask_ref, bf16[128,2048]{1,0:T(8,128)(2,1)} %get-tuple-element.31.query_ref, bf16[640,256]{1,0:T(8,128)(2,1)} %get-tuple-element.29.key_ref, bf16[640,256]{1,0:T(8,128)(2,1)} %get-tuple-element.52.value_ref, ...), custom_call_target="tpu_custom_call" | custom-call | tf_op jit(solution)/shard_map/pallas_call | solution.py:104
  160.4 0.0 copy-done.4
  160.4 2.1 %maximum_bitcast_fusion = bf16[1,128,4096]{2,1,0:T(8,128)(2,1)} fusion(bf16[128,2048]{1,0:T(8,128)(2,1)} %shard_map.98, bf16[128,2048]{1,0:T(8,128)(2,1)S(1)} %copy-done.4), kind=kLoop, calls=%fused_computation.44 | loop fusion | flops 2097152 | bytes 2097152 | tf_op jit(solution)/shard_map/broadcast_in_dim | solution.py:263
  162.5 1.5 reduce_sum.53
  164.0 0.0 all-to-all-done.3
  164.0 0.1 reduce_sum.54
  164.1 0.0 copy-done.5
  164.1 0.0 copy-start.3
  164.2 4.1 %convolution_add_fusion.1 = f32[128,4096]{1,0:T(8,128)S(1)} fusion(bf16[1,4096,512]{2,1,0:T(8,128)(2,1)} %param.12, f32[128,2048]{1,0:T(8,128)S(1)} %copy-done.5, f32[128,2048]{1,0:T(8,128)} %get-tuple-element.16, bf16[128,256]{1,0:T(8,128)(2,1)S(1)} %get-tuple-element.43, bf16[128,256]{1,0:T(8,128)(2,1)S(1)} %get-tuple-element.41), kind=kOutput, calls=%fused_computation.2 | convolution fusion | flops 538181632 | bytes 8519680 | tf_op jit(solution)/shard_map/dot_general | solution.py:250
  168.3 1.6 fusion.25
  169.9 2.9 %fusion.42 = bf16[1,128,4096]{2,1,0:T(8,128)(2,1)} fusion(bf16[1,128,4096]{2,1,0:T(8,128)(2,1)S(1)} %copy-done, f32[128,4096]{1,0:T(8,128)S(1)} %get-tuple-element.51, f32[128]{0:T(128)S(1)} %broadcast_multiply_fusion, f32[128]{0:T(128)S(1)} %get-tuple-element.48, f32[128]{0:T(128)S(1)} %get-tuple-element.49, bf16[1,128,4096]{2,1,0:T(8,128)(2,1)} %collective-permute-done.1), kind=kLoop, calls=%fused_computation.43 | loop fusion | flops 4194304 | bytes 5244416 | tf_op jit(solution)/shard_map/broadcast_in_dim | solution.py:263
  (14 shorter events, 0.1 us)
Async XLA Ops:
  0.6 19.0 %collective-permute-start = (bf16[1,128,4096]{2,1,0:T(8,128)(2,1)}, bf16[1,128,4096]{2,1,0:T(8,128)(2,1)S(1)}, u32[]{:S(2)}, u32[]{:S(2)}) collective-permute-start(bf16[1,128,4096]{2,1,0:T(8,128)(2,1)} %param.8), channel_id=1, source_target_pairs={{120,0},{0,8},{8,16},{16,24},{24,32},{32,40},{40,48},{48,56},{56,6... | collective-permute-start | bytes 3145736 | tf_op jit(solution)/shard_map/ppermute | solution.py:20
  2.2 3.5 %copy-start = (bf16[1,128,4096]{2,1,0:T(8,128)(2,1)S(1)}, bf16[1,128,4096]{2,1,0:T(8,128)(2,1)}, u32[]{:S(2)}) copy-start(bf16[1,128,4096]{2,1,0:T(8,128)(2,1)} %param.10) | copy-start | bytes 3145732
  2.2 4.1 %copy-start.1 = (bf16[1,4096,512]{2,1,0:T(8,128)(2,1)S(1)}, bf16[1,4096,512]{2,1,0:T(8,128)(2,1)}, u32[]{:S(2)}) copy-start(bf16[1,4096,512]{2,1,0:T(8,128)(2,1)} %param.13) | copy-start | bytes 12582916
  2.3 4.1 %copy-start.6 = (f32[1,4096]{1,0:T(1,128)S(1)}, f32[1,4096]{1,0:T(1,128)}, u32[]{:S(2)}) copy-start(f32[1,4096]{1,0:T(1,128)} %param.11) | copy-start | bytes 49156
  8.8 9.4 %copy-start.7 = (s32[1024]{0:T(1024)S(1)}, s32[1024]{0:T(1024)}, u32[]{:S(2)}) copy-start(s32[1024]{0:T(1024)} %param.14) | copy-start | bytes 12292
  8.8 9.4 %copy-start.8 = (s32[1024]{0:T(1024)S(1)}, s32[1024]{0:T(1024)}, u32[]{:S(2)}) copy-start(s32[1024]{0:T(1024)} %param.15) | copy-start | bytes 12292
  8.8 46.6 %all-to-all-start.1 = ((bf16[8,128,1024]{2,1,0:T(8,128)(2,1)}), bf16[8,128,1024]{2,1,0:T(8,128)(2,1)}, u32[]{:S(2)}, u32[]{:S(2)}) async-start(bf16[8,128,1024]{2,1,0:T(8,128)(2,1)} %broadcast_in_dim.9), calls=%async_computation.1 | async-start | bytes 4194304 | tf_op jit(solution)/shard_map/all_to_all | solution.py:26
  16.7 49.6 %collective-permute-start.1 = (bf16[1,128,4096]{2,1,0:T(8,128)(2,1)}, bf16[1,128,4096]{2,1,0:T(8,128)(2,1)}, u32[]{:S(2)}, u32[]{:S(2)}) collective-permute-start(bf16[1,128,4096]{2,1,0:T(8,128)(2,1)} %param.9), channel_id=1, source_target_pairs={{8,0},{16,8},{24,16},{32,24},{40,32},{48,40},{56,48},{64,56},{72,6... | collective-permute-start | bytes 3145736 | tf_op jit(solution)/shard_map/ppermute | solution.py:20
  20.0 3.5 %copy-start.2 = (bf16[1,4096,512]{2,1,0:T(8,128)(2,1)S(1)}, bf16[1,4096,512]{2,1,0:T(8,128)(2,1)}, u32[]{:S(2)}) copy-start(bf16[1,4096,512]{2,1,0:T(8,128)(2,1)} %param.13) | copy-start | bytes 12582916
  57.0 57.0 %all-to-all-start = ((bf16[8,128,1024]{2,1,0:T(8,128)(2,1)}), bf16[8,128,1024]{2,1,0:T(8,128)(2,1)}, u32[]{:S(2)}, u32[]{:S(2)}) async-start(bf16[8,128,1024]{2,1,0:T(8,128)(2,1)} %broadcast_in_dim.8), calls=%async_computation | async-start | bytes 4194304 | tf_op jit(solution)/shard_map/all_to_all | solution.py:26
  114.0 24.3 %all-to-all-start.2 = ((bf16[8,128,512]{2,1,0:T(8,128)(2,1)}), bf16[8,128,512]{2,1,0:T(8,128)(2,1)}, u32[]{:S(2)}, u32[]{:S(2)}) async-start(bf16[8,128,512]{2,1,0:T(8,128)(2,1)} %bitcast.75), calls=%async_computation.2 | async-start | bytes 2097152 | tf_op jit(solution)/shard_map/all_to_all | solution.py:33
  138.3 25.7 %all-to-all-start.3 = ((bf16[8,128,512]{2,1,0:T(8,128)(2,1)}), bf16[8,128,512]{2,1,0:T(8,128)(2,1)S(1)}, u32[]{:S(2)}, u32[]{:S(2)}) async-start(bf16[8,128,512]{2,1,0:T(8,128)(2,1)} %bitcast.12), calls=%async_computation.3 | async-start | bytes 2097152 | tf_op jit(solution)/shard_map/all_to_all | solution.py:33
  152.8 7.6 %copy-start.4 = (bf16[128,2048]{1,0:T(8,128)(2,1)S(1)}, bf16[128,2048]{1,0:T(8,128)(2,1)}, u32[]{:S(2)}) copy-start(bf16[128,2048]{1,0:T(8,128)(2,1)} %shard_map.97) | copy-start | bytes 1572868
  162.5 1.7 copy-start.5
  164.1 4.1 %copy-start.3 = (bf16[1,4096,512]{2,1,0:T(8,128)(2,1)S(1)}, bf16[1,4096,512]{2,1,0:T(8,128)(2,1)}, u32[]{:S(2)}) copy-start(bf16[1,4096,512]{2,1,0:T(8,128)(2,1)} %param.13) | copy-start | bytes 12582916

commit v8 on v6

--- a/solution.py
+++ b/solution.py
@@ -5,12 +5,14 @@
 from jax import lax
 from jax.sharding import PartitionSpec as P
 from jax.experimental import pallas as pl
+from jax.experimental.pallas import tpu as pltpu
 
 HD = 128
 
 
 EPSILON = 1e-05
 NEGATIVE = -1e30
+SEGMENT_MAX = 512
 
 
 def shifted(block, axis, distance):
@@ -42,10 +44,12 @@
 INTERPRET = False
 
 
-def forward_kernel(mask_ref, query_ref, key_ref, value_ref, input_ref, out_ref, *, heads, scale):
+def forward_kernel(start_ref, mask_ref, query_ref, key_ref, value_ref, input_ref, out_ref, *, heads, scale):
     allowed = mask_ref[...] != 0
-    keys = key_ref[...]
-    values = value_ref[...]
+    window = mask_ref.shape[1]
+    start = pl.multiple_of(start_ref[0], HD)
+    keys = key_ref[pl.ds(start, window), :]
+    values = value_ref[pl.ds(start, window), :]
     for head in range(heads):
         cols = slice(head * HD, (head + 1) * HD)
         scores = lax.dot_general(
@@ -59,12 +63,14 @@
         out_ref[:, cols] = (input_ref[:, cols].astype(jnp.float32) + product / total).astype(out_ref.dtype)
 
 
-def backward_kernel(mask_ref, query_ref, key_ref, value_ref, grad_ref, dquery_ref, dkey_ref, dvalue_ref, *, heads, scale):
+def backward_kernel(start_ref, mask_ref, query_ref, key_ref, value_ref, grad_ref, dquery_ref, dkey_ref, dvalue_ref, *, heads, scale):
     allowed = mask_ref[...] != 0
-    keys = key_ref[...]
-    values = value_ref[...]
-    dkey_acc = jnp.zeros(dkey_ref.shape, jnp.float32)
-    dvalue_acc = jnp.zeros(dvalue_ref.shape, jnp.float32)
+    window = mask_ref.shape[1]
+    start = pl.multiple_of(start_ref[0], HD)
+    keys = key_ref[pl.ds(start, window), :]
+    values = value_ref[pl.ds(start, window), :]
+    dkey_acc = jnp.zeros((window, HD), jnp.float32)
+    dvalue_acc = jnp.zeros((window, HD), jnp.float32)
     for head in range(heads):
         cols = slice(head * HD, (head + 1) * HD)
         query = query_ref[:, cols]
@@ -90,13 +96,16 @@
         dvalue_acc = dvalue_acc + lax.dot_general(
             probs_b, grad, (((0,), (0,)), ((), ())), preferred_element_type=jnp.float32
         )
-    dkey_ref[...] = dkey_acc * scale
-    dvalue_ref[...] = dvalue_acc
-
-
-def attention_forward(mask, query, keys, values, inputs, group_size):
+    dkey_ref[...] = jnp.zeros(dkey_ref.shape, dkey_ref.dtype)
+    dvalue_ref[...] = jnp.zeros(dvalue_ref.shape, dvalue_ref.dtype)
+    dkey_ref[pl.ds(start, window), :] = dkey_acc * scale
+    dvalue_ref[pl.ds(start, window), :] = dvalue_acc
+
+
+def attention_forward(start, mask, query, keys, values, inputs, group_size):
     rows, width = query.shape
     seq_len, kv_width = keys.shape
+    window = mask.shape[1]
     groups = kv_width // HD
     cols = group_size * HD
     kernel = functools.partial(forward_kernel, heads=group_size, scale=HD ** (-0.5))
@@ -104,7 +113,8 @@
         kernel,
         grid=(groups,),
         in_specs=[
-            pl.BlockSpec((rows, seq_len), lambda g: (0, 0)),
+            pl.BlockSpec(memory_space=pltpu.SMEM),
+            pl.BlockSpec((rows, window), lambda g: (0, 0)),
             pl.BlockSpec((rows, cols), lambda g: (0, g)),
             pl.BlockSpec((seq_len, HD), lambda g: (0, g)),
             pl.BlockSpec((seq_len, HD), lambda g: (0, g)),
@@ -113,12 +123,13 @@
         out_specs=pl.BlockSpec((rows, cols), lambda g: (0, g)),
         out_shape=jax.ShapeDtypeStruct((rows, width), jnp.bfloat16),
         interpret=INTERPRET,
-    )(mask, query, keys, values, inputs)
-
-
-def attention_backward(mask, query, keys, values, grad, group_size):
+    )(start, mask, query, keys, values, inputs)
+
+
+def attention_backward(start, mask, query, keys, values, grad, group_size):
     rows, width = query.shape
     seq_len, kv_width = keys.shape
+    window = mask.shape[1]
     groups = kv_width // HD
     cols = group_size * HD
     kernel = functools.partial(backward_kernel, heads=group_size, scale=HD ** (-0.5))
@@ -126,7 +137,8 @@
         kernel,
         grid=(groups,),
         in_specs=[
-            pl.BlockSpec((rows, seq_len), lambda g: (0, 0)),
+            pl.BlockSpec(memory_space=pltpu.SMEM),
+            pl.BlockSpec((rows, window), lambda g: (0, 0)),
             pl.BlockSpec((rows, cols), lambda g: (0, g)),
             pl.BlockSpec((seq_len, HD), lambda g: (0, g)),
             pl.BlockSpec((seq_len, HD), lambda g: (0, g)),
@@ -143,7 +155,7 @@
             jax.ShapeDtypeStruct((seq_len, kv_width), jnp.float32),
         ],
         interpret=INTERPRET,
-    )(mask, query, keys, values, grad)
+    )(start, mask, query, keys, values, grad)
 
 
 def body(sent_fwd, sent_grad, saved_bwd, norm_gain, key_proj, value_proj, seg_fwd, seg_bwd):
@@ -178,6 +190,10 @@
         key_pos = jnp.arange(segment.shape[0], dtype=jnp.int32)
         return (key_pos[None, :] <= query_pos[:, None]) & (seg_query[:, None] == segment[None, :])
 
+    back_blocks = -(-(SEGMENT_MAX - 1) // tok_rows)
+    window = min(back_blocks + 1, count) * tok_rows
+    window_start = jnp.minimum(jnp.maximum(rank - back_blocks, 0) * tok_rows, count * tok_rows - window)
+
     bwd_query, bwd_keys, bwd_values, bwd_wide, bwd_inverse = layer_parts(saved_bwd[0])
     bwd_all = gather_all(jnp.concatenate([bwd_keys, bwd_values], axis=1), "ctx")
     fwd_query, fwd_keys, fwd_values, fwd_wide, fwd_inverse = layer_parts(arrived)
@@ -185,7 +201,8 @@
 
     bwd_key_all = bwd_all[:, :kv_width]
     bwd_value_all = bwd_all[:, kv_width:]
-    allowed = allowed_of(seg_bwd).astype(jnp.int32)
+    allowed = lax.dynamic_slice_in_dim(allowed_of(seg_bwd).astype(jnp.int32), window_start, window, axis=1)
+    start_row = window_start.reshape(1).astype(jnp.int32)
     halves = 2
     half_kv = kv_width // halves
     half_q = width // halves
@@ -195,6 +212,7 @@
         kv_cols = slice(half * half_kv, (half + 1) * half_kv)
         q_cols = slice(half * half_q, (half + 1) * half_q)
         dquery_half, dkey_half, dvalue_half = attention_backward(
+            start_row,
             allowed,
             bwd_query.reshape(tok_rows, width)[:, q_cols],
             bwd_key_all[:, kv_cols],
@@ -215,13 +233,14 @@
 
     key_piece = fwd_all[:, :kv_width]
     value_piece = fwd_all[:, kv_width:]
-    allowed = allowed_of(seg_fwd).astype(jnp.int32)
+    allowed = lax.dynamic_slice_in_dim(allowed_of(seg_fwd).astype(jnp.int32), window_start, window, axis=1)
     fwd_parts = []
     for half in range(halves):
         kv_cols = slice(half * half_kv, (half + 1) * half_kv)
         q_cols = slice(half * half_q, (half + 1) * half_q)
         fwd_parts.append(
             attention_forward(
+                start_row,
                 allowed,
                 fwd_query.reshape(tok_rows, width)[:, q_cols],
                 key_piece[:, kv_cols],

time: 166 us -> 160 us (0.964)
  Pallas kernels: 46.7 us -> 40.8 us
    pallas_call x4, Pallas kernels: 46.7 us -> 40.8 us  [the longest x2 25.8 us: attention_backward(): pl.pallas_call(kernel, grid=(groups,), in_specs=[pl.BlockSpec(memory_spac...]
  transfers between devices with their start and end apart: 6 -> 6, of which waited for: 2 -> 2; matrix products, arithmetic and copies ran while one was open for 20% -> 21% of each run, Pallas kernels for 28% -> 26%
where the time goes in v8:
time: 160 us
  waiting for transfers between devices  46 us (29%)
  Pallas kernels  40.8 us (25%)
  starting transfers between devices  28.1 us (18%)
  local copies, waits for them, and re-layouts  16 us (10%)
  other arithmetic  14.1 us (9%)
  matrix products  13.9 us (9%)
    all_to_all x2, waiting for transfers between devices, gather_all(): moved = lax.all_to_all(spread, axis, 0, 0)  31.1 us
    pallas_call x2, Pallas kernels, attention_backward(): pl.pallas_call(kernel, grid=(groups,), in_specs=[pl.BlockSpec(memory_spac...  25.8 us
    all_to_all x2, starting transfers between devices, gather_all(): moved = lax.all_to_all(spread, axis, 0, 0)  15.5 us
    pallas_call x2, Pallas kernels, attention_forward(): pl.pallas_call(kernel, grid=(groups,), in_specs=[pl.BlockSpec(memory_spac...  15 us
    all_to_all x2, waiting for transfers between devices, reduce_all(): lax.all_to_all(terms.astype(jnp.bfloat16).reshape((count, rows) + terms.s...  14.9 us
    all_to_all x2, starting transfers between devices, reduce_all(): lax.all_to_all(terms.astype(jnp.bfloat16).reshape((count, rows) + terms.s...  11 us
    dot_general x2, matrix products, layer_parts(): jnp.dot(flat, key_weight, preferred_element_type=jnp.float32)  6.52 us
    broadcast_in_dim x2, other arithmetic, body(): return (fwd_out[None], grad_out[None])  4.98 us
  transfers between devices with their start and end apart: 6, of which 2 were waited for; matrix products, arithmetic and copies ran while one was open for 21% of the time, Pallas kernels for 26%

profile of v8, /device:TPU:6, one launch (start us, length us, event | category | flops | bytes accessed | tf_op | source)
XLA Modules:
  0.0 159.6 jit_solution(14338169411368895009)
XLA Ops:
  0.6 0.1 collective-permute-start
  0.7 1.5 fusion.18
  2.2 0.0 copy-start
  2.2 0.0 copy-start.1
  2.3 0.0 copy-start.6
  2.3 3.4 %fusion.31 = bf16[128,512]{1,0:T(8,128)(2,1)S(1)} fusion(bf16[1,4096,512]{2,1,0:T(8,128)(2,1)} %param.12, bf16[1,128,4096]{2,1,0:T(8,128)(2,1)} %param.10, f32[128]{0:T(128)S(1)} %get-tuple-element.45, f32[4096]{0:T(1024)} %bitcast.77), kind=kOutput, calls=%fused_computation.38 | convolution fusion | flops 539033600 | bytes 5390848 | tf_op jit(solution)/shard_map/dot_general | solution.py:182
  5.7 0.0 copy-done
  5.7 0.6 copy-done.1
  6.3 0.0 copy-done.6
  6.3 0.8 fusion.37
  7.2 1.6 %broadcast_in_dim.9 = bf16[8,128,1024]{2,1,0:T(8,128)(2,1)} broadcast(bf16[128,1024]{1,0:T(8,128)(2,1)S(1)} %pad_maximum_fusion.3), dimensions={1,2} | broadcast | bytes 2359296 | tf_op jit(solution)/shard_map/broadcast_in_dim | solution.py:26
  8.8 0.0 copy-start.7
  8.8 0.0 copy-start.8
  8.8 7.9 %all-to-all-start.1 = ((bf16[8,128,1024]{2,1,0:T(8,128)(2,1)}), bf16[8,128,1024]{2,1,0:T(8,128)(2,1)}, u32[]{:S(2)}, u32[]{:S(2)}) async-start(bf16[8,128,1024]{2,1,0:T(8,128)(2,1)} %broadcast_in_dim.9), calls=%async_computation.1 | async-start | bytes 4194304 | tf_op jit(solution)/shard_map/all_to_all | solution.py:27
  16.7 1.5 collective-permute-start.1
  18.2 0.0 copy-done.7
  18.2 0.1 dynamic-slice
  18.2 0.0 copy-done.8
  18.2 0.1 dynamic-slice.1
  18.3 0.1 dynamic_slice.12
  18.4 0.1 dynamic_slice.14
  18.5 0.1 iota_compare_fusion
  18.6 1.1 and_convert_fusion
  19.7 0.0 collective-permute-done
  19.7 0.3 fusion.15
  20.0 0.0 copy-start.2
  20.0 3.1 %fusion.28 = bf16[128,512]{1,0:T(8,128)(2,1)S(1)} fusion(bf16[1,4096,512]{2,1,0:T(8,128)(2,1)} %param.12, bf16[1,128,4096]{2,1,0:T(8,128)(2,1)S(1)} %collective-permute-done, f32[4096]{0:T(1024)S(1)} %bitcast.79, f32[128]{0:T(128)S(1)} %add_rsqrt_fusion.1), kind=kOutput, calls=%fused_computation.37 | convolution fusion | flops 539033600 | bytes 5390848 | tf_op jit(solution)/shard_map/dot_general | solution.py:182
  23.1 0.3 copy-done.2
  23.5 0.8 fusion.34
  24.3 31.1 %all-to-all-done.1 = bf16[8,128,1024]{2,1,0:T(8,128)(2,1)} async-done(((bf16[8,128,1024]{2,1,0:T(8,128)(2,1)}), bf16[8,128,1024]{2,1,0:T(8,128)(2,1)}, u32[]{:S(2)}, u32[]{:S(2)}) %all-to-all-start.1) | async-done | bytes 2097184 | tf_op jit(solution)/shard_map/all_to_all | solution.py:27
  55.4 1.6 broadcast_in_dim.8
  57.0 7.6 %all-to-all-start = ((bf16[8,128,1024]{2,1,0:T(8,128)(2,1)}), bf16[8,128,1024]{2,1,0:T(8,128)(2,1)}, u32[]{:S(2)}, u32[]{:S(2)}) async-start(bf16[8,128,1024]{2,1,0:T(8,128)(2,1)} %broadcast_in_dim.8), calls=%async_computation | async-start | bytes 4194304 | tf_op jit(solution)/shard_map/all_to_all | solution.py:27
  64.6 0.6 fusion.20
  65.2 1.1 fusion.60
  66.3 0.0 collective-permute-done.1
  66.3 2.3 %fusion.59 = (bf16[128,2048]{1,0:T(8,128)(2,1)}, bf16[128,2048]{1,0:T(8,128)(2,1)}) fusion(bf16[128,4096]{1,0:T(8,128)(2,1)} %bitcast.10), kind=kLoop, calls=%fused_computation.67 | loop fusion | bytes 2097152 | tf_op jit(solution)/shard_map/slice | solution.py:220
  68.6 2.9 %fusion.56 = (bf16[1024,256]{1,0:T(8,128)(2,1)}, bf16[1024,256]{1,0:T(8,128)(2,1)}, bf16[1024,256]{1,0:T(8,128)(2,1)}, bf16[1024,256]{1,0:T(8,128)(2,1)}) fusion(bf16[1024,1024]{1,0:T(8,128)(2,1)} %bitcast.9), kind=kLoop, calls=%fused_computation.64 | loop fusion | bytes 4194304 | tf_op jit(solution)/shard_map/slice | solution.py:219
  71.5 12.9 %shard_map.96 = (f32[128,2048]{1,0:T(8,128)}, f32[1024,256]{1,0:T(8,128)}, f32[1024,256]{1,0:T(8,128)}) custom-call(s32[1]{0:T(128)} %bitcast.start_ref, s32[128,640]{1,0:T(8,128)} %get-tuple-element.40.mask_ref, bf16[128,2048]{1,0:T(8,128)(2,1)} %get-tuple-element.34.query_ref, bf16[1024,256]{1,0:T(8,128)(2,1)} %get-tuple-element.25.key_ref, ...), custom_call_target="tpu_custom_call" | custom-call | tf_op jit(solution)/shard_map/pallas_call | solution.py:136
  84.4 12.9 %shard_map.95 = (f32[128,2048]{1,0:T(8,128)}, f32[1024,256]{1,0:T(8,128)}, f32[1024,256]{1,0:T(8,128)}) custom-call(s32[1]{0:T(128)} %bitcast.start_ref, s32[128,640]{1,0:T(8,128)} %get-tuple-element.40.mask_ref, bf16[128,2048]{1,0:T(8,128)(2,1)} %get-tuple-element.35.query_ref, bf16[1024,256]{1,0:T(8,128)(2,1)} %get-tuple-element.27.key_ref, ...), custom_call_target="tpu_custom_call" | custom-call | tf_op jit(solution)/shard_map/pallas_call | solution.py:136
  97.3 3.8 %pad_maximum_fusion = (bf16[1024,512]{1,0:T(8,128)(2,1)}, bf16[1024,512]{1,0:T(8,128)(2,1)}) fusion(f32[1024,256]{1,0:T(8,128)} %get-tuple-element.12, f32[1024,256]{1,0:T(8,128)} %get-tuple-element.11, f32[1024,256]{1,0:T(8,128)} %get-tuple-element.14, f32[1024,256]{1,0:T(8,128)} %get-tuple-element.13), kind=kLoop, calls=%fused_computation.34 | loop fusion | flops 4194304 | bytes 6291456 | tf_op jit(solution)/shard_map/concatenate | solution.py:224
  101.1 0.0 all-to-all-done
  101.1 7.2 %all-to-all-start.2 = ((bf16[8,128,512]{2,1,0:T(8,128)(2,1)}), bf16[8,128,512]{2,1,0:T(8,128)(2,1)}, u32[]{:S(2)}, u32[]{:S(2)}) async-start(bf16[8,128,512]{2,1,0:T(8,128)(2,1)} %bitcast.76), calls=%async_computation.2 | async-start | bytes 2097152 | tf_op jit(solution)/shard_map/all_to_all | solution.py:34
  108.4 1.0 fusion.58
  109.4 1.2 fusion.57
  110.6 14.9 %all-to-all-done.2 = bf16[8,128,512]{2,1,0:T(8,128)(2,1)} async-done(((bf16[8,128,512]{2,1,0:T(8,128)(2,1)}), bf16[8,128,512]{2,1,0:T(8,128)(2,1)}, u32[]{:S(2)}, u32[]{:S(2)}) %all-to-all-start.2) | async-done | bytes 1048608 | tf_op jit(solution)/shard_map/all_to_all | solution.py:34
  125.5 3.8 %all-to-all-start.3 = ((bf16[8,128,512]{2,1,0:T(8,128)(2,1)}), bf16[8,128,512]{2,1,0:T(8,128)(2,1)S(1)}, u32[]{:S(2)}, u32[]{:S(2)}) async-start(bf16[8,128,512]{2,1,0:T(8,128)(2,1)} %bitcast.13), calls=%async_computation.3 | async-start | bytes 2097152 | tf_op jit(solution)/shard_map/all_to_all | solution.py:34
  129.2 2.9 %fusion.55 = (bf16[1024,256]{1,0:T(8,128)(2,1)}, bf16[1024,256]{1,0:T(8,128)(2,1)}, bf16[1024,256]{1,0:T(8,128)(2,1)}, bf16[1024,256]{1,0:T(8,128)(2,1)}) fusion(bf16[1024,1024]{1,0:T(8,128)(2,1)} %bitcast.6), kind=kLoop, calls=%fused_computation.63 | loop fusion | bytes 4194304 | tf_op jit(solution)/shard_map/slice | solution.py:247
  132.2 7.5 %shard_map.97 = bf16[128,2048]{1,0:T(8,128)(2,1)} custom-call(s32[1]{0:T(128)} %bitcast.start_ref, s32[128,640]{1,0:T(8,128)} %get-tuple-element.41.mask_ref, bf16[128,2048]{1,0:T(8,128)(2,1)} %get-tuple-element.30.query_ref, bf16[1024,256]{1,0:T(8,128)(2,1)} %get-tuple-element.23.key_ref, bf16[1024,256]{1,0:T(8,128)(2,1)} %get-tuple-element.20.value_ref, ...), custom_call_target="tpu_custom_call" | custom-call | tf_op jit(solution)/shard_map/pallas_call | solution.py:112
  139.7 0.0 copy-start.4
  139.7 7.5 %shard_map.98 = bf16[128,2048]{1,0:T(8,128)(2,1)} custom-call(s32[1]{0:T(128)} %bitcast.start_ref, s32[128,640]{1,0:T(8,128)} %get-tuple-element.41.mask_ref, bf16[128,2048]{1,0:T(8,128)(2,1)} %get-tuple-element.31.query_ref, bf16[1024,256]{1,0:T(8,128)(2,1)} %get-tuple-element.22.key_ref, bf16[1024,256]{1,0:T(8,128)(2,1)} %get-tuple-element.21.value_ref, ...), custom_call_target="tpu_custom_call" | custom-call | tf_op jit(solution)/shard_map/pallas_call | solution.py:112
  147.2 0.0 copy-done.4
  147.2 2.1 %maximum_bitcast_fusion = bf16[1,128,4096]{2,1,0:T(8,128)(2,1)} fusion(bf16[128,2048]{1,0:T(8,128)(2,1)} %shard_map.98, bf16[128,2048]{1,0:T(8,128)(2,1)S(1)} %copy-done.4), kind=kLoop, calls=%fused_computation.44 | loop fusion | flops 2097152 | bytes 2097152 | tf_op jit(solution)/shard_map/broadcast_in_dim | solution.py:267
  149.3 0.0 copy-start.5
  149.3 1.5 reduce_sum.53
  150.8 0.0 all-to-all-done.3
  150.8 0.1 reduce_sum.54
  151.0 0.0 copy-done.5
  151.0 0.0 copy-start.3
  151.0 4.1 %convolution_add_fusion.1 = f32[128,4096]{1,0:T(8,128)S(1)} fusion(bf16[1,4096,512]{2,1,0:T(8,128)(2,1)} %param.12, f32[128,2048]{1,0:T(8,128)S(1)} %copy-done.5, f32[128,2048]{1,0:T(8,128)} %get-tuple-element.16, bf16[128,256]{1,0:T(8,128)(2,1)S(1)} %get-tuple-element.39, bf16[128,256]{1,0:T(8,128)(2,1)S(1)} %get-tuple-element.37), kind=kOutput, calls=%fused_computation.2 | convolution fusion | flops 538181632 | bytes 8519680 | tf_op jit(solution)/shard_map/dot_general | solution.py:254
  155.1 0.0 copy-done.3
  155.1 1.6 %fusion.25 = (f32[128]{0:T(128)S(1)}, f32[128,4096]{1,0:T(8,128)S(1)}) fusion(bf16[1,128,4096]{2,1,0:T(8,128)(2,1)S(1)} %copy-done, f32[128,4096]{1,0:T(8,128)S(1)} %convolution_add_fusion.1, bf16[1,4096,512]{2,1,0:T(8,128)(2,1)S(1)} %copy-done.3, bf16[128,256]{1,0:T(8,128)(2,1)S(1)} %get-tuple-element.38, bf16[128,256]{1,0:T(8,128)(2,1)S(1)} %get-tuple-element.36, ...), kind=kOutput, calls=%fused_computation.31 | convolution fusion | flops 539754368 | bytes 9585152 | tf_op jit(solution)/shard_map/dot_general | solution.py:257
  156.7 2.9 %fusion.42 = bf16[1,128,4096]{2,1,0:T(8,128)(2,1)} fusion(bf16[1,128,4096]{2,1,0:T(8,128)(2,1)S(1)} %copy-done, f32[128,4096]{1,0:T(8,128)S(1)} %get-tuple-element.47, f32[128]{0:T(128)S(1)} %broadcast_multiply_fusion, f32[128]{0:T(128)S(1)} %get-tuple-element.44, f32[128]{0:T(128)S(1)} %get-tuple-element.45, bf16[1,128,4096]{2,1,0:T(8,128)(2,1)} %collective-permute-done.1), kind=kLoop, calls=%fused_computation.43 | loop fusion | flops 4194304 | bytes 5244416 | tf_op jit(solution)/shard_map/broadcast_in_dim | solution.py:267
  (8 shorter events, 0.1 us)
Async XLA Ops:
  0.6 19.1 %collective-permute-start = (bf16[1,128,4096]{2,1,0:T(8,128)(2,1)}, bf16[1,128,4096]{2,1,0:T(8,128)(2,1)S(1)}, u32[]{:S(2)}, u32[]{:S(2)}) collective-permute-start(bf16[1,128,4096]{2,1,0:T(8,128)(2,1)} %param.8), channel_id=1, source_target_pairs={{120,0},{0,8},{8,16},{16,24},{24,32},{32,40},{40,48},{48,56},{56,6... | collective-permute-start | bytes 3145736 | tf_op jit(solution)/shard_map/ppermute | solution.py:21
  2.2 3.5 %copy-start = (bf16[1,128,4096]{2,1,0:T(8,128)(2,1)S(1)}, bf16[1,128,4096]{2,1,0:T(8,128)(2,1)}, u32[]{:S(2)}) copy-start(bf16[1,128,4096]{2,1,0:T(8,128)(2,1)} %param.10) | copy-start | bytes 3145732
  2.2 4.1 %copy-start.1 = (bf16[1,4096,512]{2,1,0:T(8,128)(2,1)S(1)}, bf16[1,4096,512]{2,1,0:T(8,128)(2,1)}, u32[]{:S(2)}) copy-start(bf16[1,4096,512]{2,1,0:T(8,128)(2,1)} %param.13) | copy-start | bytes 12582916
  2.3 4.1 %copy-start.6 = (f32[1,4096]{1,0:T(1,128)S(1)}, f32[1,4096]{1,0:T(1,128)}, u32[]{:S(2)}) copy-start(f32[1,4096]{1,0:T(1,128)} %param.11) | copy-start | bytes 49156
  8.8 9.4 %copy-start.7 = (s32[1024]{0:T(1024)S(1)}, s32[1024]{0:T(1024)}, u32[]{:S(2)}) copy-start(s32[1024]{0:T(1024)} %param.14) | copy-start | bytes 12292
  8.8 9.4 %copy-start.8 = (s32[1024]{0:T(1024)S(1)}, s32[1024]{0:T(1024)}, u32[]{:S(2)}) copy-start(s32[1024]{0:T(1024)} %param.15) | copy-start | bytes 12292
  8.8 46.6 %all-to-all-start.1 = ((bf16[8,128,1024]{2,1,0:T(8,128)(2,1)}), bf16[8,128,1024]{2,1,0:T(8,128)(2,1)}, u32[]{:S(2)}, u32[]{:S(2)}) async-start(bf16[8,128,1024]{2,1,0:T(8,128)(2,1)} %broadcast_in_dim.9), calls=%async_computation.1 | async-start | bytes 4194304 | tf_op jit(solution)/shard_map/all_to_all | solution.py:27
  16.7 49.6 %collective-permute-start.1 = (bf16[1,128,4096]{2,1,0:T(8,128)(2,1)}, bf16[1,128,4096]{2,1,0:T(8,128)(2,1)}, u32[]{:S(2)}, u32[]{:S(2)}) collective-permute-start(bf16[1,128,4096]{2,1,0:T(8,128)(2,1)} %param.9), channel_id=1, source_target_pairs={{8,0},{16,8},{24,16},{32,24},{40,32},{48,40},{56,48},{64,56},{72,6... | collective-permute-start | bytes 3145736 | tf_op jit(solution)/shard_map/ppermute | solution.py:21
  20.0 3.5 %copy-start.2 = (bf16[1,4096,512]{2,1,0:T(8,128)(2,1)S(1)}, bf16[1,4096,512]{2,1,0:T(8,128)(2,1)}, u32[]{:S(2)}) copy-start(bf16[1,4096,512]{2,1,0:T(8,128)(2,1)} %param.13) | copy-start | bytes 12582916
  57.0 44.1 %all-to-all-start = ((bf16[8,128,1024]{2,1,0:T(8,128)(2,1)}), bf16[8,128,1024]{2,1,0:T(8,128)(2,1)}, u32[]{:S(2)}, u32[]{:S(2)}) async-start(bf16[8,128,1024]{2,1,0:T(8,128)(2,1)} %broadcast_in_dim.8), calls=%async_computation | async-start | bytes 4194304 | tf_op jit(solution)/shard_map/all_to_all | solution.py:27
  101.1 24.3 %all-to-all-start.2 = ((bf16[8,128,512]{2,1,0:T(8,128)(2,1)}), bf16[8,128,512]{2,1,0:T(8,128)(2,1)}, u32[]{:S(2)}, u32[]{:S(2)}) async-start(bf16[8,128,512]{2,1,0:T(8,128)(2,1)} %bitcast.76), calls=%async_computation.2 | async-start | bytes 2097152 | tf_op jit(solution)/shard_map/all_to_all | solution.py:34
  125.5 25.3 %all-to-all-start.3 = ((bf16[8,128,512]{2,1,0:T(8,128)(2,1)}), bf16[8,128,512]{2,1,0:T(8,128)(2,1)S(1)}, u32[]{:S(2)}, u32[]{:S(2)}) async-start(bf16[8,128,512]{2,1,0:T(8,128)(2,1)} %bitcast.13), calls=%async_computation.3 | async-start | bytes 2097152 | tf_op jit(solution)/shard_map/all_to_all | solution.py:34
  139.7 7.5 %copy-start.4 = (bf16[128,2048]{1,0:T(8,128)(2,1)S(1)}, bf16[128,2048]{1,0:T(8,128)(2,1)}, u32[]{:S(2)}) copy-start(bf16[128,2048]{1,0:T(8,128)(2,1)} %shard_map.97) | copy-start | bytes 1572868
  149.3 1.7 %copy-start.5 = (f32[128,2048]{1,0:T(8,128)S(1)}, f32[128,2048]{1,0:T(8,128)}, u32[]{:S(2)}) copy-start(f32[128,2048]{1,0:T(8,128)} %get-tuple-element.17) | copy-start | bytes 3145732
  151.0 4.1 %copy-start.3 = (bf16[1,4096,512]{2,1,0:T(8,128)(2,1)S(1)}, bf16[1,4096,512]{2,1,0:T(8,128)(2,1)}, u32[]{:S(2)}) copy-start(bf16[1,4096,512]{2,1,0:T(8,128)(2,1)} %param.13) | copy-start | bytes 12582916

commit v9 on v8

--- a/solution.py
+++ b/solution.py
@@ -223,17 +223,18 @@
         dquery_parts.append(dquery_half)
         half_terms.append(jnp.concatenate([dkey_half, dvalue_half], axis=1))
     fwd_all, half_terms = lax.optimization_barrier((fwd_all, half_terms))
-    for terms in half_terms:
-        dkv_half = reduce_all(terms, "ctx").astype(jnp.bfloat16)
-        dkey_parts.append(dkv_half[:, :half_kv])
-        dvalue_parts.append(dkv_half[:, half_kv:])
+
+    key_piece = fwd_all[:, :kv_width]
+    value_piece = fwd_all[:, kv_width:]
+    allowed = lax.dynamic_slice_in_dim(allowed_of(seg_fwd).astype(jnp.int32), window_start, window, axis=1)
+    dkv_all = reduce_all(jnp.concatenate(half_terms, axis=1), "ctx").astype(jnp.bfloat16)
+    for half in range(halves):
+        base = half * 2 * half_kv
+        dkey_parts.append(dkv_all[:, base:base + half_kv])
+        dvalue_parts.append(dkv_all[:, base + half_kv:base + 2 * half_kv])
     dquery = jnp.concatenate(dquery_parts, axis=1)
     dkeys = jnp.concatenate(dkey_parts, axis=1)
     dvalues = jnp.concatenate(dvalue_parts, axis=1)
-
-    key_piece = fwd_all[:, :kv_width]
-    value_piece = fwd_all[:, kv_width:]
-    allowed = lax.dynamic_slice_in_dim(allowed_of(seg_fwd).astype(jnp.int32), window_start, window, axis=1)
     fwd_parts = []
     for half in range(halves):
         kv_cols = slice(half * half_kv, (half + 1) * half_kv)

time: 160 us -> 151 us (0.944)
  waiting for transfers between devices: 46 us -> 37.2 us
  starting transfers between devices: 28.1 us -> 24.3 us
  other arithmetic: 14.1 us -> 17.5 us
    all_to_all x2 -> x1, waiting for transfers between devices: 14.9 us -> 6.11 us  [reduce_all(): lax.all_to_all(terms.astype(jnp.bfloat16).reshape((count, rows) + terms.s...]
    all_to_all x2 -> x1, starting transfers between devices: 11 us -> 7.21 us  [reduce_all(): lax.all_to_all(terms.astype(jnp.bfloat16).reshape((count, rows) + terms.s...]
    concatenate x0 -> x1, other arithmetic: none -> 3.1 us  [body(): jnp.concatenate(half_terms, axis=1)]
  transfers between devices with their start and end apart: 6 -> 5, of which waited for: 2 -> 2; matrix products, arithmetic and copies ran while one was open for 21% -> 22% of each run, Pallas kernels for 26% -> 27%
where the time goes in v9:
time: 151 us; the launch traced here: 150 us
  Pallas kernels  40.7 us (27%)
  waiting for transfers between devices  37.2 us (25%)
  starting transfers between devices  24.3 us (16%)
  other arithmetic  17.5 us (12%)
  local copies, waits for them, and re-layouts  15.9 us (11%)
  matrix products  13.9 us (9%)
    all_to_all x2, waiting for transfers between devices, gather_all(): moved = lax.all_to_all(spread, axis, 0, 0)  31.1 us
    pallas_call x2, Pallas kernels, attention_backward(): pl.pallas_call(kernel, grid=(groups,), in_specs=[pl.BlockSpec(memory_spac...  25.7 us
    all_to_all x2, starting transfers between devices, gather_all(): moved = lax.all_to_all(spread, axis, 0, 0)  15.5 us
    pallas_call x2, Pallas kernels, attention_forward(): pl.pallas_call(kernel, grid=(groups,), in_specs=[pl.BlockSpec(memory_spac...  15 us
    all_to_all x1, starting transfers between devices, reduce_all(): lax.all_to_all(terms.astype(jnp.bfloat16).reshape((count, rows) + terms.s...  7.21 us
    dot_general x2, matrix products, layer_parts(): jnp.dot(flat, key_weight, preferred_element_type=jnp.float32)  6.52 us
    all_to_all x1, waiting for transfers between devices, reduce_all(): lax.all_to_all(terms.astype(jnp.bfloat16).reshape((count, rows) + terms.s...  6.11 us
    broadcast_in_dim x2, other arithmetic, body(): return (fwd_out[None], grad_out[None])  5.07 us
  transfers between devices with their start and end apart: 5, of which 2 were waited for; matrix products, arithmetic and copies ran while one was open for 22% of the time, Pallas kernels for 27%

profile of v9, /device:TPU:6, one launch (start us, length us, event | category | flops | bytes accessed | tf_op | source)
XLA Modules:
  0.0 150.3 jit_solution(13040903904852043974)
XLA Ops:
  0.6 0.1 collective-permute-start
  0.7 1.5 %fusion.18 = f32[128]{0:T(128)S(1)} fusion(bf16[1,128,4096]{2,1,0:T(8,128)(2,1)} %param.10), kind=kLoop, calls=%fused_computation.24 | loop fusion | flops 1572736 | bytes 1049088 | tf_op jit(solution)/shard_map/reduce_sum | solution.py:40
  2.2 0.0 copy-start
  2.2 0.0 copy-start.1
  2.3 0.0 copy-start.6
  2.3 3.4 %fusion.31 = bf16[128,512]{1,0:T(8,128)(2,1)S(1)} fusion(bf16[1,4096,512]{2,1,0:T(8,128)(2,1)} %param.12, bf16[1,128,4096]{2,1,0:T(8,128)(2,1)} %param.10, f32[128]{0:T(128)S(1)} %get-tuple-element.45, f32[4096]{0:T(1024)} %bitcast.78), kind=kOutput, calls=%fused_computation.39 | convolution fusion | flops 539033600 | bytes 5390848 | tf_op jit(solution)/shard_map/dot_general | solution.py:182
  5.7 0.0 copy-done
  5.7 0.6 copy-done.1
  6.3 0.0 copy-done.6
  6.3 0.8 fusion.37
  7.2 1.6 %broadcast_in_dim.9 = bf16[8,128,1024]{2,1,0:T(8,128)(2,1)} broadcast(bf16[128,1024]{1,0:T(8,128)(2,1)S(1)} %pad_maximum_fusion.4), dimensions={1,2} | broadcast | bytes 2359296 | tf_op jit(solution)/shard_map/broadcast_in_dim | solution.py:26
  8.8 0.0 copy-start.7
  8.8 0.0 copy-start.8
  8.8 7.9 %all-to-all-start.1 = ((bf16[8,128,1024]{2,1,0:T(8,128)(2,1)}), bf16[8,128,1024]{2,1,0:T(8,128)(2,1)}, u32[]{:S(2)}, u32[]{:S(2)}) async-start(bf16[8,128,1024]{2,1,0:T(8,128)(2,1)} %broadcast_in_dim.9), calls=%async_computation.1 | async-start | bytes 4194304 | tf_op jit(solution)/shard_map/all_to_all | solution.py:27
  16.7 1.5 collective-permute-start.1
  18.2 0.0 copy-done.7
  18.2 0.1 dynamic-slice
  18.2 0.0 copy-done.8
  18.2 0.1 dynamic-slice.1
  18.3 0.1 dynamic_slice.12
  18.4 0.1 dynamic_slice.14
  18.5 0.1 iota_compare_fusion
  18.6 1.1 and_convert_fusion
  19.7 0.0 collective-permute-done
  19.7 0.3 fusion.15
  20.0 0.0 copy-start.2
  20.0 3.1 %fusion.28 = bf16[128,512]{1,0:T(8,128)(2,1)S(1)} fusion(bf16[1,4096,512]{2,1,0:T(8,128)(2,1)} %param.12, bf16[1,128,4096]{2,1,0:T(8,128)(2,1)S(1)} %collective-permute-done, f32[4096]{0:T(1024)S(1)} %bitcast.80, f32[128]{0:T(128)S(1)} %add_rsqrt_fusion.1), kind=kOutput, calls=%fused_computation.38 | convolution fusion | flops 539033600 | bytes 5390848 | tf_op jit(solution)/shard_map/dot_general | solution.py:182
  23.1 0.3 copy-done.2
  23.4 0.8 fusion.34
  24.3 31.1 %all-to-all-done.1 = bf16[8,128,1024]{2,1,0:T(8,128)(2,1)} async-done(((bf16[8,128,1024]{2,1,0:T(8,128)(2,1)}), bf16[8,128,1024]{2,1,0:T(8,128)(2,1)}, u32[]{:S(2)}, u32[]{:S(2)}) %all-to-all-start.1) | async-done | bytes 2097184 | tf_op jit(solution)/shard_map/all_to_all | solution.py:27
  55.4 1.6 %broadcast_in_dim.8 = bf16[8,128,1024]{2,1,0:T(8,128)(2,1)} broadcast(bf16[128,1024]{1,0:T(8,128)(2,1)S(1)} %pad_maximum_fusion.3), dimensions={1,2} | broadcast | bytes 2359296 | tf_op jit(solution)/shard_map/broadcast_in_dim | solution.py:26
  57.0 7.6 %all-to-all-start = ((bf16[8,128,1024]{2,1,0:T(8,128)(2,1)}), bf16[8,128,1024]{2,1,0:T(8,128)(2,1)}, u32[]{:S(2)}, u32[]{:S(2)}) async-start(bf16[8,128,1024]{2,1,0:T(8,128)(2,1)} %broadcast_in_dim.8), calls=%async_computation | async-start | bytes 4194304 | tf_op jit(solution)/shard_map/all_to_all | solution.py:27
  64.6 0.6 fusion.20
  65.2 1.0 fusion.60
  66.2 0.0 collective-permute-done.1
  66.3 2.3 %fusion.59 = (bf16[128,2048]{1,0:T(8,128)(2,1)}, bf16[128,2048]{1,0:T(8,128)(2,1)}) fusion(bf16[128,4096]{1,0:T(8,128)(2,1)} %bitcast.10), kind=kLoop, calls=%fused_computation.68 | loop fusion | bytes 2097152 | tf_op jit(solution)/shard_map/slice | solution.py:220
  68.6 2.9 %fusion.56 = (bf16[1024,256]{1,0:T(8,128)(2,1)}, bf16[1024,256]{1,0:T(8,128)(2,1)}, bf16[1024,256]{1,0:T(8,128)(2,1)}, bf16[1024,256]{1,0:T(8,128)(2,1)}) fusion(bf16[1024,1024]{1,0:T(8,128)(2,1)} %bitcast.9), kind=kLoop, calls=%fused_computation.65 | loop fusion | bytes 4194304 | tf_op jit(solution)/shard_map/slice | solution.py:219
  71.5 12.8 %shard_map.96 = (f32[128,2048]{1,0:T(8,128)}, f32[1024,256]{1,0:T(8,128)}, f32[1024,256]{1,0:T(8,128)}) custom-call(s32[1]{0:T(128)} %bitcast.start_ref, s32[128,640]{1,0:T(8,128)} %get-tuple-element.40.mask_ref, bf16[128,2048]{1,0:T(8,128)(2,1)} %get-tuple-element.34.query_ref, bf16[1024,256]{1,0:T(8,128)(2,1)} %get-tuple-element.25.key_ref, ...), custom_call_target="tpu_custom_call" | custom-call | tf_op jit(solution)/shard_map/pallas_call | solution.py:136
  84.3 12.9 %shard_map.95 = (f32[128,2048]{1,0:T(8,128)}, f32[1024,256]{1,0:T(8,128)}, f32[1024,256]{1,0:T(8,128)}) custom-call(s32[1]{0:T(128)} %bitcast.start_ref, s32[128,640]{1,0:T(8,128)} %get-tuple-element.40.mask_ref, bf16[128,2048]{1,0:T(8,128)(2,1)} %get-tuple-element.35.query_ref, bf16[1024,256]{1,0:T(8,128)(2,1)} %get-tuple-element.27.key_ref, ...), custom_call_target="tpu_custom_call" | custom-call | tf_op jit(solution)/shard_map/pallas_call | solution.py:136
  97.2 3.7 %pad_maximum_fusion = (bf16[1024,512]{1,0:T(8,128)(2,1)}, bf16[1024,512]{1,0:T(8,128)(2,1)}) fusion(f32[1024,256]{1,0:T(8,128)} %get-tuple-element.12, f32[1024,256]{1,0:T(8,128)} %get-tuple-element.11, f32[1024,256]{1,0:T(8,128)} %get-tuple-element.14, f32[1024,256]{1,0:T(8,128)} %get-tuple-element.13), kind=kLoop, calls=%fused_computation.34 | loop fusion | flops 4194304 | bytes 6291456 | tf_op jit(solution)/shard_map/concatenate | solution.py:224
  100.9 0.0 all-to-all-done
  100.9 3.1 %pad_maximum_fusion.2 = bf16[8,128,1024]{2,1,0:T(8,128)(2,1)} fusion(bf16[8,128,512]{2,1,0:T(8,128)(2,1)} %bitcast.77, bf16[8,128,512]{2,1,0:T(8,128)(2,1)} %bitcast.76), kind=kLoop, calls=%fused_computation.36 | loop fusion | flops 4194304 | bytes 4194304 | tf_op jit(solution)/shard_map/concatenate | solution.py:230
  104.0 7.2 %all-to-all-start.2 = ((bf16[8,128,1024]{2,1,0:T(8,128)(2,1)}), bf16[8,128,1024]{2,1,0:T(8,128)(2,1)}, u32[]{:S(2)}, u32[]{:S(2)}) async-start(bf16[8,128,1024]{2,1,0:T(8,128)(2,1)} %pad_maximum_fusion.2), calls=%async_computation.2 | async-start | bytes 4194304 | tf_op jit(solution)/shard_map/all_to_all | solution.py:34
  111.2 1.1 fusion.58
  112.3 1.1 fusion.57
  113.4 2.9 %fusion.55 = (bf16[1024,256]{1,0:T(8,128)(2,1)}, bf16[1024,256]{1,0:T(8,128)(2,1)}, bf16[1024,256]{1,0:T(8,128)(2,1)}, bf16[1024,256]{1,0:T(8,128)(2,1)}) fusion(bf16[1024,1024]{1,0:T(8,128)(2,1)} %bitcast.6), kind=kLoop, calls=%fused_computation.64 | loop fusion | bytes 4194304 | tf_op jit(solution)/shard_map/slice | solution.py:248
  116.3 7.5 %shard_map.97 = bf16[128,2048]{1,0:T(8,128)(2,1)} custom-call(s32[1]{0:T(128)} %bitcast.start_ref, s32[128,640]{1,0:T(8,128)} %get-tuple-element.41.mask_ref, bf16[128,2048]{1,0:T(8,128)(2,1)} %get-tuple-element.30.query_ref, bf16[1024,256]{1,0:T(8,128)(2,1)} %get-tuple-element.23.key_ref, bf16[1024,256]{1,0:T(8,128)(2,1)} %get-tuple-element.20.value_ref, ...), custom_call_target="tpu_custom_call" | custom-call | tf_op jit(solution)/shard_map/pallas_call | solution.py:112
  123.8 0.0 copy-start.4
  123.8 7.5 %shard_map.98 = bf16[128,2048]{1,0:T(8,128)(2,1)} custom-call(s32[1]{0:T(128)} %bitcast.start_ref, s32[128,640]{1,0:T(8,128)} %get-tuple-element.41.mask_ref, bf16[128,2048]{1,0:T(8,128)(2,1)} %get-tuple-element.31.query_ref, bf16[1024,256]{1,0:T(8,128)(2,1)} %get-tuple-element.22.key_ref, bf16[1024,256]{1,0:T(8,128)(2,1)} %get-tuple-element.21.value_ref, ...), custom_call_target="tpu_custom_call" | custom-call | tf_op jit(solution)/shard_map/pallas_call | solution.py:112
  131.3 0.0 copy-done.4
  131.3 0.0 copy-start.5
  131.3 2.2 %maximum_bitcast_fusion = bf16[1,128,4096]{2,1,0:T(8,128)(2,1)} fusion(bf16[128,2048]{1,0:T(8,128)(2,1)} %shard_map.98, bf16[128,2048]{1,0:T(8,128)(2,1)S(1)} %copy-done.4), kind=kLoop, calls=%fused_computation.45 | loop fusion | flops 2097152 | bytes 2097152 | tf_op jit(solution)/shard_map/broadcast_in_dim | solution.py:268
  133.5 6.1 %all-to-all-done.2 = bf16[8,128,1024]{2,1,0:T(8,128)(2,1)} async-done(((bf16[8,128,1024]{2,1,0:T(8,128)(2,1)}), bf16[8,128,1024]{2,1,0:T(8,128)(2,1)}, u32[]{:S(2)}, u32[]{:S(2)}) %all-to-all-start.2) | async-done | bytes 2097184 | tf_op jit(solution)/shard_map/all_to_all | solution.py:34
  139.6 2.0 %reduce_sum.41 = bf16[128,1024]{1,0:T(8,128)(2,1)S(1)} reduce(bf16[8,128,1024]{2,1,0:T(8,128)(2,1)} %all-to-all-done.2, bf16[]{:T(256)} %constant.25.clone.1), dimensions={0}, to_apply=%region_2.0 | reduce | flops 917504 | bytes 2359298 | tf_op jit(solution)/shard_map/reduce_sum | solution.py:35
  141.6 0.0 copy-done.5
  141.6 0.0 copy-start.3
  141.6 4.1 %convolution_add_fusion.1 = f32[128,4096]{1,0:T(8,128)S(1)} fusion(bf16[1,4096,512]{2,1,0:T(8,128)(2,1)} %param.12, f32[128,2048]{1,0:T(8,128)S(1)} %copy-done.5, f32[128,2048]{1,0:T(8,128)} %get-tuple-element.16, bf16[128,256]{1,0:T(8,128)(2,1)S(1)} %get-tuple-element.38, bf16[128,256]{1,0:T(8,128)(2,1)S(1)} %get-tuple-element.39), kind=kOutput, calls=%fused_computation.2 | convolution fusion | flops 538181632 | bytes 8519680 | tf_op jit(solution)/shard_map/dot_general | solution.py:255
  145.7 0.0 copy-done.3
  145.8 1.6 %fusion.25 = (f32[128]{0:T(128)S(1)}, f32[128,4096]{1,0:T(8,128)S(1)}) fusion(bf16[1,128,4096]{2,1,0:T(8,128)(2,1)S(1)} %copy-done, f32[128,4096]{1,0:T(8,128)S(1)} %convolution_add_fusion.1, bf16[1,4096,512]{2,1,0:T(8,128)(2,1)S(1)} %copy-done.3, bf16[128,256]{1,0:T(8,128)(2,1)S(1)} %get-tuple-element.37, bf16[128,256]{1,0:T(8,128)(2,1)S(1)} %get-tuple-element.36, ...), kind=kOutput, calls=%fused_computation.31 | convolution fusion | flops 539754368 | bytes 9585152 | tf_op jit(solution)/shard_map/dot_general | solution.py:258
  147.4 2.9 %fusion.42 = bf16[1,128,4096]{2,1,0:T(8,128)(2,1)} fusion(bf16[1,128,4096]{2,1,0:T(8,128)(2,1)S(1)} %copy-done, f32[128,4096]{1,0:T(8,128)S(1)} %get-tuple-element.47, f32[128]{0:T(128)S(1)} %broadcast_multiply_fusion, f32[128]{0:T(128)S(1)} %get-tuple-element.44, f32[128]{0:T(128)S(1)} %get-tuple-element.45, bf16[1,128,4096]{2,1,0:T(8,128)(2,1)} %collective-permute-done.1), kind=kLoop, calls=%fused_computation.44 | loop fusion | flops 4194304 | bytes 5244416 | tf_op jit(solution)/shard_map/broadcast_in_dim | solution.py:268
  (7 shorter events, 0.1 us)
Async XLA Ops:
  0.6 19.1 %collective-permute-start = (bf16[1,128,4096]{2,1,0:T(8,128)(2,1)}, bf16[1,128,4096]{2,1,0:T(8,128)(2,1)S(1)}, u32[]{:S(2)}, u32[]{:S(2)}) collective-permute-start(bf16[1,128,4096]{2,1,0:T(8,128)(2,1)} %param.8), channel_id=1, source_target_pairs={{120,0},{0,8},{8,16},{16,24},{24,32},{32,40},{40,48},{48,56},{56,6... | collective-permute-start | bytes 3145736 | tf_op jit(solution)/shard_map/ppermute | solution.py:21
  2.2 3.5 %copy-start = (bf16[1,128,4096]{2,1,0:T(8,128)(2,1)S(1)}, bf16[1,128,4096]{2,1,0:T(8,128)(2,1)}, u32[]{:S(2)}) copy-start(bf16[1,128,4096]{2,1,0:T(8,128)(2,1)} %param.10) | copy-start | bytes 3145732
  2.2 4.1 %copy-start.1 = (bf16[1,4096,512]{2,1,0:T(8,128)(2,1)S(1)}, bf16[1,4096,512]{2,1,0:T(8,128)(2,1)}, u32[]{:S(2)}) copy-start(bf16[1,4096,512]{2,1,0:T(8,128)(2,1)} %param.13) | copy-start | bytes 12582916
  2.3 4.1 %copy-start.6 = (f32[1,4096]{1,0:T(1,128)S(1)}, f32[1,4096]{1,0:T(1,128)}, u32[]{:S(2)}) copy-start(f32[1,4096]{1,0:T(1,128)} %param.11) | copy-start | bytes 49156
  8.8 9.4 %copy-start.7 = (s32[1024]{0:T(1024)S(1)}, s32[1024]{0:T(1024)}, u32[]{:S(2)}) copy-start(s32[1024]{0:T(1024)} %param.14) | copy-start | bytes 12292
  8.8 9.4 %copy-start.8 = (s32[1024]{0:T(1024)S(1)}, s32[1024]{0:T(1024)}, u32[]{:S(2)}) copy-start(s32[1024]{0:T(1024)} %param.15) | copy-start | bytes 12292
  8.8 46.6 %all-to-all-start.1 = ((bf16[8,128,1024]{2,1,0:T(8,128)(2,1)}), bf16[8,128,1024]{2,1,0:T(8,128)(2,1)}, u32[]{:S(2)}, u32[]{:S(2)}) async-start(bf16[8,128,1024]{2,1,0:T(8,128)(2,1)} %broadcast_in_dim.9), calls=%async_computation.1 | async-start | bytes 4194304 | tf_op jit(solution)/shard_map/all_to_all | solution.py:27
  16.7 49.5 %collective-permute-start.1 = (bf16[1,128,4096]{2,1,0:T(8,128)(2,1)}, bf16[1,128,4096]{2,1,0:T(8,128)(2,1)}, u32[]{:S(2)}, u32[]{:S(2)}) collective-permute-start(bf16[1,128,4096]{2,1,0:T(8,128)(2,1)} %param.9), channel_id=1, source_target_pairs={{8,0},{16,8},{24,16},{32,24},{40,32},{48,40},{56,48},{64,56},{72,6... | collective-permute-start | bytes 3145736 | tf_op jit(solution)/shard_map/ppermute | solution.py:21
  20.0 3.5 %copy-start.2 = (bf16[1,4096,512]{2,1,0:T(8,128)(2,1)S(1)}, bf16[1,4096,512]{2,1,0:T(8,128)(2,1)}, u32[]{:S(2)}) copy-start(bf16[1,4096,512]{2,1,0:T(8,128)(2,1)} %param.13) | copy-start | bytes 12582916
  57.0 43.9 %all-to-all-start = ((bf16[8,128,1024]{2,1,0:T(8,128)(2,1)}), bf16[8,128,1024]{2,1,0:T(8,128)(2,1)}, u32[]{:S(2)}, u32[]{:S(2)}) async-start(bf16[8,128,1024]{2,1,0:T(8,128)(2,1)} %broadcast_in_dim.8), calls=%async_computation | async-start | bytes 4194304 | tf_op jit(solution)/shard_map/all_to_all | solution.py:27
  104.0 35.6 %all-to-all-start.2 = ((bf16[8,128,1024]{2,1,0:T(8,128)(2,1)}), bf16[8,128,1024]{2,1,0:T(8,128)(2,1)}, u32[]{:S(2)}, u32[]{:S(2)}) async-start(bf16[8,128,1024]{2,1,0:T(8,128)(2,1)} %pad_maximum_fusion.2), calls=%async_computation.2 | async-start | bytes 4194304 | tf_op jit(solution)/shard_map/all_to_all | solution.py:34
  123.8 7.5 %copy-start.4 = (bf16[128,2048]{1,0:T(8,128)(2,1)S(1)}, bf16[128,2048]{1,0:T(8,128)(2,1)}, u32[]{:S(2)}) copy-start(bf16[128,2048]{1,0:T(8,128)(2,1)} %shard_map.97) | copy-start | bytes 1572868
  131.3 10.3 %copy-start.5 = (f32[128,2048]{1,0:T(8,128)S(1)}, f32[128,2048]{1,0:T(8,128)}, u32[]{:S(2)}) copy-start(f32[128,2048]{1,0:T(8,128)} %get-tuple-element.17) | copy-start | bytes 3145732
  141.6 4.1 %copy-start.3 = (bf16[1,4096,512]{2,1,0:T(8,128)(2,1)S(1)}, bf16[1,4096,512]{2,1,0:T(8,128)(2,1)}, u32[]{:S(2)}) copy-start(bf16[1,4096,512]{2,1,0:T(8,128)(2,1)} %param.13) | copy-start | bytes 12582916

commit v10 on v9

--- a/solution.py
+++ b/solution.py
@@ -57,7 +57,7 @@
         ) * scale
         scores = jnp.where(allowed, scores, NEGATIVE)
         rowmax = jnp.max(scores, axis=1, keepdims=True)
-        expo = jnp.where(allowed, jnp.exp(scores - rowmax), 0.0)
+        expo = jnp.exp(scores - rowmax)
         total = jnp.sum(expo, axis=1, keepdims=True)
         product = jnp.dot(expo.astype(jnp.bfloat16), values, preferred_element_type=jnp.float32)
         out_ref[:, cols] = (input_ref[:, cols].astype(jnp.float32) + product / total).astype(out_ref.dtype)
@@ -80,9 +80,9 @@
         ) * scale
         scores = jnp.where(allowed, scores, NEGATIVE)
         rowmax = jnp.max(scores, axis=1, keepdims=True)
-        expo = jnp.where(allowed, jnp.exp(scores - rowmax), 0.0)
+        expo = jnp.exp(scores - rowmax)
         total = jnp.sum(expo, axis=1, keepdims=True)
-        probs = expo / total
+        probs = expo * (1.0 / total)
         dprob = lax.dot_general(
             grad, values, (((1,), (1,)), ((), ())), preferred_element_type=jnp.float32
         )

time: 151 us -> 151 us (level)
  no operation moved by 1% of the time
where the time goes in v10:
time: 151 us; the launch traced here: 150 us
  Pallas kernels  40.2 us (27%)
  waiting for transfers between devices  37.5 us (25%)
  starting transfers between devices  24.3 us (16%)
  other arithmetic  17.5 us (12%)
  local copies, waits for them, and re-layouts  15.9 us (11%)
  matrix products  13.9 us (9%)
    all_to_all x2, waiting for transfers between devices, gather_all(): moved = lax.all_to_all(spread, axis, 0, 0)  31.1 us
    pallas_call x2, Pallas kernels, attention_backward(): pl.pallas_call(kernel, grid=(groups,), in_specs=[pl.BlockSpec(memory_spac...  25.4 us
    all_to_all x2, starting transfers between devices, gather_all(): moved = lax.all_to_all(spread, axis, 0, 0)  15.5 us
    pallas_call x2, Pallas kernels, attention_forward(): pl.pallas_call(kernel, grid=(groups,), in_specs=[pl.BlockSpec(memory_spac...  14.8 us
    all_to_all x1, starting transfers between devices, reduce_all(): lax.all_to_all(terms.astype(jnp.bfloat16).reshape((count, rows) + terms.s...  7.21 us
    dot_general x2, matrix products, layer_parts(): jnp.dot(flat, key_weight, preferred_element_type=jnp.float32)  6.52 us
    all_to_all x1, waiting for transfers between devices, reduce_all(): lax.all_to_all(terms.astype(jnp.bfloat16).reshape((count, rows) + terms.s...  6.33 us
    broadcast_in_dim x2, other arithmetic, body(): return (fwd_out[None], grad_out[None])  5.07 us
  transfers between devices with their start and end apart: 5, of which 2 were waited for; matrix products, arithmetic and copies ran while one was open for 22% of the time, Pallas kernels for 27%

profile of v10, /device:TPU:6, one launch (start us, length us, event | category | flops | bytes accessed | tf_op | source)
XLA Modules:
  0.0 149.9 jit_solution(17935058475223230483)
XLA Ops:
  0.6 0.1 collective-permute-start
  0.7 1.5 %fusion.18 = f32[128]{0:T(128)S(1)} fusion(bf16[1,128,4096]{2,1,0:T(8,128)(2,1)} %param.10), kind=kLoop, calls=%fused_computation.24 | loop fusion | flops 1572736 | bytes 1049088 | tf_op jit(solution)/shard_map/reduce_sum | solution.py:40
  2.2 0.0 copy-start
  2.2 0.0 copy-start.1
  2.3 0.0 copy-start.6
  2.3 3.4 %fusion.31 = bf16[128,512]{1,0:T(8,128)(2,1)S(1)} fusion(bf16[1,4096,512]{2,1,0:T(8,128)(2,1)} %param.12, bf16[1,128,4096]{2,1,0:T(8,128)(2,1)} %param.10, f32[128]{0:T(128)S(1)} %get-tuple-element.45, f32[4096]{0:T(1024)} %bitcast.78), kind=kOutput, calls=%fused_computation.39 | convolution fusion | flops 539033600 | bytes 5390848 | tf_op jit(solution)/shard_map/dot_general | solution.py:182
  5.7 0.0 copy-done
  5.7 0.6 copy-done.1
  6.3 0.0 copy-done.6
  6.3 0.8 fusion.37
  7.2 1.6 %broadcast_in_dim.9 = bf16[8,128,1024]{2,1,0:T(8,128)(2,1)} broadcast(bf16[128,1024]{1,0:T(8,128)(2,1)S(1)} %pad_maximum_fusion.4), dimensions={1,2} | broadcast | bytes 2359296 | tf_op jit(solution)/shard_map/broadcast_in_dim | solution.py:26
  8.8 0.0 copy-start.7
  8.8 0.0 copy-start.8
  8.8 7.9 %all-to-all-start.1 = ((bf16[8,128,1024]{2,1,0:T(8,128)(2,1)}), bf16[8,128,1024]{2,1,0:T(8,128)(2,1)}, u32[]{:S(2)}, u32[]{:S(2)}) async-start(bf16[8,128,1024]{2,1,0:T(8,128)(2,1)} %broadcast_in_dim.9), calls=%async_computation.1 | async-start | bytes 4194304 | tf_op jit(solution)/shard_map/all_to_all | solution.py:27
  16.7 1.5 collective-permute-start.1
  18.2 0.0 copy-done.7
  18.2 0.1 dynamic-slice
  18.2 0.0 copy-done.8
  18.2 0.1 dynamic-slice.1
  18.3 0.1 dynamic_slice.12
  18.4 0.1 dynamic_slice.14
  18.5 0.1 iota_compare_fusion
  18.6 1.1 and_convert_fusion
  19.7 0.0 collective-permute-done
  19.7 0.3 fusion.15
  20.0 0.0 copy-start.2
  20.0 3.1 %fusion.28 = bf16[128,512]{1,0:T(8,128)(2,1)S(1)} fusion(bf16[1,4096,512]{2,1,0:T(8,128)(2,1)} %param.12, bf16[1,128,4096]{2,1,0:T(8,128)(2,1)S(1)} %collective-permute-done, f32[4096]{0:T(1024)S(1)} %bitcast.80, f32[128]{0:T(128)S(1)} %add_rsqrt_fusion.1), kind=kOutput, calls=%fused_computation.38 | convolution fusion | flops 539033600 | bytes 5390848 | tf_op jit(solution)/shard_map/dot_general | solution.py:182
  23.1 0.3 copy-done.2
  23.4 0.8 fusion.34
  24.3 31.1 %all-to-all-done.1 = bf16[8,128,1024]{2,1,0:T(8,128)(2,1)} async-done(((bf16[8,128,1024]{2,1,0:T(8,128)(2,1)}), bf16[8,128,1024]{2,1,0:T(8,128)(2,1)}, u32[]{:S(2)}, u32[]{:S(2)}) %all-to-all-start.1) | async-done | bytes 2097184 | tf_op jit(solution)/shard_map/all_to_all | solution.py:27
  55.4 1.6 %broadcast_in_dim.8 = bf16[8,128,1024]{2,1,0:T(8,128)(2,1)} broadcast(bf16[128,1024]{1,0:T(8,128)(2,1)S(1)} %pad_maximum_fusion.3), dimensions={1,2} | broadcast | bytes 2359296 | tf_op jit(solution)/shard_map/broadcast_in_dim | solution.py:26
  57.0 7.6 %all-to-all-start = ((bf16[8,128,1024]{2,1,0:T(8,128)(2,1)}), bf16[8,128,1024]{2,1,0:T(8,128)(2,1)}, u32[]{:S(2)}, u32[]{:S(2)}) async-start(bf16[8,128,1024]{2,1,0:T(8,128)(2,1)} %broadcast_in_dim.8), calls=%async_computation | async-start | bytes 4194304 | tf_op jit(solution)/shard_map/all_to_all | solution.py:27
  64.6 0.6 fusion.20
  65.2 1.0 fusion.60
  66.2 0.0 collective-permute-done.1
  66.3 2.3 %fusion.59 = (bf16[128,2048]{1,0:T(8,128)(2,1)}, bf16[128,2048]{1,0:T(8,128)(2,1)}) fusion(bf16[128,4096]{1,0:T(8,128)(2,1)} %bitcast.10), kind=kLoop, calls=%fused_computation.68 | loop fusion | bytes 2097152 | tf_op jit(solution)/shard_map/slice | solution.py:220
  68.6 2.9 %fusion.56 = (bf16[1024,256]{1,0:T(8,128)(2,1)}, bf16[1024,256]{1,0:T(8,128)(2,1)}, bf16[1024,256]{1,0:T(8,128)(2,1)}, bf16[1024,256]{1,0:T(8,128)(2,1)}) fusion(bf16[1024,1024]{1,0:T(8,128)(2,1)} %bitcast.9), kind=kLoop, calls=%fused_computation.65 | loop fusion | bytes 4194304 | tf_op jit(solution)/shard_map/slice | solution.py:219
  71.5 12.7 %shard_map.96 = (f32[128,2048]{1,0:T(8,128)}, f32[1024,256]{1,0:T(8,128)}, f32[1024,256]{1,0:T(8,128)}) custom-call(s32[1]{0:T(128)} %bitcast.start_ref, s32[128,640]{1,0:T(8,128)} %get-tuple-element.40.mask_ref, bf16[128,2048]{1,0:T(8,128)(2,1)} %get-tuple-element.34.query_ref, bf16[1024,256]{1,0:T(8,128)(2,1)} %get-tuple-element.25.key_ref, ...), custom_call_target="tpu_custom_call" | custom-call | tf_op jit(solution)/shard_map/pallas_call | solution.py:136
  84.2 12.7 %shard_map.95 = (f32[128,2048]{1,0:T(8,128)}, f32[1024,256]{1,0:T(8,128)}, f32[1024,256]{1,0:T(8,128)}) custom-call(s32[1]{0:T(128)} %bitcast.start_ref, s32[128,640]{1,0:T(8,128)} %get-tuple-element.40.mask_ref, bf16[128,2048]{1,0:T(8,128)(2,1)} %get-tuple-element.35.query_ref, bf16[1024,256]{1,0:T(8,128)(2,1)} %get-tuple-element.27.key_ref, ...), custom_call_target="tpu_custom_call" | custom-call | tf_op jit(solution)/shard_map/pallas_call | solution.py:136
  96.9 3.7 %pad_maximum_fusion = (bf16[1024,512]{1,0:T(8,128)(2,1)}, bf16[1024,512]{1,0:T(8,128)(2,1)}) fusion(f32[1024,256]{1,0:T(8,128)} %get-tuple-element.12, f32[1024,256]{1,0:T(8,128)} %get-tuple-element.11, f32[1024,256]{1,0:T(8,128)} %get-tuple-element.14, f32[1024,256]{1,0:T(8,128)} %get-tuple-element.13), kind=kLoop, calls=%fused_computation.34 | loop fusion | flops 4194304 | bytes 6291456 | tf_op jit(solution)/shard_map/concatenate | solution.py:224
  100.6 0.0 all-to-all-done
  100.6 3.1 %pad_maximum_fusion.2 = bf16[8,128,1024]{2,1,0:T(8,128)(2,1)} fusion(bf16[8,128,512]{2,1,0:T(8,128)(2,1)} %bitcast.77, bf16[8,128,512]{2,1,0:T(8,128)(2,1)} %bitcast.76), kind=kLoop, calls=%fused_computation.36 | loop fusion | flops 4194304 | bytes 4194304 | tf_op jit(solution)/shard_map/concatenate | solution.py:230
  103.7 7.2 %all-to-all-start.2 = ((bf16[8,128,1024]{2,1,0:T(8,128)(2,1)}), bf16[8,128,1024]{2,1,0:T(8,128)(2,1)}, u32[]{:S(2)}, u32[]{:S(2)}) async-start(bf16[8,128,1024]{2,1,0:T(8,128)(2,1)} %pad_maximum_fusion.2), calls=%async_computation.2 | async-start | bytes 4194304 | tf_op jit(solution)/shard_map/all_to_all | solution.py:34
  110.9 1.1 fusion.58
  112.0 1.1 fusion.57
  113.1 2.9 %fusion.55 = (bf16[1024,256]{1,0:T(8,128)(2,1)}, bf16[1024,256]{1,0:T(8,128)(2,1)}, bf16[1024,256]{1,0:T(8,128)(2,1)}, bf16[1024,256]{1,0:T(8,128)(2,1)}) fusion(bf16[1024,1024]{1,0:T(8,128)(2,1)} %bitcast.6), kind=kLoop, calls=%fused_computation.64 | loop fusion | bytes 4194304 | tf_op jit(solution)/shard_map/slice | solution.py:248
  116.0 7.4 %shard_map.97 = bf16[128,2048]{1,0:T(8,128)(2,1)} custom-call(s32[1]{0:T(128)} %bitcast.start_ref, s32[128,640]{1,0:T(8,128)} %get-tuple-element.41.mask_ref, bf16[128,2048]{1,0:T(8,128)(2,1)} %get-tuple-element.30.query_ref, bf16[1024,256]{1,0:T(8,128)(2,1)} %get-tuple-element.23.key_ref, bf16[1024,256]{1,0:T(8,128)(2,1)} %get-tuple-element.20.value_ref, ...), custom_call_target="tpu_custom_call" | custom-call | tf_op jit(solution)/shard_map/pallas_call | solution.py:112
  123.3 0.0 copy-start.4
  123.3 7.4 %shard_map.98 = bf16[128,2048]{1,0:T(8,128)(2,1)} custom-call(s32[1]{0:T(128)} %bitcast.start_ref, s32[128,640]{1,0:T(8,128)} %get-tuple-element.41.mask_ref, bf16[128,2048]{1,0:T(8,128)(2,1)} %get-tuple-element.31.query_ref, bf16[1024,256]{1,0:T(8,128)(2,1)} %get-tuple-element.22.key_ref, bf16[1024,256]{1,0:T(8,128)(2,1)} %get-tuple-element.21.value_ref, ...), custom_call_target="tpu_custom_call" | custom-call | tf_op jit(solution)/shard_map/pallas_call | solution.py:112
  130.8 0.0 copy-done.4
  130.8 0.0 copy-start.5
  130.8 2.2 %maximum_bitcast_fusion = bf16[1,128,4096]{2,1,0:T(8,128)(2,1)} fusion(bf16[128,2048]{1,0:T(8,128)(2,1)} %shard_map.98, bf16[128,2048]{1,0:T(8,128)(2,1)S(1)} %copy-done.4), kind=kLoop, calls=%fused_computation.45 | loop fusion | flops 2097152 | bytes 2097152 | tf_op jit(solution)/shard_map/broadcast_in_dim | solution.py:268
  132.9 6.3 %all-to-all-done.2 = bf16[8,128,1024]{2,1,0:T(8,128)(2,1)} async-done(((bf16[8,128,1024]{2,1,0:T(8,128)(2,1)}), bf16[8,128,1024]{2,1,0:T(8,128)(2,1)}, u32[]{:S(2)}, u32[]{:S(2)}) %all-to-all-start.2) | async-done | bytes 2097184 | tf_op jit(solution)/shard_map/all_to_all | solution.py:34
  139.3 2.0 %reduce_sum.41 = bf16[128,1024]{1,0:T(8,128)(2,1)S(1)} reduce(bf16[8,128,1024]{2,1,0:T(8,128)(2,1)} %all-to-all-done.2, bf16[]{:T(256)} %constant.25.clone.1), dimensions={0}, to_apply=%region_2.0 | reduce | flops 917504 | bytes 2359298 | tf_op jit(solution)/shard_map/reduce_sum | solution.py:35
  141.3 0.0 copy-done.5
  141.3 0.0 copy-start.3
  141.3 4.1 %convolution_add_fusion.1 = f32[128,4096]{1,0:T(8,128)S(1)} fusion(bf16[1,4096,512]{2,1,0:T(8,128)(2,1)} %param.12, f32[128,2048]{1,0:T(8,128)S(1)} %copy-done.5, f32[128,2048]{1,0:T(8,128)} %get-tuple-element.16, bf16[128,256]{1,0:T(8,128)(2,1)S(1)} %get-tuple-element.38, bf16[128,256]{1,0:T(8,128)(2,1)S(1)} %get-tuple-element.39), kind=kOutput, calls=%fused_computation.2 | convolution fusion | flops 538181632 | bytes 8519680 | tf_op jit(solution)/shard_map/dot_general | solution.py:255
  145.4 0.0 copy-done.3
  145.4 1.6 %fusion.25 = (f32[128]{0:T(128)S(1)}, f32[128,4096]{1,0:T(8,128)S(1)}) fusion(bf16[1,128,4096]{2,1,0:T(8,128)(2,1)S(1)} %copy-done, f32[128,4096]{1,0:T(8,128)S(1)} %convolution_add_fusion.1, bf16[1,4096,512]{2,1,0:T(8,128)(2,1)S(1)} %copy-done.3, bf16[128,256]{1,0:T(8,128)(2,1)S(1)} %get-tuple-element.37, bf16[128,256]{1,0:T(8,128)(2,1)S(1)} %get-tuple-element.36, ...), kind=kOutput, calls=%fused_computation.31 | convolution fusion | flops 539754368 | bytes 9585152 | tf_op jit(solution)/shard_map/dot_general | solution.py:258
  147.0 2.9 %fusion.42 = bf16[1,128,4096]{2,1,0:T(8,128)(2,1)} fusion(bf16[1,128,4096]{2,1,0:T(8,128)(2,1)S(1)} %copy-done, f32[128,4096]{1,0:T(8,128)S(1)} %get-tuple-element.47, f32[128]{0:T(128)S(1)} %broadcast_multiply_fusion, f32[128]{0:T(128)S(1)} %get-tuple-element.44, f32[128]{0:T(128)S(1)} %get-tuple-element.45, bf16[1,128,4096]{2,1,0:T(8,128)(2,1)} %collective-permute-done.1), kind=kLoop, calls=%fused_computation.44 | loop fusion | flops 4194304 | bytes 5244416 | tf_op jit(solution)/shard_map/broadcast_in_dim | solution.py:268
  (7 shorter events, 0.1 us)
Async XLA Ops:
  0.6 19.1 %collective-permute-start = (bf16[1,128,4096]{2,1,0:T(8,128)(2,1)}, bf16[1,128,4096]{2,1,0:T(8,128)(2,1)S(1)}, u32[]{:S(2)}, u32[]{:S(2)}) collective-permute-start(bf16[1,128,4096]{2,1,0:T(8,128)(2,1)} %param.8), channel_id=1, source_target_pairs={{120,0},{0,8},{8,16},{16,24},{24,32},{32,40},{40,48},{48,56},{56,6... | collective-permute-start | bytes 3145736 | tf_op jit(solution)/shard_map/ppermute | solution.py:21
  2.2 3.5 %copy-start = (bf16[1,128,4096]{2,1,0:T(8,128)(2,1)S(1)}, bf16[1,128,4096]{2,1,0:T(8,128)(2,1)}, u32[]{:S(2)}) copy-start(bf16[1,128,4096]{2,1,0:T(8,128)(2,1)} %param.10) | copy-start | bytes 3145732
  2.2 4.1 %copy-start.1 = (bf16[1,4096,512]{2,1,0:T(8,128)(2,1)S(1)}, bf16[1,4096,512]{2,1,0:T(8,128)(2,1)}, u32[]{:S(2)}) copy-start(bf16[1,4096,512]{2,1,0:T(8,128)(2,1)} %param.13) | copy-start | bytes 12582916
  2.3 4.1 %copy-start.6 = (f32[1,4096]{1,0:T(1,128)S(1)}, f32[1,4096]{1,0:T(1,128)}, u32[]{:S(2)}) copy-start(f32[1,4096]{1,0:T(1,128)} %param.11) | copy-start | bytes 49156
  8.8 9.4 %copy-start.7 = (s32[1024]{0:T(1024)S(1)}, s32[1024]{0:T(1024)}, u32[]{:S(2)}) copy-start(s32[1024]{0:T(1024)} %param.14) | copy-start | bytes 12292
  8.8 9.4 %copy-start.8 = (s32[1024]{0:T(1024)S(1)}, s32[1024]{0:T(1024)}, u32[]{:S(2)}) copy-start(s32[1024]{0:T(1024)} %param.15) | copy-start | bytes 12292
  8.8 46.6 %all-to-all-start.1 = ((bf16[8,128,1024]{2,1,0:T(8,128)(2,1)}), bf16[8,128,1024]{2,1,0:T(8,128)(2,1)}, u32[]{:S(2)}, u32[]{:S(2)}) async-start(bf16[8,128,1024]{2,1,0:T(8,128)(2,1)} %broadcast_in_dim.9), calls=%async_computation.1 | async-start | bytes 4194304 | tf_op jit(solution)/shard_map/all_to_all | solution.py:27
  16.7 49.5 %collective-permute-start.1 = (bf16[1,128,4096]{2,1,0:T(8,128)(2,1)}, bf16[1,128,4096]{2,1,0:T(8,128)(2,1)}, u32[]{:S(2)}, u32[]{:S(2)}) collective-permute-start(bf16[1,128,4096]{2,1,0:T(8,128)(2,1)} %param.9), channel_id=1, source_target_pairs={{8,0},{16,8},{24,16},{32,24},{40,32},{48,40},{56,48},{64,56},{72,6... | collective-permute-start | bytes 3145736 | tf_op jit(solution)/shard_map/ppermute | solution.py:21
  20.0 3.5 %copy-start.2 = (bf16[1,4096,512]{2,1,0:T(8,128)(2,1)S(1)}, bf16[1,4096,512]{2,1,0:T(8,128)(2,1)}, u32[]{:S(2)}) copy-start(bf16[1,4096,512]{2,1,0:T(8,128)(2,1)} %param.13) | copy-start | bytes 12582916
  57.0 43.6 %all-to-all-start = ((bf16[8,128,1024]{2,1,0:T(8,128)(2,1)}), bf16[8,128,1024]{2,1,0:T(8,128)(2,1)}, u32[]{:S(2)}, u32[]{:S(2)}) async-start(bf16[8,128,1024]{2,1,0:T(8,128)(2,1)} %broadcast_in_dim.8), calls=%async_computation | async-start | bytes 4194304 | tf_op jit(solution)/shard_map/all_to_all | solution.py:27
  103.7 35.6 %all-to-all-start.2 = ((bf16[8,128,1024]{2,1,0:T(8,128)(2,1)}), bf16[8,128,1024]{2,1,0:T(8,128)(2,1)}, u32[]{:S(2)}, u32[]{:S(2)}) async-start(bf16[8,128,1024]{2,1,0:T(8,128)(2,1)} %pad_maximum_fusion.2), calls=%async_computation.2 | async-start | bytes 4194304 | tf_op jit(solution)/shard_map/all_to_all | solution.py:34
  123.3 7.4 %copy-start.4 = (bf16[128,2048]{1,0:T(8,128)(2,1)S(1)}, bf16[128,2048]{1,0:T(8,128)(2,1)}, u32[]{:S(2)}) copy-start(bf16[128,2048]{1,0:T(8,128)(2,1)} %shard_map.97) | copy-start | bytes 1572868
  130.8 10.5 %copy-start.5 = (f32[128,2048]{1,0:T(8,128)S(1)}, f32[128,2048]{1,0:T(8,128)}, u32[]{:S(2)}) copy-start(f32[128,2048]{1,0:T(8,128)} %get-tuple-element.17) | copy-start | bytes 3145732
  141.3 4.1 %copy-start.3 = (bf16[1,4096,512]{2,1,0:T(8,128)(2,1)S(1)}, bf16[1,4096,512]{2,1,0:T(8,128)(2,1)}, u32[]{:S(2)}) copy-start(bf16[1,4096,512]{2,1,0:T(8,128)(2,1)} %param.13) | copy-start | bytes 12582916

commit v11 on v9

--- a/solution.py
+++ b/solution.py
@@ -204,6 +204,7 @@
     allowed = lax.dynamic_slice_in_dim(allowed_of(seg_bwd).astype(jnp.int32), window_start, window, axis=1)
     start_row = window_start.reshape(1).astype(jnp.int32)
     halves = 2
+    fwd_halves = 1
     half_kv = kv_width // halves
     half_q = width // halves
     dquery_parts, dkey_parts, dvalue_parts = ([], [], [])
@@ -236,9 +237,11 @@
     dkeys = jnp.concatenate(dkey_parts, axis=1)
     dvalues = jnp.concatenate(dvalue_parts, axis=1)
     fwd_parts = []
-    for half in range(halves):
-        kv_cols = slice(half * half_kv, (half + 1) * half_kv)
-        q_cols = slice(half * half_q, (half + 1) * half_q)
+    fwd_kv = kv_width // fwd_halves
+    fwd_q = width // fwd_halves
+    for half in range(fwd_halves):
+        kv_cols = slice(half * fwd_kv, (half + 1) * fwd_kv)
+        q_cols = slice(half * fwd_q, (half + 1) * fwd_q)
         fwd_parts.append(
             attention_forward(
                 start_row,

time: 151 us -> 145 us (0.960)
  other arithmetic: 17.5 us -> 10.6 us
  waiting for transfers between devices: 37.2 us -> 43.3 us
  local copies, waits for them, and re-layouts: 15.9 us -> 12.8 us
  Pallas kernels: 40.7 us -> 38.6 us
    all_to_all x1, waiting for transfers between devices: 6.11 us -> 12.2 us  [reduce_all(): lax.all_to_all(terms.astype(jnp.bfloat16).reshape((count, rows) + terms.s...]
    broadcast_in_dim x2 -> x1, other arithmetic: 5.07 us -> 1.66 us  [body(): return (fwd_out[None], grad_out[None])]
    pallas_call x2 -> x1, Pallas kernels: 15 us -> 12.9 us  [attention_forward(): pl.pallas_call(kernel, grid=(groups,), in_specs=[pl.BlockSpec(memory_spac...]
    slice x3 -> x1, local copies, waits for them, and re-layouts: 5.05 us -> 3.07 us  [body(): value_piece = fwd_all[:, kv_width:]]
    reduce_sum x1, other arithmetic: 1.97 us -> 0.36 us  [reduce_all(): return jnp.sum(moved.astype(jnp.float32), axis=0)]
  transfers between devices with their start and end apart: 5 -> 5, of which waited for: 2 -> 2; matrix products, arithmetic and copies ran while one was open for 22% -> 19% of each run, Pallas kernels for 27% -> 27%
where the time goes in v11:
time: 145 us
  waiting for transfers between devices  43.3 us (30%)
  Pallas kernels  38.6 us (27%)
  starting transfers between devices  24.3 us (17%)
  matrix products  14.1 us (10%)
  local copies, waits for them, and re-layouts  12.8 us (9%)
  other arithmetic  10.6 us (7%)
    all_to_all x2, waiting for transfers between devices, gather_all(): moved = lax.all_to_all(spread, axis, 0, 0)  31.1 us
    pallas_call x2, Pallas kernels, attention_backward(): pl.pallas_call(kernel, grid=(groups,), in_specs=[pl.BlockSpec(memory_spac...  25.7 us
    all_to_all x2, starting transfers between devices, gather_all(): moved = lax.all_to_all(spread, axis, 0, 0)  15.5 us
    pallas_call x1, Pallas kernels, attention_forward(): pl.pallas_call(kernel, grid=(groups,), in_specs=[pl.BlockSpec(memory_spac...  12.9 us
    all_to_all x1, waiting for transfers between devices, reduce_all(): lax.all_to_all(terms.astype(jnp.bfloat16).reshape((count, rows) + terms.s...  12.2 us
    all_to_all x1, starting transfers between devices, reduce_all(): lax.all_to_all(terms.astype(jnp.bfloat16).reshape((count, rows) + terms.s...  7.22 us
    dot_general x2, matrix products, layer_parts(): jnp.dot(flat, key_weight, preferred_element_type=jnp.float32)  6.52 us
    dot_general x1, matrix products, body(): jnp.dot(dkeys, jnp.transpose(key_weight), preferred_element_type=jnp.floa...  4.43 us
  transfers between devices with their start and end apart: 5, of which 2 were waited for; matrix products, arithmetic and copies ran while one was open for 19% of the time, Pallas kernels for 27%

profile of v11, /device:TPU:6, one launch (start us, length us, event | category | flops | bytes accessed | tf_op | source)
XLA Modules:
  0.0 144.6 jit_solution(12712695743924357163)
XLA Ops:
  0.6 0.1 collective-permute-start
  0.7 1.5 %fusion.18 = f32[128]{0:T(128)S(1)} fusion(bf16[1,128,4096]{2,1,0:T(8,128)(2,1)} %param.10), kind=kLoop, calls=%fused_computation.24 | loop fusion | flops 1572736 | bytes 1049088 | tf_op jit(solution)/shard_map/reduce_sum | solution.py:40
  2.2 0.0 copy-start
  2.2 0.0 copy-start.2
  2.3 0.0 copy-start.7
  2.3 3.4 %fusion.31 = bf16[128,512]{1,0:T(8,128)(2,1)S(1)} fusion(bf16[1,4096,512]{2,1,0:T(8,128)(2,1)} %param.12, bf16[1,128,4096]{2,1,0:T(8,128)(2,1)} %param.10, f32[128]{0:T(128)S(1)} %get-tuple-element.39, f32[4096]{0:T(1024)} %bitcast.79), kind=kOutput, calls=%fused_computation.39 | convolution fusion | flops 539033600 | bytes 5390848 | tf_op jit(solution)/shard_map/dot_general | solution.py:182
  5.7 0.0 copy-done
  5.7 0.6 copy-done.2
  6.3 0.0 copy-done.7
  6.3 0.8 fusion.37
  7.2 1.6 %broadcast_in_dim.9 = bf16[8,128,1024]{2,1,0:T(8,128)(2,1)} broadcast(bf16[128,1024]{1,0:T(8,128)(2,1)S(1)} %pad_maximum_fusion.4), dimensions={1,2} | broadcast | bytes 2359296 | tf_op jit(solution)/shard_map/broadcast_in_dim | solution.py:26
  8.8 0.0 copy-start.8
  8.8 0.0 copy-start.9
  8.8 7.9 %all-to-all-start.1 = ((bf16[8,128,1024]{2,1,0:T(8,128)(2,1)}), bf16[8,128,1024]{2,1,0:T(8,128)(2,1)}, u32[]{:S(2)}, u32[]{:S(2)}) async-start(bf16[8,128,1024]{2,1,0:T(8,128)(2,1)} %broadcast_in_dim.9), calls=%async_computation.1 | async-start | bytes 4194304 | tf_op jit(solution)/shard_map/all_to_all | solution.py:27
  16.7 1.5 %collective-permute-start.1 = (bf16[1,128,4096]{2,1,0:T(8,128)(2,1)}, bf16[1,128,4096]{2,1,0:T(8,128)(2,1)S(1)}, u32[]{:S(2)}, u32[]{:S(2)}) collective-permute-start(bf16[1,128,4096]{2,1,0:T(8,128)(2,1)} %param.9), channel_id=1, source_target_pairs={{8,0},{16,8},{24,16},{32,24},{40,32},{48,40},{56,48},{64,56},{72,6... | collective-permute-start | bytes 3145736 | tf_op jit(solution)/shard_map/ppermute | solution.py:21
  18.2 0.0 copy-done.8
  18.2 0.1 dynamic-slice
  18.2 0.0 copy-done.9
  18.2 0.1 dynamic-slice.1
  18.3 0.1 dynamic_slice.12
  18.4 0.1 dynamic_slice.14
  18.5 0.1 iota_compare_fusion
  18.6 1.0 and_convert_fusion
  19.6 0.0 collective-permute-done
  19.6 0.0 copy-start.1
  19.6 0.3 fusion.15
  19.9 0.0 copy-start.3
  20.0 3.1 %fusion.28 = bf16[128,512]{1,0:T(8,128)(2,1)S(1)} fusion(bf16[1,4096,512]{2,1,0:T(8,128)(2,1)} %param.12, bf16[1,128,4096]{2,1,0:T(8,128)(2,1)S(1)} %collective-permute-done, f32[4096]{0:T(1024)S(1)} %bitcast.81, f32[128]{0:T(128)S(1)} %add_rsqrt_fusion.1), kind=kOutput, calls=%fused_computation.38 | convolution fusion | flops 539033600 | bytes 5390848 | tf_op jit(solution)/shard_map/dot_general | solution.py:182
  23.1 0.4 copy-done.3
  23.5 0.8 fusion.34
  24.3 31.1 %all-to-all-done.1 = bf16[8,128,1024]{2,1,0:T(8,128)(2,1)} async-done(((bf16[8,128,1024]{2,1,0:T(8,128)(2,1)}), bf16[8,128,1024]{2,1,0:T(8,128)(2,1)}, u32[]{:S(2)}, u32[]{:S(2)}) %all-to-all-start.1) | async-done | bytes 2097184 | tf_op jit(solution)/shard_map/all_to_all | solution.py:27
  55.4 1.6 %broadcast_in_dim.8 = bf16[8,128,1024]{2,1,0:T(8,128)(2,1)} broadcast(bf16[128,1024]{1,0:T(8,128)(2,1)S(1)} %pad_maximum_fusion.3), dimensions={1,2} | broadcast | bytes 2359296 | tf_op jit(solution)/shard_map/broadcast_in_dim | solution.py:26
  57.0 7.6 %all-to-all-start = ((bf16[8,128,1024]{2,1,0:T(8,128)(2,1)}), bf16[8,128,1024]{2,1,0:T(8,128)(2,1)}, u32[]{:S(2)}, u32[]{:S(2)}) async-start(bf16[8,128,1024]{2,1,0:T(8,128)(2,1)} %broadcast_in_dim.8), calls=%async_computation | async-start | bytes 4194304 | tf_op jit(solution)/shard_map/all_to_all | solution.py:27
  64.6 0.0 copy-done.1
  64.6 1.6 %fusion.20 = (bf16[128,4096]{1,0:T(8,128)(2,1)S(1)}, bf16[128,4096]{1,0:T(8,128)(2,1)}) fusion(bf16[1,128,4096]{2,1,0:T(8,128)(2,1)S(1)} %copy-done, f32[128]{0:T(128)S(1)} %get-tuple-element.39, f32[4096]{0:T(1024)S(1)} %bitcast.83, f32[128]{0:T(128)S(1)} %add_rsqrt_fusion.1, bf16[1,128,4096]{2,1,0:T(8,128)(2,1)S(1)} %collective-permute-done), kind=kLoop, calls=%fused_computation.26 | loop fusion | flops 4194304 | bytes 4211712 | tf_op jit(solution)/shard_map/convert_element_type | solution.py:181
  66.2 1.1 fusion.58
  67.3 0.0 collective-permute-done.1
  67.3 0.0 copy-start.5
  67.3 1.1 fusion.57
  68.4 2.9 %fusion.56 = (bf16[1024,256]{1,0:T(8,128)(2,1)}, bf16[1024,256]{1,0:T(8,128)(2,1)}, bf16[1024,256]{1,0:T(8,128)(2,1)}, bf16[1024,256]{1,0:T(8,128)(2,1)}) fusion(bf16[1024,1024]{1,0:T(8,128)(2,1)} %bitcast.9), kind=kLoop, calls=%fused_computation.64 | loop fusion | bytes 4194304 | tf_op jit(solution)/shard_map/slice | solution.py:220
  71.3 0.0 copy-done.5
  71.3 12.8 %shard_map.96 = (f32[128,2048]{1,0:T(8,128)}, f32[1024,256]{1,0:T(8,128)}, f32[1024,256]{1,0:T(8,128)}) custom-call(s32[1]{0:T(128)} %bitcast.start_ref, s32[128,640]{1,0:T(8,128)} %get-tuple-element.34.mask_ref, bf16[128,2048]{1,0:T(8,128)(2,1)} %get-tuple-element.28.query_ref, bf16[1024,256]{1,0:T(8,128)(2,1)} %get-tuple-element.23.key_ref, ...), custom_call_target="tpu_custom_call" | custom-call | tf_op jit(solution)/shard_map/pallas_call | solution.py:136
  84.1 12.9 %shard_map.95 = (f32[128,2048]{1,0:T(8,128)}, f32[1024,256]{1,0:T(8,128)}, f32[1024,256]{1,0:T(8,128)}) custom-call(s32[1]{0:T(128)} %bitcast.start_ref, s32[128,640]{1,0:T(8,128)} %get-tuple-element.34.mask_ref, bf16[128,2048]{1,0:T(8,128)(2,1)} %get-tuple-element.29.query_ref, bf16[1024,256]{1,0:T(8,128)(2,1)} %get-tuple-element.25.key_ref, ...), custom_call_target="tpu_custom_call" | custom-call | tf_op jit(solution)/shard_map/pallas_call | solution.py:136
  97.0 2.4 %pad_maximum_fusion = (bf16[1024,512]{1,0:T(8,128)(2,1)S(1)}, bf16[1024,512]{1,0:T(8,128)(2,1)S(1)}) fusion(f32[1024,256]{1,0:T(8,128)} %get-tuple-element.12, f32[1024,256]{1,0:T(8,128)} %get-tuple-element.11, f32[1024,256]{1,0:T(8,128)} %get-tuple-element.14, f32[1024,256]{1,0:T(8,128)} %get-tuple-element.13), kind=kLoop, calls=%fused_computation.34 | loop fusion | flops 4194304 | bytes 6291456 | tf_op jit(solution)/shard_map/concatenate | solution.py:225
  99.4 0.0 all-to-all-done
  99.4 1.6 %pad_maximum_fusion.2 = bf16[8,128,1024]{2,1,0:T(8,128)(2,1)} fusion(bf16[8,128,512]{2,1,0:T(8,128)(2,1)S(1)} %bitcast.77, bf16[8,128,512]{2,1,0:T(8,128)(2,1)S(1)} %bitcast.76), kind=kLoop, calls=%fused_computation.36 | loop fusion | flops 4194304 | bytes 4194304 | tf_op jit(solution)/shard_map/concatenate | solution.py:231
  101.0 7.2 %all-to-all-start.2 = ((bf16[8,128,1024]{2,1,0:T(8,128)(2,1)}), bf16[8,128,1024]{2,1,0:T(8,128)(2,1)S(1)}, u32[]{:S(2)}, u32[]{:S(2)}) async-start(bf16[8,128,1024]{2,1,0:T(8,128)(2,1)} %pad_maximum_fusion.2), calls=%async_computation.2 | async-start | bytes 4194304 | tf_op jit(solution)/shard_map/all_to_all | solution.py:34
  108.3 3.1 %fusion.55 = (bf16[1024,512]{1,0:T(8,128)(2,1)}, bf16[1024,512]{1,0:T(8,128)(2,1)}) fusion(bf16[1024,1024]{1,0:T(8,128)(2,1)} %bitcast.6), kind=kLoop, calls=%fused_computation.63 | loop fusion | bytes 4194304 | tf_op jit(solution)/shard_map/slice | solution.py:229
  111.3 12.9 %shard_map.97 = bf16[128,4096]{1,0:T(8,128)(2,1)} custom-call(s32[1]{0:T(128)} %bitcast.start_ref, s32[128,640]{1,0:T(8,128)} %get-tuple-element.35.mask_ref, bf16[128,4096]{1,0:T(8,128)(2,1)} %get-tuple-element.37.query_ref, bf16[1024,512]{1,0:T(8,128)(2,1)} %get-tuple-element.21.key_ref, bf16[1024,512]{1,0:T(8,128)(2,1)} %get-tuple-element.20.value_ref, ...), custom_call_target="tpu_custom_call" | custom-call | tf_op jit(solution)/shard_map/pallas_call | solution.py:112
  124.3 12.2 %all-to-all-done.2 = bf16[8,128,1024]{2,1,0:T(8,128)(2,1)S(1)} async-done(((bf16[8,128,1024]{2,1,0:T(8,128)(2,1)}), bf16[8,128,1024]{2,1,0:T(8,128)(2,1)S(1)}, u32[]{:S(2)}, u32[]{:S(2)}) %all-to-all-start.2) | async-done | bytes 2097184 | tf_op jit(solution)/shard_map/all_to_all | solution.py:34
  136.5 0.4 reduce_sum.41
  136.9 0.0 copy-start.4
  136.9 4.4 %convolution_add_fusion.1 = f32[128,4096]{1,0:T(8,128)S(1)} fusion(bf16[1,4096,512]{2,1,0:T(8,128)(2,1)} %param.12, f32[128,2048]{1,0:T(8,128)} %get-tuple-element.17, f32[128,2048]{1,0:T(8,128)} %get-tuple-element.16, bf16[128,256]{1,0:T(8,128)(2,1)S(1)} %get-tuple-element.32, bf16[128,256]{1,0:T(8,128)(2,1)S(1)} %get-tuple-element.33), kind=kOutput, calls=%fused_computation.2 | convolution fusion | flops 538181632 | bytes 8519680 | tf_op jit(solution)/shard_map/dot_general | solution.py:258
  141.3 0.0 copy-done.4
  141.4 0.0 copy-start.6
  141.4 1.6 %fusion.25 = (f32[128]{0:T(128)S(1)}, f32[128,4096]{1,0:T(8,128)S(1)}) fusion(bf16[1,128,4096]{2,1,0:T(8,128)(2,1)S(1)} %copy-done, f32[128,4096]{1,0:T(8,128)S(1)} %convolution_add_fusion.1, bf16[1,4096,512]{2,1,0:T(8,128)(2,1)S(1)} %copy-done.4, bf16[128,256]{1,0:T(8,128)(2,1)S(1)} %get-tuple-element.31, bf16[128,256]{1,0:T(8,128)(2,1)S(1)} %get-tuple-element.30, ...), kind=kOutput, calls=%fused_computation.31 | convolution fusion | flops 539754368 | bytes 9585152 | tf_op jit(solution)/shard_map/dot_general | solution.py:261
  143.0 0.0 copy-done.6
  143.0 1.7 %fusion.42 = bf16[1,128,4096]{2,1,0:T(8,128)(2,1)} fusion(bf16[1,128,4096]{2,1,0:T(8,128)(2,1)S(1)} %copy-done, f32[128,4096]{1,0:T(8,128)S(1)} %get-tuple-element.41, f32[128]{0:T(128)S(1)} %broadcast_multiply_fusion, f32[128]{0:T(128)S(1)} %get-tuple-element.38, f32[128]{0:T(128)S(1)} %get-tuple-element.39, bf16[1,128,4096]{2,1,0:T(8,128)(2,1)S(1)} %copy-done.6), kind=kLoop, calls=%fused_computation.44 | loop fusion | flops 4194304 | bytes 5244416 | tf_op jit(solution)/shard_map/broadcast_in_dim | solution.py:271
  (7 shorter events, 0.1 us)
Async XLA Ops:
  0.6 19.0 %collective-permute-start = (bf16[1,128,4096]{2,1,0:T(8,128)(2,1)}, bf16[1,128,4096]{2,1,0:T(8,128)(2,1)S(1)}, u32[]{:S(2)}, u32[]{:S(2)}) collective-permute-start(bf16[1,128,4096]{2,1,0:T(8,128)(2,1)} %param.8), channel_id=1, source_target_pairs={{120,0},{0,8},{8,16},{16,24},{24,32},{32,40},{40,48},{48,56},{56,6... | collective-permute-start | bytes 3145736 | tf_op jit(solution)/shard_map/ppermute | solution.py:21
  2.2 3.5 %copy-start = (bf16[1,128,4096]{2,1,0:T(8,128)(2,1)S(1)}, bf16[1,128,4096]{2,1,0:T(8,128)(2,1)}, u32[]{:S(2)}) copy-start(bf16[1,128,4096]{2,1,0:T(8,128)(2,1)} %param.10) | copy-start | bytes 3145732
  2.2 4.1 %copy-start.2 = (bf16[1,4096,512]{2,1,0:T(8,128)(2,1)S(1)}, bf16[1,4096,512]{2,1,0:T(8,128)(2,1)}, u32[]{:S(2)}) copy-start(bf16[1,4096,512]{2,1,0:T(8,128)(2,1)} %param.13) | copy-start | bytes 12582916
  2.3 4.1 %copy-start.7 = (f32[1,4096]{1,0:T(1,128)S(1)}, f32[1,4096]{1,0:T(1,128)}, u32[]{:S(2)}) copy-start(f32[1,4096]{1,0:T(1,128)} %param.11) | copy-start | bytes 49156
  8.8 9.4 %copy-start.8 = (s32[1024]{0:T(1024)S(1)}, s32[1024]{0:T(1024)}, u32[]{:S(2)}) copy-start(s32[1024]{0:T(1024)} %param.14) | copy-start | bytes 12292
  8.8 9.4 %copy-start.9 = (s32[1024]{0:T(1024)S(1)}, s32[1024]{0:T(1024)}, u32[]{:S(2)}) copy-start(s32[1024]{0:T(1024)} %param.15) | copy-start | bytes 12292
  8.8 46.6 %all-to-all-start.1 = ((bf16[8,128,1024]{2,1,0:T(8,128)(2,1)}), bf16[8,128,1024]{2,1,0:T(8,128)(2,1)}, u32[]{:S(2)}, u32[]{:S(2)}) async-start(bf16[8,128,1024]{2,1,0:T(8,128)(2,1)} %broadcast_in_dim.9), calls=%async_computation.1 | async-start | bytes 4194304 | tf_op jit(solution)/shard_map/all_to_all | solution.py:27
  16.7 50.6 %collective-permute-start.1 = (bf16[1,128,4096]{2,1,0:T(8,128)(2,1)}, bf16[1,128,4096]{2,1,0:T(8,128)(2,1)S(1)}, u32[]{:S(2)}, u32[]{:S(2)}) collective-permute-start(bf16[1,128,4096]{2,1,0:T(8,128)(2,1)} %param.9), channel_id=1, source_target_pairs={{8,0},{16,8},{24,16},{32,24},{40,32},{48,40},{56,48},{64,56},{72,6... | collective-permute-start | bytes 3145736 | tf_op jit(solution)/shard_map/ppermute | solution.py:21
  19.6 45.0 %copy-start.1 = (bf16[1,128,4096]{2,1,0:T(8,128)(2,1)}, bf16[1,128,4096]{2,1,0:T(8,128)(2,1)S(1)}, u32[]{:S(2)}) copy-start(bf16[1,128,4096]{2,1,0:T(8,128)(2,1)S(1)} %collective-permute-done) | copy-start | bytes 3145732
  19.9 3.5 %copy-start.3 = (bf16[1,4096,512]{2,1,0:T(8,128)(2,1)S(1)}, bf16[1,4096,512]{2,1,0:T(8,128)(2,1)}, u32[]{:S(2)}) copy-start(bf16[1,4096,512]{2,1,0:T(8,128)(2,1)} %param.13) | copy-start | bytes 12582916
  57.0 42.4 %all-to-all-start = ((bf16[8,128,1024]{2,1,0:T(8,128)(2,1)}), bf16[8,128,1024]{2,1,0:T(8,128)(2,1)}, u32[]{:S(2)}, u32[]{:S(2)}) async-start(bf16[8,128,1024]{2,1,0:T(8,128)(2,1)} %broadcast_in_dim.8), calls=%async_computation | async-start | bytes 4194304 | tf_op jit(solution)/shard_map/all_to_all | solution.py:27
  67.3 4.1 %copy-start.5 = (bf16[1,128,4096]{2,1,0:T(8,128)(2,1)}, bf16[1,128,4096]{2,1,0:T(8,128)(2,1)S(1)}, u32[]{:S(2)}) copy-start(bf16[1,128,4096]{2,1,0:T(8,128)(2,1)S(1)} %collective-permute-done.1) | copy-start | bytes 3145732
  101.0 35.5 %all-to-all-start.2 = ((bf16[8,128,1024]{2,1,0:T(8,128)(2,1)}), bf16[8,128,1024]{2,1,0:T(8,128)(2,1)S(1)}, u32[]{:S(2)}, u32[]{:S(2)}) async-start(bf16[8,128,1024]{2,1,0:T(8,128)(2,1)} %pad_maximum_fusion.2), calls=%async_computation.2 | async-start | bytes 4194304 | tf_op jit(solution)/shard_map/all_to_all | solution.py:34
  136.9 4.4 %copy-start.4 = (bf16[1,4096,512]{2,1,0:T(8,128)(2,1)S(1)}, bf16[1,4096,512]{2,1,0:T(8,128)(2,1)}, u32[]{:S(2)}) copy-start(bf16[1,4096,512]{2,1,0:T(8,128)(2,1)} %param.13) | copy-start | bytes 12582916
  141.4 1.6 %copy-start.6 = (bf16[1,128,4096]{2,1,0:T(8,128)(2,1)S(1)}, bf16[1,128,4096]{2,1,0:T(8,128)(2,1)}, u32[]{:S(2)}) copy-start(bf16[1,128,4096]{2,1,0:T(8,128)(2,1)} %copy-done.5) | copy-start | bytes 3145732

commit v12 on v11

--- a/solution.py
+++ b/solution.py
@@ -98,8 +98,8 @@
         )
     dkey_ref[...] = jnp.zeros(dkey_ref.shape, dkey_ref.dtype)
     dvalue_ref[...] = jnp.zeros(dvalue_ref.shape, dvalue_ref.dtype)
-    dkey_ref[pl.ds(start, window), :] = dkey_acc * scale
-    dvalue_ref[pl.ds(start, window), :] = dvalue_acc
+    dkey_ref[pl.ds(start, window), :] = (dkey_acc * scale).astype(dkey_ref.dtype)
+    dvalue_ref[pl.ds(start, window), :] = dvalue_acc.astype(dvalue_ref.dtype)
 
 
 def attention_forward(start, mask, query, keys, values, inputs, group_size):
@@ -151,8 +151,8 @@
         ],
         out_shape=[
             jax.ShapeDtypeStruct((rows, width), jnp.float32),
-            jax.ShapeDtypeStruct((seq_len, kv_width), jnp.float32),
-            jax.ShapeDtypeStruct((seq_len, kv_width), jnp.float32),
+            jax.ShapeDtypeStruct((seq_len, kv_width), jnp.bfloat16),
+            jax.ShapeDtypeStruct((seq_len, kv_width), jnp.bfloat16),
         ],
         interpret=INTERPRET,
     )(start, mask, query, keys, values, grad)

time: 145 us -> 144 us (level)
  transfers between devices with their start and end apart: 5 -> 5, of which waited for: 2 -> 2; matrix products, arithmetic and copies ran while one was open for 19% -> 18% of each run, Pallas kernels for 27% -> 27%
where the time goes in v12:
time: 144 us
  waiting for transfers between devices  43.4 us (30%)
  Pallas kernels  38.3 us (27%)
  starting transfers between devices  24.2 us (17%)
  matrix products  14.2 us (10%)
  local copies, waits for them, and re-layouts  12.8 us (9%)
  other arithmetic  9.94 us (7%)
    all_to_all x2, waiting for transfers between devices, gather_all(): moved = lax.all_to_all(spread, axis, 0, 0)  31.1 us
    pallas_call x2, Pallas kernels, attention_backward(): pl.pallas_call(kernel, grid=(groups,), in_specs=[pl.BlockSpec(memory_spac...  25.4 us
    all_to_all x2, starting transfers between devices, gather_all(): moved = lax.all_to_all(spread, axis, 0, 0)  15.5 us
    pallas_call x1, Pallas kernels, attention_forward(): pl.pallas_call(kernel, grid=(groups,), in_specs=[pl.BlockSpec(memory_spac...  12.9 us
    all_to_all x1, waiting for transfers between devices, reduce_all(): lax.all_to_all(terms.astype(jnp.bfloat16).reshape((count, rows) + terms.s...  12.3 us
    all_to_all x1, starting transfers between devices, reduce_all(): lax.all_to_all(terms.astype(jnp.bfloat16).reshape((count, rows) + terms.s...  7.18 us
    dot_general x2, matrix products, layer_parts(): jnp.dot(flat, key_weight, preferred_element_type=jnp.float32)  6.52 us
    dot_general x1, matrix products, body(): jnp.dot(dkeys, jnp.transpose(key_weight), preferred_element_type=jnp.floa...  4.44 us
  transfers between devices with their start and end apart: 5, of which 2 were waited for; matrix products, arithmetic and copies ran while one was open for 18% of the time, Pallas kernels for 27%

profile of v12, /device:TPU:6, one launch (start us, length us, event | category | flops | bytes accessed | tf_op | source)
XLA Modules:
  0.0 143.6 jit_solution(15907154017022064384)
XLA Ops:
  0.6 0.1 collective-permute-start
  0.7 1.5 %fusion.18 = f32[128]{0:T(128)S(1)} fusion(bf16[1,128,4096]{2,1,0:T(8,128)(2,1)} %param.10), kind=kLoop, calls=%fused_computation.24 | loop fusion | flops 1572736 | bytes 1049088 | tf_op jit(solution)/shard_map/reduce_sum | solution.py:40
  2.2 0.0 copy-start
  2.2 0.0 copy-start.2
  2.3 0.0 copy-start.7
  2.3 3.4 %fusion.31 = bf16[128,512]{1,0:T(8,128)(2,1)S(1)} fusion(bf16[1,4096,512]{2,1,0:T(8,128)(2,1)} %param.12, bf16[1,128,4096]{2,1,0:T(8,128)(2,1)} %param.10, f32[128]{0:T(128)S(1)} %get-tuple-element.39, f32[4096]{0:T(1024)} %bitcast.77), kind=kOutput, calls=%fused_computation.37 | convolution fusion | flops 539033600 | bytes 5390848 | tf_op jit(solution)/shard_map/dot_general | solution.py:182
  5.7 0.0 copy-done
  5.7 0.6 copy-done.2
  6.3 0.0 copy-done.7
  6.3 0.8 fusion.37
  7.2 1.6 %broadcast_in_dim.9 = bf16[8,128,1024]{2,1,0:T(8,128)(2,1)} broadcast(bf16[128,1024]{1,0:T(8,128)(2,1)S(1)} %pad_maximum_fusion.4), dimensions={1,2} | broadcast | bytes 2359296 | tf_op jit(solution)/shard_map/broadcast_in_dim | solution.py:26
  8.8 0.0 copy-start.8
  8.8 0.0 copy-start.9
  8.8 7.9 %all-to-all-start.1 = ((bf16[8,128,1024]{2,1,0:T(8,128)(2,1)}), bf16[8,128,1024]{2,1,0:T(8,128)(2,1)}, u32[]{:S(2)}, u32[]{:S(2)}) async-start(bf16[8,128,1024]{2,1,0:T(8,128)(2,1)} %broadcast_in_dim.9), calls=%async_computation.1 | async-start | bytes 4194304 | tf_op jit(solution)/shard_map/all_to_all | solution.py:27
  16.7 1.5 %collective-permute-start.1 = (bf16[1,128,4096]{2,1,0:T(8,128)(2,1)}, bf16[1,128,4096]{2,1,0:T(8,128)(2,1)S(1)}, u32[]{:S(2)}, u32[]{:S(2)}) collective-permute-start(bf16[1,128,4096]{2,1,0:T(8,128)(2,1)} %param.9), channel_id=1, source_target_pairs={{8,0},{16,8},{24,16},{32,24},{40,32},{48,40},{56,48},{64,56},{72,6... | collective-permute-start | bytes 3145736 | tf_op jit(solution)/shard_map/ppermute | solution.py:21
  18.2 0.0 copy-done.8
  18.2 0.1 dynamic-slice
  18.2 0.0 copy-done.9
  18.2 0.1 dynamic-slice.1
  18.3 0.1 dynamic_slice.12
  18.4 0.1 dynamic_slice.14
  18.5 0.1 iota_compare_fusion
  18.6 1.0 and_convert_fusion
  19.7 0.0 collective-permute-done
  19.7 0.0 copy-start.1
  19.7 0.3 fusion.15
  20.0 0.0 copy-start.3
  20.0 3.1 %fusion.28 = bf16[128,512]{1,0:T(8,128)(2,1)S(1)} fusion(bf16[1,4096,512]{2,1,0:T(8,128)(2,1)} %param.12, bf16[1,128,4096]{2,1,0:T(8,128)(2,1)S(1)} %collective-permute-done, f32[4096]{0:T(1024)S(1)} %bitcast.79, f32[128]{0:T(128)S(1)} %add_rsqrt_fusion.1), kind=kOutput, calls=%fused_computation.36 | convolution fusion | flops 539033600 | bytes 5390848 | tf_op jit(solution)/shard_map/dot_general | solution.py:182
  23.1 0.4 copy-done.3
  23.5 0.8 fusion.34
  24.3 31.1 %all-to-all-done.1 = bf16[8,128,1024]{2,1,0:T(8,128)(2,1)} async-done(((bf16[8,128,1024]{2,1,0:T(8,128)(2,1)}), bf16[8,128,1024]{2,1,0:T(8,128)(2,1)}, u32[]{:S(2)}, u32[]{:S(2)}) %all-to-all-start.1) | async-done | bytes 2097184 | tf_op jit(solution)/shard_map/all_to_all | solution.py:27
  55.4 1.6 %broadcast_in_dim.8 = bf16[8,128,1024]{2,1,0:T(8,128)(2,1)} broadcast(bf16[128,1024]{1,0:T(8,128)(2,1)S(1)} %pad_maximum_fusion.3), dimensions={1,2} | broadcast | bytes 2359296 | tf_op jit(solution)/shard_map/broadcast_in_dim | solution.py:26
  57.0 7.6 %all-to-all-start = ((bf16[8,128,1024]{2,1,0:T(8,128)(2,1)}), bf16[8,128,1024]{2,1,0:T(8,128)(2,1)}, u32[]{:S(2)}, u32[]{:S(2)}) async-start(bf16[8,128,1024]{2,1,0:T(8,128)(2,1)} %broadcast_in_dim.8), calls=%async_computation | async-start | bytes 4194304 | tf_op jit(solution)/shard_map/all_to_all | solution.py:27
  64.6 0.0 copy-done.1
  64.6 1.6 %fusion.20 = (bf16[128,4096]{1,0:T(8,128)(2,1)S(1)}, bf16[128,4096]{1,0:T(8,128)(2,1)}) fusion(bf16[1,128,4096]{2,1,0:T(8,128)(2,1)S(1)} %copy-done, f32[128]{0:T(128)S(1)} %get-tuple-element.39, f32[4096]{0:T(1024)S(1)} %bitcast.81, f32[128]{0:T(128)S(1)} %add_rsqrt_fusion.1, bf16[1,128,4096]{2,1,0:T(8,128)(2,1)S(1)} %collective-permute-done), kind=kLoop, calls=%fused_computation.26 | loop fusion | flops 4194304 | bytes 4211712 | tf_op jit(solution)/shard_map/convert_element_type | solution.py:181
  66.2 1.1 fusion.58
  67.2 0.0 collective-permute-done.1
  67.3 0.0 copy-start.5
  67.3 1.1 fusion.57
  68.4 2.9 %fusion.56 = (bf16[1024,256]{1,0:T(8,128)(2,1)}, bf16[1024,256]{1,0:T(8,128)(2,1)}, bf16[1024,256]{1,0:T(8,128)(2,1)}, bf16[1024,256]{1,0:T(8,128)(2,1)}) fusion(bf16[1024,1024]{1,0:T(8,128)(2,1)} %bitcast.9), kind=kLoop, calls=%fused_computation.64 | loop fusion | bytes 4194304 | tf_op jit(solution)/shard_map/slice | solution.py:220
  71.3 0.0 copy-done.5
  71.3 12.7 %shard_map.96 = (f32[128,2048]{1,0:T(8,128)}, bf16[1024,256]{1,0:T(8,128)(2,1)}, bf16[1024,256]{1,0:T(8,128)(2,1)}) custom-call(s32[1]{0:T(128)} %bitcast.start_ref, s32[128,640]{1,0:T(8,128)} %get-tuple-element.34.mask_ref, bf16[128,2048]{1,0:T(8,128)(2,1)} %get-tuple-element.28.query_ref, bf16[1024,256]{1,0:T(8,128)(2,1)} %get-tuple-element.23.key_ref, ...), custom_call_target="tpu_custom_call" | custom-call | tf_op jit(solution)/shard_map/pallas_call | solution.py:136
  84.0 12.7 %shard_map.95 = (f32[128,2048]{1,0:T(8,128)}, bf16[1024,256]{1,0:T(8,128)(2,1)}, bf16[1024,256]{1,0:T(8,128)(2,1)}) custom-call(s32[1]{0:T(128)} %bitcast.start_ref, s32[128,640]{1,0:T(8,128)} %get-tuple-element.34.mask_ref, bf16[128,2048]{1,0:T(8,128)(2,1)} %get-tuple-element.29.query_ref, bf16[1024,256]{1,0:T(8,128)(2,1)} %get-tuple-element.25.key_ref, ...), custom_call_target="tpu_custom_call" | custom-call | tf_op jit(solution)/shard_map/pallas_call | solution.py:136
  96.7 1.7 %pad_maximum_fusion.1 = (bf16[1024,512]{1,0:T(8,128)(2,1)S(1)}, bf16[1024,512]{1,0:T(8,128)(2,1)S(1)}) fusion(bf16[1024,256]{1,0:T(8,128)(2,1)} %get-tuple-element.12, bf16[1024,256]{1,0:T(8,128)(2,1)} %get-tuple-element.11, bf16[1024,256]{1,0:T(8,128)(2,1)} %get-tuple-element.14, bf16[1024,256]{1,0:T(8,128)(2,1)} %get-tuple-element.13), kind=kLoop, calls=%fused_computation.43 | loop fusion | flops 4194304 | bytes 4194304 | tf_op jit(solution)/shard_map/concatenate | solution.py:225
  98.4 0.0 all-to-all-done
  98.4 1.6 %pad_maximum_fusion = bf16[1024,1024]{1,0:T(8,128)(2,1)} fusion(bf16[1024,512]{1,0:T(8,128)(2,1)S(1)} %get-tuple-element.19, bf16[1024,512]{1,0:T(8,128)(2,1)S(1)} %get-tuple-element.18), kind=kLoop, calls=%fused_computation.34 | loop fusion | flops 4194304 | bytes 4194304 | tf_op jit(solution)/shard_map/concatenate | solution.py:231
  100.1 7.2 %all-to-all-start.2 = ((bf16[8,128,1024]{2,1,0:T(8,128)(2,1)}), bf16[8,128,1024]{2,1,0:T(8,128)(2,1)S(1)}, u32[]{:S(2)}, u32[]{:S(2)}) async-start(bf16[8,128,1024]{2,1,0:T(8,128)(2,1)} %bitcast.74), calls=%async_computation.2 | async-start | bytes 4194304 | tf_op jit(solution)/shard_map/all_to_all | solution.py:34
  107.2 3.1 %fusion.55 = (bf16[1024,512]{1,0:T(8,128)(2,1)}, bf16[1024,512]{1,0:T(8,128)(2,1)}) fusion(bf16[1024,1024]{1,0:T(8,128)(2,1)} %bitcast.6), kind=kLoop, calls=%fused_computation.63 | loop fusion | bytes 4194304 | tf_op jit(solution)/shard_map/slice | solution.py:229
  110.3 12.9 %shard_map.97 = bf16[128,4096]{1,0:T(8,128)(2,1)} custom-call(s32[1]{0:T(128)} %bitcast.start_ref, s32[128,640]{1,0:T(8,128)} %get-tuple-element.35.mask_ref, bf16[128,4096]{1,0:T(8,128)(2,1)} %get-tuple-element.37.query_ref, bf16[1024,512]{1,0:T(8,128)(2,1)} %get-tuple-element.21.key_ref, bf16[1024,512]{1,0:T(8,128)(2,1)} %get-tuple-element.20.value_ref, ...), custom_call_target="tpu_custom_call" | custom-call | tf_op jit(solution)/shard_map/pallas_call | solution.py:112
  123.2 12.3 %all-to-all-done.2 = bf16[8,128,1024]{2,1,0:T(8,128)(2,1)S(1)} async-done(((bf16[8,128,1024]{2,1,0:T(8,128)(2,1)}), bf16[8,128,1024]{2,1,0:T(8,128)(2,1)S(1)}, u32[]{:S(2)}, u32[]{:S(2)}) %all-to-all-start.2) | async-done | bytes 2097184 | tf_op jit(solution)/shard_map/all_to_all | solution.py:34
  135.5 0.4 reduce_sum.41
  135.9 0.0 copy-start.4
  135.9 4.4 %convolution_add_fusion.1 = f32[128,4096]{1,0:T(8,128)S(1)} fusion(bf16[1,4096,512]{2,1,0:T(8,128)(2,1)} %param.12, f32[128,2048]{1,0:T(8,128)} %get-tuple-element.17, f32[128,2048]{1,0:T(8,128)} %get-tuple-element.16, bf16[128,256]{1,0:T(8,128)(2,1)S(1)} %get-tuple-element.32, bf16[128,256]{1,0:T(8,128)(2,1)S(1)} %get-tuple-element.33), kind=kOutput, calls=%fused_computation.2 | convolution fusion | flops 538181632 | bytes 8519680 | tf_op jit(solution)/shard_map/dot_general | solution.py:258
  140.4 0.0 copy-done.4
  140.4 0.0 copy-start.6
  140.4 1.6 %fusion.25 = (f32[128]{0:T(128)S(1)}, f32[128,4096]{1,0:T(8,128)S(1)}) fusion(bf16[1,128,4096]{2,1,0:T(8,128)(2,1)S(1)} %copy-done, f32[128,4096]{1,0:T(8,128)S(1)} %convolution_add_fusion.1, bf16[1,4096,512]{2,1,0:T(8,128)(2,1)S(1)} %copy-done.4, bf16[128,256]{1,0:T(8,128)(2,1)S(1)} %get-tuple-element.31, bf16[128,256]{1,0:T(8,128)(2,1)S(1)} %get-tuple-element.30, ...), kind=kOutput, calls=%fused_computation.31 | convolution fusion | flops 539754368 | bytes 9585152 | tf_op jit(solution)/shard_map/dot_general | solution.py:261
  142.0 0.0 copy-done.6
  142.0 1.7 %fusion.42 = bf16[1,128,4096]{2,1,0:T(8,128)(2,1)} fusion(bf16[1,128,4096]{2,1,0:T(8,128)(2,1)S(1)} %copy-done, f32[128,4096]{1,0:T(8,128)S(1)} %get-tuple-element.41, f32[128]{0:T(128)S(1)} %broadcast_multiply_fusion, f32[128]{0:T(128)S(1)} %get-tuple-element.38, f32[128]{0:T(128)S(1)} %get-tuple-element.39, bf16[1,128,4096]{2,1,0:T(8,128)(2,1)S(1)} %copy-done.6), kind=kLoop, calls=%fused_computation.42 | loop fusion | flops 4194304 | bytes 5244416 | tf_op jit(solution)/shard_map/broadcast_in_dim | solution.py:271
  (7 shorter events, 0.1 us)
Async XLA Ops:
  0.6 19.0 %collective-permute-start = (bf16[1,128,4096]{2,1,0:T(8,128)(2,1)}, bf16[1,128,4096]{2,1,0:T(8,128)(2,1)S(1)}, u32[]{:S(2)}, u32[]{:S(2)}) collective-permute-start(bf16[1,128,4096]{2,1,0:T(8,128)(2,1)} %param.8), channel_id=1, source_target_pairs={{120,0},{0,8},{8,16},{16,24},{24,32},{32,40},{40,48},{48,56},{56,6... | collective-permute-start | bytes 3145736 | tf_op jit(solution)/shard_map/ppermute | solution.py:21
  2.2 3.5 %copy-start = (bf16[1,128,4096]{2,1,0:T(8,128)(2,1)S(1)}, bf16[1,128,4096]{2,1,0:T(8,128)(2,1)}, u32[]{:S(2)}) copy-start(bf16[1,128,4096]{2,1,0:T(8,128)(2,1)} %param.10) | copy-start | bytes 3145732
  2.2 4.1 %copy-start.2 = (bf16[1,4096,512]{2,1,0:T(8,128)(2,1)S(1)}, bf16[1,4096,512]{2,1,0:T(8,128)(2,1)}, u32[]{:S(2)}) copy-start(bf16[1,4096,512]{2,1,0:T(8,128)(2,1)} %param.13) | copy-start | bytes 12582916
  2.3 4.1 %copy-start.7 = (f32[1,4096]{1,0:T(1,128)S(1)}, f32[1,4096]{1,0:T(1,128)}, u32[]{:S(2)}) copy-start(f32[1,4096]{1,0:T(1,128)} %param.11) | copy-start | bytes 49156
  8.8 9.4 %copy-start.8 = (s32[1024]{0:T(1024)S(1)}, s32[1024]{0:T(1024)}, u32[]{:S(2)}) copy-start(s32[1024]{0:T(1024)} %param.14) | copy-start | bytes 12292
  8.8 9.4 %copy-start.9 = (s32[1024]{0:T(1024)S(1)}, s32[1024]{0:T(1024)}, u32[]{:S(2)}) copy-start(s32[1024]{0:T(1024)} %param.15) | copy-start | bytes 12292
  8.8 46.6 %all-to-all-start.1 = ((bf16[8,128,1024]{2,1,0:T(8,128)(2,1)}), bf16[8,128,1024]{2,1,0:T(8,128)(2,1)}, u32[]{:S(2)}, u32[]{:S(2)}) async-start(bf16[8,128,1024]{2,1,0:T(8,128)(2,1)} %broadcast_in_dim.9), calls=%async_computation.1 | async-start | bytes 4194304 | tf_op jit(solution)/shard_map/all_to_all | solution.py:27
  16.7 50.6 %collective-permute-start.1 = (bf16[1,128,4096]{2,1,0:T(8,128)(2,1)}, bf16[1,128,4096]{2,1,0:T(8,128)(2,1)S(1)}, u32[]{:S(2)}, u32[]{:S(2)}) collective-permute-start(bf16[1,128,4096]{2,1,0:T(8,128)(2,1)} %param.9), channel_id=1, source_target_pairs={{8,0},{16,8},{24,16},{32,24},{40,32},{48,40},{56,48},{64,56},{72,6... | collective-permute-start | bytes 3145736 | tf_op jit(solution)/shard_map/ppermute | solution.py:21
  19.7 44.9 %copy-start.1 = (bf16[1,128,4096]{2,1,0:T(8,128)(2,1)}, bf16[1,128,4096]{2,1,0:T(8,128)(2,1)S(1)}, u32[]{:S(2)}) copy-start(bf16[1,128,4096]{2,1,0:T(8,128)(2,1)S(1)} %collective-permute-done) | copy-start | bytes 3145732
  20.0 3.5 %copy-start.3 = (bf16[1,4096,512]{2,1,0:T(8,128)(2,1)S(1)}, bf16[1,4096,512]{2,1,0:T(8,128)(2,1)}, u32[]{:S(2)}) copy-start(bf16[1,4096,512]{2,1,0:T(8,128)(2,1)} %param.13) | copy-start | bytes 12582916
  57.0 41.4 %all-to-all-start = ((bf16[8,128,1024]{2,1,0:T(8,128)(2,1)}), bf16[8,128,1024]{2,1,0:T(8,128)(2,1)}, u32[]{:S(2)}, u32[]{:S(2)}) async-start(bf16[8,128,1024]{2,1,0:T(8,128)(2,1)} %broadcast_in_dim.8), calls=%async_computation | async-start | bytes 4194304 | tf_op jit(solution)/shard_map/all_to_all | solution.py:27
  67.3 4.1 %copy-start.5 = (bf16[1,128,4096]{2,1,0:T(8,128)(2,1)}, bf16[1,128,4096]{2,1,0:T(8,128)(2,1)S(1)}, u32[]{:S(2)}) copy-start(bf16[1,128,4096]{2,1,0:T(8,128)(2,1)S(1)} %collective-permute-done.1) | copy-start | bytes 3145732
  100.1 35.4 %all-to-all-start.2 = ((bf16[8,128,1024]{2,1,0:T(8,128)(2,1)}), bf16[8,128,1024]{2,1,0:T(8,128)(2,1)S(1)}, u32[]{:S(2)}, u32[]{:S(2)}) async-start(bf16[8,128,1024]{2,1,0:T(8,128)(2,1)} %bitcast.74), calls=%async_computation.2 | async-start | bytes 4194304 | tf_op jit(solution)/shard_map/all_to_all | solution.py:34
  135.9 4.5 %copy-start.4 = (bf16[1,4096,512]{2,1,0:T(8,128)(2,1)S(1)}, bf16[1,4096,512]{2,1,0:T(8,128)(2,1)}, u32[]{:S(2)}) copy-start(bf16[1,4096,512]{2,1,0:T(8,128)(2,1)} %param.13) | copy-start | bytes 12582916
  140.4 1.6 %copy-start.6 = (bf16[1,128,4096]{2,1,0:T(8,128)(2,1)S(1)}, bf16[1,128,4096]{2,1,0:T(8,128)(2,1)}, u32[]{:S(2)}) copy-start(bf16[1,128,4096]{2,1,0:T(8,128)(2,1)} %copy-done.5) | copy-start | bytes 3145732
